TPU v7x, 512 devices: a whole 4x4x16 slice. The times are simulated.
512 devices in a mesh: pipe: 8 (over x, y_hi), expert: 64 (over z, y_lo, core).
Axes of the slice: x: 4, y: 4 (y_hi: 2, y_lo: 2; y = y_hi * 2 + y_lo), z: 16, core: 2. Of those that a mesh axis runs over, the one named last changes fastest.
Arguments:
- acts_down: bfloat16 [8, 2048, 3584], P('pipe', 'expert'), may hold values from -6 to 6
- routes_down: int32 [8, 2048, 1], P('pipe', 'expert'), may hold values from 0 to 7; in each aligned block of 32 rows (0 to 31, 32 to 63, ..., all dimensions but the last counted through in order) at most 6 rows name the same one
- gates_down: float32 [8, 2048, 1], P('pipe', 'expert'), may hold values from 0.05 to 1
- grads_up: bfloat16 [8, 2048, 3584], P('pipe', 'expert'), may hold values from -6 to 6
- routes_up: int32 [8, 2048, 1], P('pipe', 'expert'), may hold values from 0 to 7; in each aligned block of 32 rows (0 to 31, 32 to 63, ..., all dimensions but the last counted through in order) at most 6 rows name the same one
- gates_up: float32 [8, 2048, 1], P('pipe', 'expert'), may hold values from 0.05 to 1
- weight_in: bfloat16 [8, 64, 448, 2048], P('pipe', 'expert'), may hold values from -0.09375 to 0.09375
- weight_out: bfloat16 [8, 64, 1024, 448], P('pipe', 'expert'), may hold values from -0.1875 to 0.1875
- saved_pre: bfloat16 [8, 64, 48, 2048], P('pipe', 'expert'), may hold values from -5 to 5
Outputs:
- mixed_down: bfloat16 [8, 2048, 3584], P('pipe', 'expert')
- input_grads: bfloat16 [8, 2048, 3584], P('pipe', 'expert')
Inputs may be any that keep to these rules, and one draw needn't show every extreme that they name: `routes_down`: each row names one expert. In each aligned block of 32 tokens no expert is named more than 6 times, a bound that some block reaches. `routes_up`: as for routes_down.
All inputs are finite; a program needn't handle non-finite values.
Results may differ from a plain program's by a relative error of at most 0.0034.
Values may be sent and summed in bfloat16 or wider, within the bound.
No kernel may reach another device: no remote copies, remote signals or barrier semaphores. Data moves between devices by JAX's collectives and lax.ppermute only.
A program may use at most 64 MiB of HBM per device.

v0:
```python
import jax
import jax.numpy as jnp
from jax import lax
from jax.sharding import PartitionSpec as P

EXPERTS = 8
MOST = 6


def partner(block, axis, bit):
    count = lax.axis_size(axis)
    route = []
    for low in range(count):
        high = low | 1 << bit
        if high != low and high < count:
            route += [(low, high), (high, low)]
    return lax.ppermute(block, axis, route)


def shifted(block, axis, distance):
    devices = range(lax.axis_size(axis))
    route = [((i - distance) % len(devices), i) for i in devices]
    return lax.ppermute(block, axis, route)


def slot_table(routes, experts, capacity):
    tok_rows, top_count = routes.shape
    flat_routes = routes.reshape(-1)
    onehot = (flat_routes[:, None] == jnp.arange(experts, dtype=jnp.int32)[None, :]).astype(
        jnp.int32
    )
    before = jnp.cumsum(onehot, axis=0) - onehot
    rank_within = jnp.sum(before * onehot, axis=1)
    return (flat_routes * capacity + rank_within).reshape(tok_rows, top_count)


def fill_slots(token_rows, slots, slot_count):
    tok_rows = token_rows.shape[0]
    source = jnp.repeat(jnp.arange(tok_rows, dtype=jnp.int32), slots.shape[1])
    owner_row = jnp.full((slot_count,), tok_rows, dtype=jnp.int32).at[slots.reshape(-1)].set(source)
    padded = jnp.concatenate(
        [token_rows, jnp.zeros((1, token_rows.shape[1]), token_rows.dtype)], axis=0
    )
    return jnp.take(padded, owner_row, axis=0)


def share_sum(partial_sums, member, group_size):
    current = partial_sums
    for bit_level in reversed(range(group_size.bit_length() - 1)):
        half_rows = current.shape[0] // 2
        lower_half = current[:half_rows]
        upper_half = current[half_rows:]
        high_bit = member >> bit_level & 1 == 1
        kept_part = jnp.where(high_bit, upper_half, lower_half)
        sent_part = jnp.where(high_bit, lower_half, upper_half)
        current = kept_part + partner(sent_part, "expert", bit_level)
    return current


def share_gather(piece, member, group_size):
    current = piece
    for bit_level in range(group_size.bit_length() - 1):
        partner_rows = partner(current, "expert", bit_level)
        high_bit = member >> bit_level & 1 == 1
        current = jnp.where(
            high_bit,
            jnp.concatenate([partner_rows, current], axis=0),
            jnp.concatenate([current, partner_rows], axis=0),
        )
    return current


def forward_rows(slot_rows, proj_in, proj_out, member, group_size):
    hidden_units = proj_out.shape[0]
    partial_pre = jnp.dot(slot_rows, proj_in, preferred_element_type=jnp.float32)
    pre_share = share_sum(partial_pre, member, group_size)
    hidden_share = (jax.nn.silu(pre_share[:, :hidden_units]) * pre_share[:, hidden_units:]).astype(
        jnp.bfloat16
    )
    hidden = share_gather(hidden_share, member, group_size)
    return jnp.dot(hidden, proj_out, preferred_element_type=jnp.float32).astype(jnp.bfloat16)


def backward_rows(slot_rows, proj_in, proj_out, saved, member, group_size):
    hidden_units = proj_out.shape[0]
    partial_grad = lax.dot_general(
        slot_rows, proj_out, (((1,), (1,)), ((), ())), preferred_element_type=jnp.float32
    )
    hidden_grad = share_sum(partial_grad, member, group_size)
    gate_pre = saved[:, :hidden_units].astype(jnp.float32)
    up_pre = saved[:, hidden_units:].astype(jnp.float32)
    sigmoid_gate = jax.nn.sigmoid(gate_pre)
    gate_grad = hidden_grad * up_pre * sigmoid_gate * (1.0 + gate_pre * (1.0 - sigmoid_gate))
    up_grad = hidden_grad * gate_pre * sigmoid_gate
    grad_share = jnp.concatenate([gate_grad, up_grad], axis=1).astype(jnp.bfloat16)
    pre_grad = share_gather(grad_share, member, group_size)
    return lax.dot_general(
        pre_grad, proj_in, (((1,), (1,)), ((), ())), preferred_element_type=jnp.float32
    ).astype(jnp.bfloat16)


def combine(token_rows, returned, slots, gates):
    tok_rows, top_count = slots.shape
    gathered = jnp.take(returned, slots.reshape(-1), axis=0).reshape(
        tok_rows, top_count, returned.shape[1]
    )
    summed = token_rows.astype(jnp.float32) + jnp.einsum(
        "tk,tkd->td", gates, gathered.astype(jnp.float32)
    )
    return summed.astype(jnp.bfloat16)


def body(
    acts_down,
    routes_down,
    gates_down,
    grads_up,
    routes_up,
    gates_up,
    weight_in,
    weight_out,
    saved_pre,
):
    devices = lax.axis_size("expert")
    group_size = devices // EXPERTS
    member = lax.axis_index("expert") % group_size
    model_width = acts_down.shape[2]
    share_width = model_width // group_size
    slot_count = EXPERTS * MOST
    proj_in = weight_in[0, 0]
    proj_out = weight_out[0, 0]
    saved = saved_pre[0, 0]

    def to_devices(full_rows):
        return (
            full_rows.reshape(EXPERTS, MOST, group_size, share_width)
            .transpose(0, 2, 1, 3)
            .reshape(devices, MOST, share_width)
        )

    def from_devices(returned):
        return (
            returned.reshape(EXPERTS, group_size, MOST, share_width)
            .transpose(0, 2, 1, 3)
            .reshape(slot_count, model_width)
        )

    arrived = shifted(acts_down[0], "pipe", 1)
    incoming = shifted(grads_up[0], "pipe", -1)
    slots_down = slot_table(routes_down[0], EXPERTS, MOST)
    slots_up = slot_table(routes_up[0], EXPERTS, MOST)
    send_down = to_devices(fill_slots(arrived, slots_down, slot_count))
    send_up = to_devices(fill_slots(incoming, slots_up, slot_count))
    slot_rows = lax.all_to_all(send_down, "expert", split_axis=0, concat_axis=0, tiled=True)
    result = forward_rows(
        slot_rows.reshape(-1, share_width), proj_in, proj_out, member, group_size
    ).reshape(slot_rows.shape)
    back_down = lax.all_to_all(result, "expert", split_axis=0, concat_axis=0, tiled=True)
    got_up = lax.all_to_all(send_up, "expert", split_axis=0, concat_axis=0, tiled=True)
    out_up = backward_rows(
        got_up.reshape(-1, share_width), proj_in, proj_out, saved, member, group_size
    ).reshape(got_up.shape)
    back_up = lax.all_to_all(out_up, "expert", split_axis=0, concat_axis=0, tiled=True)
    mixed_rows = combine(arrived, from_devices(back_down), slots_down, gates_down[0])
    grad_rows = combine(incoming, from_devices(back_up), slots_up, gates_up[0])
    return (mixed_rows[None], grad_rows[None])


def solution(mesh):
    placed = (
        P("pipe", "expert", None),
        P("pipe", "expert", None),
        P("pipe", "expert", None),
        P("pipe", "expert", None),
        P("pipe", "expert", None),
        P("pipe", "expert", None),
        P("pipe", "expert", None, None),
        P("pipe", "expert", None, None),
        P("pipe", "expert", None, None),
    )
    return jax.shard_map(
        body,
        mesh=mesh,
        in_specs=placed,
        out_specs=(P("pipe", "expert", None), P("pipe", "expert", None)),
        check_vma=False,
    )
```

profile of v0, /device:TPU:8, one launch (start us, length us, event | category | flops | bytes accessed | tf_op | source)
XLA Modules:
  0.0 314.8 jit_solution(4365410298730226678)
XLA Ops:
  0.6 4.3 %collective-permute-start = (bf16[32,3584]{1,0:T(8,128)(2,1)}, bf16[32,3584]{1,0:T(8,128)(2,1)S(1)}, u32[]{:S(2)}, u32[]{:S(2)}) collective-permute-start(bf16[32,3584]{1,0:T(8,128)(2,1)} %bitcast.82), channel_id=1, source_target_pairs={{448,0},{0,64},{64,128},{128,192},{192,256},{256,320},{320,384},{3... | collective-permute-start | bytes 688136 | tf_op jit(solution)/shard_map/ppermute | solution.py:23
  5.0 5.3 %collective-permute-start.7 = (bf16[32,3584]{1,0:T(8,128)(2,1)}, bf16[32,3584]{1,0:T(8,128)(2,1)S(1)}, u32[]{:S(2)}, u32[]{:S(2)}) collective-permute-start(bf16[32,3584]{1,0:T(8,128)(2,1)} %bitcast.81), channel_id=1, source_target_pairs={{64,0},{128,64},{192,128},{256,192},{320,256},{384,320},{448,384},... | collective-permute-start | bytes 688136 | tf_op jit(solution)/shard_map/ppermute | solution.py:23
  10.2 0.7 fusion.34
  11.0 0.8 select_reduce_fusion.1
  11.9 0.7 fusion.35
  12.5 0.7 fusion.33
  13.3 0.8 select_reduce_fusion
  14.2 0.7 fusion.36
  14.8 0.7 scatter_custom_fusion.1
  15.5 0.7 scatter_custom_fusion
  16.2 2.5 collective-permute-done.7
  18.8 0.7 copy-done.8
  19.5 0.8 gather_fusion.2
  20.8 1.0 copy.26
  21.9 17.1 %all-to-all-start.2 = ((bf16[64,6,448]{2,1,0:T(8,128)(2,1)}), bf16[64,6,448]{2,1,0:T(8,128)(2,1)S(1)}, u32[]{:S(2)}, u32[]{:S(2)}) async-start(bf16[64,6,448]{2,1,0:T(8,128)(2,1)} %copy.26), calls=%async_computation.2 | async-start | bytes 1048576 | tf_op jit(solution)/shard_map/all_to_all | solution.py:159
  39.1 0.7 copy-done.6
  39.8 0.8 gather_fusion
  41.1 1.0 copy.22
  42.2 30.4 %all-to-all-done.2 = bf16[64,6,448]{2,1,0:T(8,128)(2,1)S(1)} async-done(((bf16[64,6,448]{2,1,0:T(8,128)(2,1)}), bf16[64,6,448]{2,1,0:T(8,128)(2,1)S(1)}, u32[]{:S(2)}, u32[]{:S(2)}) %all-to-all-start.2) | async-done | bytes 344096 | tf_op jit(solution)/shard_map/all_to_all | solution.py:159
  72.6 5.4 %all-to-all-start = ((bf16[64,6,448]{2,1,0:T(8,128)(2,1)}), bf16[64,6,448]{2,1,0:T(8,128)(2,1)}, u32[]{:S(2)}, u32[]{:S(2)}) async-start(bf16[64,6,448]{2,1,0:T(8,128)(2,1)} %copy.22), calls=%async_computation | async-start | bytes 1048576 | tf_op jit(solution)/shard_map/all_to_all | solution.py:154
  78.0 1.0 reshape.131
  79.0 1.9 fusion.13
  80.9 1.0 slice_select_fusion.1
  81.9 3.4 %collective-permute-start.8 = (f32[192,1024]{1,0:T(8,128)}, f32[192,1024]{1,0:T(8,128)}, u32[]{:S(2)}, u32[]{:S(2)}) collective-permute-start(f32[192,1024]{1,0:T(8,128)} %slice_select_fusion.1), channel_id=1, source_target_pairs={{0,4},{4,0},{1,5},{5,1},{2,6},{6,2},{3,7},{7,3},{8,12},{12,8},{9,1... | collective-permute-start | bytes 2359304 | tf_op jit(solution)/shard_map/ppermute | solution.py:17
  85.3 26.6 %all-to-all-done = bf16[64,6,448]{2,1,0:T(8,128)(2,1)} async-done(((bf16[64,6,448]{2,1,0:T(8,128)(2,1)}), bf16[64,6,448]{2,1,0:T(8,128)(2,1)}, u32[]{:S(2)}, u32[]{:S(2)}) %all-to-all-start) | async-done | bytes 344096 | tf_op jit(solution)/shard_map/all_to_all | solution.py:154
  111.9 2.0 reshape.124
  113.9 2.0 fusion.2
  115.9 3.7 %collective-permute-done.8 = f32[192,1024]{1,0:T(8,128)} collective-permute-done((f32[192,1024]{1,0:T(8,128)}, f32[192,1024]{1,0:T(8,128)}, u32[]{:S(2)}, u32[]{:S(2)}) %collective-permute-start.8) | collective-permute-done | bytes 786464 | tf_op jit(solution)/shard_map/ppermute | solution.py:17
  119.6 1.3 select_add_fusion.1
  120.9 0.9 copy-done.3
  121.8 0.8 slice_select_fusion.3
  122.6 2.6 collective-permute-start.9
  125.2 1.4 slice_select_fusion
  126.5 2.4 collective-permute-start.1
  128.9 6.5 %collective-permute-done.9 = f32[96,1024]{1,0:T(8,128)S(1)} collective-permute-done((f32[96,1024]{1,0:T(8,128)}, f32[96,1024]{1,0:T(8,128)S(1)}, u32[]{:S(2)}, u32[]{:S(2)}) %collective-permute-start.9) | collective-permute-done | bytes 393248 | tf_op jit(solution)/shard_map/ppermute | solution.py:17
  135.6 2.2 collective-permute-start.10
  137.8 1.4 collective-permute-done.10
  139.4 2.0 collective-permute-start.11
  141.4 23.1 %collective-permute-done.1 = f32[192,2048]{1,0:T(8,128)} collective-permute-done((f32[192,2048]{1,0:T(8,128)}, f32[192,2048]{1,0:T(8,128)}, u32[]{:S(2)}, u32[]{:S(2)}) %collective-permute-start.1) | collective-permute-done | bytes 1572896 | tf_op jit(solution)/shard_map/ppermute | solution.py:17
  164.5 1.7 select_add_fusion
  166.3 3.4 %collective-permute-start.2 = (f32[96,2048]{1,0:T(8,128)S(1)}, f32[96,2048]{1,0:T(8,128)S(1)}, u32[]{:S(2)}, u32[]{:S(2)}) collective-permute-start(f32[96,2048]{1,0:T(8,128)S(1)} %slice_select_fusion.2), channel_id=1, source_target_pairs={{0,2},{2,0},{1,3},{3,1},{4,6},{6,4},{5,7},{7,5},{8,10},{10,8},{9,1... | collective-permute-start | bytes 2359304 | tf_op jit(solution)/shard_map/ppermute | solution.py:17
  169.8 2.5 collective-permute-start.12
  172.3 22.3 %collective-permute-done.12 = bf16[96,2048]{1,0:T(8,128)(2,1)S(1)} collective-permute-done((bf16[96,2048]{1,0:T(8,128)(2,1)S(1)}, bf16[96,2048]{1,0:T(8,128)(2,1)S(1)}, u32[]{:S(2)}, u32[]{:S(2)}) %collective-permute-start.12) | collective-permute-done | bytes 393248 | tf_op jit(solution)/shard_map/ppermute | solution.py:17
  194.7 2.2 collective-permute-start.13
  197.1 0.8 slice_select_fusion.4
  197.9 1.9 collective-permute-start.3
  199.9 13.7 %collective-permute-done.13 = bf16[192,2048]{1,0:T(8,128)(2,1)S(1)} collective-permute-done((bf16[192,2048]{1,0:T(8,128)(2,1)S(1)}, bf16[192,2048]{1,0:T(8,128)(2,1)S(1)}, u32[]{:S(2)}, u32[]{:S(2)}) %collective-permute-start.13) | collective-permute-done | bytes 786464 | tf_op jit(solution)/shard_map/ppermute | solution.py:17
  213.6 1.9 fusion.10
  215.5 1.1 copy.27
  216.6 1.0 reshape.132
  217.6 13.8 %all-to-all-start.3 = ((bf16[64,6,448]{2,1,0:T(8,128)(2,1)}), bf16[64,6,448]{2,1,0:T(8,128)(2,1)S(1)}, u32[]{:S(2)}, u32[]{:S(2)}) async-start(bf16[64,6,448]{2,1,0:T(8,128)(2,1)} %reshape.132), calls=%async_computation.3 | async-start | bytes 1048576 | tf_op jit(solution)/shard_map/all_to_all | solution.py:163
  231.5 2.2 collective-permute-start.4
  233.7 1.1 collective-permute-done.4
  234.9 2.4 collective-permute-start.5
  237.3 8.1 %collective-permute-done.5 = bf16[96,1024]{1,0:T(8,128)(2,1)S(1)} collective-permute-done((bf16[96,1024]{1,0:T(8,128)(2,1)S(1)}, bf16[96,1024]{1,0:T(8,128)(2,1)S(1)}, u32[]{:S(2)}, u32[]{:S(2)}) %collective-permute-start.5) | collective-permute-done | bytes 196640 | tf_op jit(solution)/shard_map/ppermute | solution.py:17
  245.5 3.2 %collective-permute-start.6 = (bf16[192,1024]{1,0:T(8,128)(2,1)S(1)}, bf16[192,1024]{1,0:T(8,128)(2,1)S(1)}, u32[]{:S(2)}, u32[]{:S(2)}) collective-permute-start(bf16[192,1024]{1,0:T(8,128)(2,1)S(1)} %maximum_select_fusion.7), channel_id=1, source_target_pairs={{0,4},{4,0},{1,5},{5,1},{2,6},{6,2},{3,7},{7,3},{8,12},{12,8},{9,1... | collective-permute-start | bytes 1179656 | tf_op jit(solution)/shard_map/ppermute | solution.py:17
  248.8 15.8 %collective-permute-done.6 = bf16[192,1024]{1,0:T(8,128)(2,1)S(1)} collective-permute-done((bf16[192,1024]{1,0:T(8,128)(2,1)S(1)}, bf16[192,1024]{1,0:T(8,128)(2,1)S(1)}, u32[]{:S(2)}, u32[]{:S(2)}) %collective-permute-start.6) | collective-permute-done | bytes 393248 | tf_op jit(solution)/shard_map/ppermute | solution.py:17
  265.4 1.0 reshape.125
  266.4 12.7 %all-to-all-start.1 = ((bf16[64,6,448]{2,1,0:T(8,128)(2,1)}), bf16[64,6,448]{2,1,0:T(8,128)(2,1)S(1)}, u32[]{:S(2)}, u32[]{:S(2)}) async-start(bf16[64,6,448]{2,1,0:T(8,128)(2,1)} %reshape.125), calls=%async_computation.1 | async-start | bytes 1048576 | tf_op jit(solution)/shard_map/all_to_all | solution.py:158
  279.8 0.7 gather_fusion.3
  280.5 0.8 fusion.23
  281.3 31.4 %all-to-all-done.1 = bf16[64,6,448]{2,1,0:T(8,128)(2,1)S(1)} async-done(((bf16[64,6,448]{2,1,0:T(8,128)(2,1)}), bf16[64,6,448]{2,1,0:T(8,128)(2,1)S(1)}, u32[]{:S(2)}, u32[]{:S(2)}) %all-to-all-start.1) | async-done | bytes 344096 | tf_op jit(solution)/shard_map/all_to_all | solution.py:158
  313.3 0.7 gather_fusion.1
  314.0 0.8 fusion.22
  (73 shorter events, 4.4 us)
Async XLA Ops:
  0.6 113.3 %copy-start = (bf16[1,1,448,2048]{3,2,1,0:T(8,128)(2,1)S(1)}, bf16[1,1,448,2048]{3,2,1,0:T(8,128)(2,1)}, u32[]{:S(2)}) copy-start(bf16[1,1,448,2048]{3,2,1,0:T(8,128)(2,1)} %param.19) | copy-start | bytes 5505028
  0.6 38.4 %collective-permute-start = (bf16[32,3584]{1,0:T(8,128)(2,1)}, bf16[32,3584]{1,0:T(8,128)(2,1)S(1)}, u32[]{:S(2)}, u32[]{:S(2)}) collective-permute-start(bf16[32,3584]{1,0:T(8,128)(2,1)} %bitcast.82), channel_id=1, source_target_pairs={{448,0},{0,64},{64,128},{128,192},{192,256},{256,320},{320,384},{3... | collective-permute-start | bytes 688136 | tf_op jit(solution)/shard_map/ppermute | solution.py:23
  5.0 13.8 %collective-permute-start.7 = (bf16[32,3584]{1,0:T(8,128)(2,1)}, bf16[32,3584]{1,0:T(8,128)(2,1)S(1)}, u32[]{:S(2)}, u32[]{:S(2)}) collective-permute-start(bf16[32,3584]{1,0:T(8,128)(2,1)} %bitcast.81), channel_id=1, source_target_pairs={{64,0},{128,64},{192,128},{256,192},{320,256},{384,320},{448,384},... | collective-permute-start | bytes 688136 | tf_op jit(solution)/shard_map/ppermute | solution.py:23
  18.8 0.7 copy-start.8
  21.9 50.7 %all-to-all-start.2 = ((bf16[64,6,448]{2,1,0:T(8,128)(2,1)}), bf16[64,6,448]{2,1,0:T(8,128)(2,1)S(1)}, u32[]{:S(2)}, u32[]{:S(2)}) async-start(bf16[64,6,448]{2,1,0:T(8,128)(2,1)} %copy.26), calls=%async_computation.2 | async-start | bytes 1048576 | tf_op jit(solution)/shard_map/all_to_all | solution.py:159
  39.0 0.7 copy-start.6
  72.6 39.3 %all-to-all-start = ((bf16[64,6,448]{2,1,0:T(8,128)(2,1)}), bf16[64,6,448]{2,1,0:T(8,128)(2,1)}, u32[]{:S(2)}, u32[]{:S(2)}) async-start(bf16[64,6,448]{2,1,0:T(8,128)(2,1)} %copy.22), calls=%async_computation | async-start | bytes 1048576 | tf_op jit(solution)/shard_map/all_to_all | solution.py:154
  81.9 37.7 %collective-permute-start.8 = (f32[192,1024]{1,0:T(8,128)}, f32[192,1024]{1,0:T(8,128)}, u32[]{:S(2)}, u32[]{:S(2)}) collective-permute-start(f32[192,1024]{1,0:T(8,128)} %slice_select_fusion.1), channel_id=1, source_target_pairs={{0,4},{4,0},{1,5},{5,1},{2,6},{6,2},{3,7},{7,3},{8,12},{12,8},{9,1... | collective-permute-start | bytes 2359304 | tf_op jit(solution)/shard_map/ppermute | solution.py:17
  115.9 9.3 %copy-start.1 = (f32[384,2048]{1,0:T(8,128)}, f32[384,2048]{1,0:T(8,128)S(1)}, u32[]{:S(2)}) copy-start(f32[384,2048]{1,0:T(8,128)S(1)} %fusion.2) | copy-start | bytes 9437188
  120.9 0.9 copy-start.3
  122.6 12.9 %copy-start.4 = (f32[192,1024]{1,0:T(8,128)S(1)}, f32[192,1024]{1,0:T(8,128)}, u32[]{:S(2)}) copy-start(f32[192,1024]{1,0:T(8,128)} %copy-done.3) | copy-start | bytes 2359300
  122.6 12.9 %collective-permute-start.9 = (f32[96,1024]{1,0:T(8,128)}, f32[96,1024]{1,0:T(8,128)S(1)}, u32[]{:S(2)}, u32[]{:S(2)}) collective-permute-start(f32[96,1024]{1,0:T(8,128)} %slice_select_fusion.3), channel_id=1, source_target_pairs={{0,2},{2,0},{1,3},{3,1},{4,6},{6,4},{5,7},{7,5},{8,10},{10,8},{9,1... | collective-permute-start | bytes 1179656 | tf_op jit(solution)/shard_map/ppermute | solution.py:17
  126.5 12.6 %copy-start.10 = (bf16[1,1,48,2048]{3,2,1,0:T(8,128)(2,1)S(1)}, bf16[1,1,48,2048]{3,2,1,0:T(8,128)(2,1)}, u32[]{:S(2)}) copy-start(bf16[1,1,48,2048]{3,2,1,0:T(8,128)(2,1)} %param.21) | copy-start | bytes 589828
  126.5 38.0 %collective-permute-start.1 = (f32[192,2048]{1,0:T(8,128)}, f32[192,2048]{1,0:T(8,128)}, u32[]{:S(2)}, u32[]{:S(2)}) collective-permute-start(f32[192,2048]{1,0:T(8,128)} %slice_select_fusion), channel_id=1, source_target_pairs={{0,4},{4,0},{1,5},{5,1},{2,6},{6,2},{3,7},{7,3},{8,12},{12,8},{9,1... | collective-permute-start | bytes 4718600 | tf_op jit(solution)/shard_map/ppermute | solution.py:17
  135.5 29.1 %copy-start.2 = (f32[384,2048]{1,0:T(8,128)S(1)}, f32[384,2048]{1,0:T(8,128)}, u32[]{:S(2)}) copy-start(f32[384,2048]{1,0:T(8,128)} %copy-done.1) | copy-start | bytes 9437188
  135.6 3.6 %collective-permute-start.10 = (f32[48,1024]{1,0:T(8,128)S(1)}, f32[48,1024]{1,0:T(8,128)S(1)}, u32[]{:S(2)}, u32[]{:S(2)}) collective-permute-start(f32[48,1024]{1,0:T(8,128)S(1)} %slice_select_fusion.5), channel_id=1, source_target_pairs={{0,1},{1,0},{2,3},{3,2},{4,5},{5,4},{6,7},{7,6},{8,9},{9,8},{10,11... | collective-permute-start | bytes 589832 | tf_op jit(solution)/shard_map/ppermute | solution.py:17
  139.4 30.3 %collective-permute-start.11 = (bf16[48,2048]{1,0:T(8,128)(2,1)S(1)}, bf16[48,2048]{1,0:T(8,128)(2,1)S(1)}, u32[]{:S(2)}, u32[]{:S(2)}) collective-permute-start(bf16[48,2048]{1,0:T(8,128)(2,1)S(1)} %pad_maximum_fusion), channel_id=1, source_target_pairs={{0,1},{1,0},{2,3},{3,2},{4,5},{5,4},{6,7},{7,6},{8,9},{9,8},{10,11... | collective-permute-start | bytes 589832 | tf_op jit(solution)/shard_map/ppermute | solution.py:17
  166.3 30.6 %collective-permute-start.2 = (f32[96,2048]{1,0:T(8,128)S(1)}, f32[96,2048]{1,0:T(8,128)S(1)}, u32[]{:S(2)}, u32[]{:S(2)}) collective-permute-start(f32[96,2048]{1,0:T(8,128)S(1)} %slice_select_fusion.2), channel_id=1, source_target_pairs={{0,2},{2,0},{1,3},{3,1},{4,6},{6,4},{5,7},{7,5},{8,10},{10,8},{9,1... | collective-permute-start | bytes 2359304 | tf_op jit(solution)/shard_map/ppermute | solution.py:17
  169.8 24.7 %collective-permute-start.12 = (bf16[96,2048]{1,0:T(8,128)(2,1)S(1)}, bf16[96,2048]{1,0:T(8,128)(2,1)S(1)}, u32[]{:S(2)}, u32[]{:S(2)}) collective-permute-start(bf16[96,2048]{1,0:T(8,128)(2,1)S(1)} %maximum_select_fusion.8), channel_id=1, source_target_pairs={{0,2},{2,0},{1,3},{3,1},{4,6},{6,4},{5,7},{7,5},{8,10},{10,8},{9,1... | collective-permute-start | bytes 1179656 | tf_op jit(solution)/shard_map/ppermute | solution.py:17
  194.7 18.9 %collective-permute-start.13 = (bf16[192,2048]{1,0:T(8,128)(2,1)S(1)}, bf16[192,2048]{1,0:T(8,128)(2,1)S(1)}, u32[]{:S(2)}, u32[]{:S(2)}) collective-permute-start(bf16[192,2048]{1,0:T(8,128)(2,1)S(1)} %maximum_select_fusion.6), channel_id=1, source_target_pairs={{0,4},{4,0},{1,5},{5,1},{2,6},{6,2},{3,7},{7,3},{8,12},{12,8},{9,1... | collective-permute-start | bytes 2359304 | tf_op jit(solution)/shard_map/ppermute | solution.py:17
  197.9 33.5 %collective-permute-start.3 = (f32[48,2048]{1,0:T(8,128)}, f32[48,2048]{1,0:T(8,128)S(1)}, u32[]{:S(2)}, u32[]{:S(2)}) collective-permute-start(f32[48,2048]{1,0:T(8,128)} %slice_select_fusion.4), channel_id=1, source_target_pairs={{0,1},{1,0},{2,3},{3,2},{4,5},{5,4},{6,7},{7,6},{8,9},{9,8},{10,11... | collective-permute-start | bytes 1179656 | tf_op jit(solution)/shard_map/ppermute | solution.py:17
  217.6 48.8 %all-to-all-start.3 = ((bf16[64,6,448]{2,1,0:T(8,128)(2,1)}), bf16[64,6,448]{2,1,0:T(8,128)(2,1)S(1)}, u32[]{:S(2)}, u32[]{:S(2)}) async-start(bf16[64,6,448]{2,1,0:T(8,128)(2,1)} %reshape.132), calls=%async_computation.3 | async-start | bytes 1048576 | tf_op jit(solution)/shard_map/all_to_all | solution.py:163
  231.4 17.4 %copy-start.11 = (s32[1,32,1]{1,2,0:T(1,128)S(1)}, s32[1,32,1]{1,2,0:T(1,128)}, u32[]{:S(2)}) copy-start(s32[1,32,1]{1,2,0:T(1,128)} %param.14) | copy-start | bytes 388
  231.4 33.2 %copy-start.5 = (bf16[1,1,1024,448]{2,3,1,0:T(8,128)(2,1)S(1)}, bf16[1,1,1024,448]{2,3,1,0:T(8,128)(2,1)}, u32[]{:S(2)}) copy-start(bf16[1,1,1024,448]{2,3,1,0:T(8,128)(2,1)} %param.20) | copy-start | bytes 2752516
  231.5 3.3 %collective-permute-start.4 = (bf16[48,1024]{1,0:T(8,128)(2,1)S(1)}, bf16[48,1024]{1,0:T(8,128)(2,1)S(1)}, u32[]{:S(2)}, u32[]{:S(2)}) collective-permute-start(bf16[48,1024]{1,0:T(8,128)(2,1)S(1)} %fusion.32), channel_id=1, source_target_pairs={{0,1},{1,0},{2,3},{3,2},{4,5},{5,4},{6,7},{7,6},{8,9},{9,8},{10,11... | collective-permute-start | bytes 294920 | tf_op jit(solution)/shard_map/ppermute | solution.py:17
  234.9 10.5 %collective-permute-start.5 = (bf16[96,1024]{1,0:T(8,128)(2,1)S(1)}, bf16[96,1024]{1,0:T(8,128)(2,1)S(1)}, u32[]{:S(2)}, u32[]{:S(2)}) collective-permute-start(bf16[96,1024]{1,0:T(8,128)(2,1)S(1)} %maximum_select_fusion.9), channel_id=1, source_target_pairs={{0,2},{2,0},{1,3},{3,1},{4,6},{6,4},{5,7},{7,5},{8,10},{10,8},{9,1... | collective-permute-start | bytes 589832 | tf_op jit(solution)/shard_map/ppermute | solution.py:17
  245.5 19.1 %collective-permute-start.6 = (bf16[192,1024]{1,0:T(8,128)(2,1)S(1)}, bf16[192,1024]{1,0:T(8,128)(2,1)S(1)}, u32[]{:S(2)}, u32[]{:S(2)}) collective-permute-start(bf16[192,1024]{1,0:T(8,128)(2,1)S(1)} %maximum_select_fusion.7), channel_id=1, source_target_pairs={{0,4},{4,0},{1,5},{5,1},{2,6},{6,2},{3,7},{7,3},{8,12},{12,8},{9,1... | collective-permute-start | bytes 1179656 | tf_op jit(solution)/shard_map/ppermute | solution.py:17
  265.2 13.9 %copy-start.12 = (s32[1,32,1]{1,2,0:T(1,128)S(1)}, s32[1,32,1]{1,2,0:T(1,128)}, u32[]{:S(2)}) copy-start(s32[1,32,1]{1,2,0:T(1,128)} %param.17) | copy-start | bytes 388
  266.4 46.3 %all-to-all-start.1 = ((bf16[64,6,448]{2,1,0:T(8,128)(2,1)}), bf16[64,6,448]{2,1,0:T(8,128)(2,1)S(1)}, u32[]{:S(2)}, u32[]{:S(2)}) async-start(bf16[64,6,448]{2,1,0:T(8,128)(2,1)} %reshape.125), calls=%async_computation.1 | async-start | bytes 1048576 | tf_op jit(solution)/shard_map/all_to_all | solution.py:158
  279.3 1.1 copy-start.9
  279.3 1.1 copy-start.13
  312.9 1.1 copy-start.7
  312.9 1.1 copy-start.14
where the time goes:
time: 316 us; the launch traced here: 315 us
  waiting for transfers between devices  187 us (59%)
  starting transfers between devices  88.9 us (28%)
  local copies, waits for them, and re-layouts  17.1 us (5%)
  other arithmetic  14.5 us (5%)
  matrix products  6.4 us (2%)
    ppermute x12, waiting for transfers between devices, partner(): return lax.ppermute(block, axis, route)  95.8 us
    all_to_all x1, waiting for transfers between devices, body(): lax.all_to_all(result, 'expert', split_axis=0, concat_axis=0, tiled=True)  31.4 us
    all_to_all x1, waiting for transfers between devices, body(): lax.all_to_all(send_up, 'expert', split_axis=0, concat_axis=0, tiled=True)  30.4 us
    ppermute x12, starting transfers between devices, partner(): return lax.ppermute(block, axis, route)  30.3 us
    all_to_all x1, waiting for transfers between devices, body(): lax.all_to_all(send_down, 'expert', split_axis=0, concat_axis=0, tiled=True)  26.6 us
    all_to_all x1, starting transfers between devices, body(): lax.all_to_all(send_up, 'expert', split_axis=0, concat_axis=0, tiled=True)  17.1 us
    all_to_all x1, starting transfers between devices, body(): lax.all_to_all(out_up, 'expert', split_axis=0, concat_axis=0, tiled=True)  13.8 us
    all_to_all x1, starting transfers between devices, body(): lax.all_to_all(result, 'expert', split_axis=0, concat_axis=0, tiled=True)  12.7 us
  transfers between devices with their start and end apart: 18, of which 13 were waited for; matrix products, arithmetic and copies ran while one was open for 10% of the time, Pallas kernels for 0%

commit v1 on v0

v1 whole, which is shorter than its diff:
```python
import numpy as np
import jax
import jax.numpy as jnp
from jax import lax
from jax.sharding import PartitionSpec as P

EXPERTS = 8
MOST = 6


def shifted(block, axis, distance):
    devices = range(lax.axis_size(axis))
    route = [((i - distance) % len(devices), i) for i in devices]
    return lax.ppermute(block, axis, route)


def slot_table(routes, experts, capacity):
    tok_rows, top_count = routes.shape
    flat_routes = routes.reshape(-1)
    onehot = (flat_routes[:, None] == jnp.arange(experts, dtype=jnp.int32)[None, :]).astype(
        jnp.int32
    )
    before = jnp.cumsum(onehot, axis=0) - onehot
    rank_within = jnp.sum(before * onehot, axis=1)
    return (flat_routes * capacity + rank_within).reshape(tok_rows, top_count)


def fill_slots(token_rows, slots, slot_count):
    tok_rows = token_rows.shape[0]
    source = jnp.repeat(jnp.arange(tok_rows, dtype=jnp.int32), slots.shape[1])
    owner_row = jnp.full((slot_count,), tok_rows, dtype=jnp.int32).at[slots.reshape(-1)].set(source)
    padded = jnp.concatenate(
        [token_rows, jnp.zeros((1, token_rows.shape[1]), token_rows.dtype)], axis=0
    )
    return jnp.take(padded, owner_row, axis=0)


def stage_bits(member_bits):
    core = member_bits[0]
    return [
        0,
        1 if core == 0 else 2,
        2 if core == 0 else 1,
    ]


def member_bits_of(member, group_size):
    return [member >> b & 1 for b in range(group_size.bit_length() - 1)]


def stage_route(axis_count, group_size, stage):
    route = []
    for index in range(axis_count):
        bits = member_bits_of(index % group_size, group_size)
        bit = stage_bits(bits)[stage]
        route.append((index, index ^ (1 << bit)))
    return route


def block_order(group_size):
    levels = group_size.bit_length() - 1
    order = [0] * group_size
    for member in range(group_size):
        bits = member_bits_of(member, group_size)
        pos = 0
        for bit in stage_bits(bits):
            pos = pos * 2 + bits[bit]
        order[pos] = member
    assert levels == 3
    return np.array(order)


def own_stage_bit(index, group_size, stage):
    member = index % group_size
    core = member & 1
    if stage == 0:
        bit = 0
    elif stage == 1:
        bit = jnp.where(core == 0, 1, 2)
    else:
        bit = jnp.where(core == 0, 2, 1)
    return (member >> bit & 1) == 1


def share_sum(partial_sums, index, group_size, axis_count):
    current = partial_sums
    for stage in range(group_size.bit_length() - 1):
        half_rows = current.shape[0] // 2
        lower_half = current[:half_rows]
        upper_half = current[half_rows:]
        high_bit = own_stage_bit(index, group_size, stage)
        kept_part = jnp.where(high_bit, upper_half, lower_half)
        sent_part = jnp.where(high_bit, lower_half, upper_half)
        route = stage_route(axis_count, group_size, stage)
        current = kept_part + lax.ppermute(sent_part, "expert", route)
    return current


def share_gather(piece, index, group_size, axis_count):
    current = piece
    for stage in reversed(range(group_size.bit_length() - 1)):
        route = stage_route(axis_count, group_size, stage)
        partner_rows = lax.ppermute(current, "expert", route)
        high_bit = own_stage_bit(index, group_size, stage)
        current = jnp.where(
            high_bit,
            jnp.concatenate([partner_rows, current], axis=0),
            jnp.concatenate([current, partner_rows], axis=0),
        )
    return current


def combine(token_rows, returned, slots, gates):
    tok_rows, top_count = slots.shape
    gathered = jnp.take(returned, slots.reshape(-1), axis=0).reshape(
        tok_rows, top_count, returned.shape[1]
    )
    summed = token_rows.astype(jnp.float32) + jnp.einsum(
        "tk,tkd->td", gates, gathered.astype(jnp.float32)
    )
    return summed.astype(jnp.bfloat16)


def body(
    acts_down,
    routes_down,
    gates_down,
    grads_up,
    routes_up,
    gates_up,
    weight_in,
    weight_out,
    saved_pre,
):
    devices = lax.axis_size("expert")
    group_size = devices // EXPERTS
    index = lax.axis_index("expert")
    model_width = acts_down.shape[2]
    share_width = model_width // group_size
    slot_count = EXPERTS * MOST
    proj_in = weight_in[0, 0]
    proj_out = weight_out[0, 0]
    saved = saved_pre[0, 0]
    hidden_units = proj_out.shape[0]
    order = block_order(group_size)
    unorder = np.argsort(order)

    def to_devices(full_rows):
        return (
            full_rows.reshape(EXPERTS, MOST, group_size, share_width)
            .transpose(0, 2, 1, 3)
            .reshape(devices, MOST, share_width)
        )

    def from_devices(returned):
        return (
            returned.reshape(EXPERTS, group_size, MOST, share_width)
            .transpose(0, 2, 1, 3)
            .reshape(slot_count, model_width)
        )

    def reorder(rows, perm):
        blocks = rows.reshape(group_size, -1, rows.shape[-1])
        return jnp.concatenate([blocks[k] for k in perm], axis=0)

    arrived = shifted(acts_down[0], "pipe", 1)
    incoming = shifted(grads_up[0], "pipe", -1)
    slots_down = slot_table(routes_down[0], EXPERTS, MOST)
    slots_up = slot_table(routes_up[0], EXPERTS, MOST)
    send_down = to_devices(fill_slots(arrived, slots_down, slot_count))
    send_up = to_devices(fill_slots(incoming, slots_up, slot_count))
    sent = jnp.stack([send_down, send_up], axis=1)
    got = lax.all_to_all(sent, "expert", split_axis=0, concat_axis=0, tiled=True)
    rows_down = got[:, 0].reshape(-1, share_width)
    rows_up = reorder(got[:, 1].reshape(-1, share_width), order)

    partial_pre = jnp.dot(rows_down, proj_in, preferred_element_type=jnp.float32)
    partial_grad = lax.dot_general(
        rows_up, proj_out, (((1,), (1,)), ((), ())), preferred_element_type=jnp.float32
    )
    summed = share_sum(
        jnp.concatenate([partial_pre, partial_grad], axis=1), index, group_size, devices
    )
    pre_share = summed[:, : 2 * hidden_units]
    hidden_grad = summed[:, 2 * hidden_units :]
    hidden_share = (
        jax.nn.silu(pre_share[:, :hidden_units]) * pre_share[:, hidden_units:]
    ).astype(jnp.bfloat16)
    gate_pre = saved[:, :hidden_units].astype(jnp.float32)
    up_pre = saved[:, hidden_units:].astype(jnp.float32)
    sigmoid_gate = jax.nn.sigmoid(gate_pre)
    gate_grad = hidden_grad * up_pre * sigmoid_gate * (1.0 + gate_pre * (1.0 - sigmoid_gate))
    up_grad = hidden_grad * gate_pre * sigmoid_gate
    grad_share = jnp.concatenate([gate_grad, up_grad], axis=1).astype(jnp.bfloat16)
    gathered = share_gather(
        jnp.concatenate([hidden_share, grad_share], axis=1), index, group_size, devices
    )
    hidden = gathered[:, :hidden_units]
    pre_grad = gathered[:, hidden_units:]
    out_down = jnp.dot(hidden, proj_out, preferred_element_type=jnp.float32).astype(
        jnp.bfloat16
    )
    out_up = lax.dot_general(
        pre_grad, proj_in, (((1,), (1,)), ((), ())), preferred_element_type=jnp.float32
    ).astype(jnp.bfloat16)
    out_up = reorder(out_up, unorder)
    result = jnp.stack(
        [out_down.reshape(devices, MOST, share_width), out_up.reshape(devices, MOST, share_width)],
        axis=1,
    )
    back = lax.all_to_all(result, "expert", split_axis=0, concat_axis=0, tiled=True)
    mixed_rows = combine(arrived, from_devices(back[:, 0]), slots_down, gates_down[0])
    grad_rows = combine(incoming, from_devices(back[:, 1]), slots_up, gates_up[0])
    return (mixed_rows[None], grad_rows[None])


def solution(mesh):
    placed = (
        P("pipe", "expert", None),
        P("pipe", "expert", None),
        P("pipe", "expert", None),
        P("pipe", "expert", None),
        P("pipe", "expert", None),
        P("pipe", "expert", None),
        P("pipe", "expert", None, None),
        P("pipe", "expert", None, None),
        P("pipe", "expert", None, None),
    )
    return jax.shard_map(
        body,
        mesh=mesh,
        in_specs=placed,
        out_specs=(P("pipe", "expert", None), P("pipe", "expert", None)),
        check_vma=False,
    )
```

time: 316 us -> 233 us (0.74)
  waiting for transfers between devices: 187 us -> 95.4 us
  starting transfers between devices: 88.9 us -> 38.3 us
  blocking collectives: 0 us -> 48.7 us
  local copies, waits for them, and re-layouts: 17.1 us -> 26 us
  other arithmetic: 14.5 us -> 17.7 us
    all_to_all x0 -> x1, blocking collectives: none -> 48.7 us  [body(): lax.all_to_all(result, 'expert', split_axis=0, concat_axis=0, tiled=True)]
    ppermute x12 -> x6, waiting for transfers between devices: 95.8 us -> 49.2 us  [the longest x3 30.3 us: share_sum(): current = kept_part + lax.ppermute(sent_part, 'expert', route)]
    all_to_all x4 -> x1, waiting for transfers between devices: 88.4 us -> 44.8 us  [body(): lax.all_to_all(sent, 'expert', split_axis=0, concat_axis=0, tiled=True)]
    all_to_all x4 -> x1, starting transfers between devices: 49 us -> 17.1 us  [body(): lax.all_to_all(sent, 'expert', split_axis=0, concat_axis=0, tiled=True)]
    ppermute x12 -> x6, starting transfers between devices: 30.3 us -> 12.7 us  [the longest x3 6.44 us: share_sum(): current = kept_part + lax.ppermute(sent_part, 'expert', route)]
    reshape x8 -> x0, local copies, waits for them, and re-layouts: 7.33 us -> none  [the longest x2 2.07 us: to_devices(): return full_rows.reshape(EXPERTS, MOST, group_size, share_width).transpos...]
    unnamed x30 -> x33, local copies, waits for them, and re-layouts: 2.33 us -> 7.84 us
    slice x0 -> x4, local copies, waits for them, and re-layouts: none -> 5.45 us  [the longest x2 2.21 us: reorder(): return jnp.concatenate([blocks[k] for k in perm], axis=0)]
  transfers between devices with their start and end apart: 18 -> 9, of which waited for: 13 -> 8; matrix products, arithmetic and copies ran while one was open for 10% -> 4% of each run, Pallas kernels for 0% -> 0%
where the time goes in v1:
time: 233 us
  waiting for transfers between devices  95.4 us (41%)
  blocking collectives  48.7 us (21%)
  starting transfers between devices  38.3 us (16%)
  local copies, waits for them, and re-layouts  26 us (11%)
  other arithmetic  17.7 us (8%)
  matrix products  5.36 us (2%)
    all_to_all x1, blocking collectives, body(): lax.all_to_all(result, 'expert', split_axis=0, concat_axis=0, tiled=True)  48.7 us
    all_to_all x1, waiting for transfers between devices, body(): lax.all_to_all(sent, 'expert', split_axis=0, concat_axis=0, tiled=True)  44.8 us
    ppermute x3, waiting for transfers between devices, share_sum(): current = kept_part + lax.ppermute(sent_part, 'expert', route)  30.3 us
    ppermute x3, waiting for transfers between devices, share_gather(): partner_rows = lax.ppermute(current, 'expert', route)  18.8 us
    all_to_all x1, starting transfers between devices, body(): lax.all_to_all(sent, 'expert', split_axis=0, concat_axis=0, tiled=True)  17.1 us
    ppermute x2, starting transfers between devices, shifted(): return lax.ppermute(block, axis, route)  8.45 us
    unnamed x33, local copies, waits for them, and re-layouts  7.84 us
    ppermute x3, starting transfers between devices, share_sum(): current = kept_part + lax.ppermute(sent_part, 'expert', route)  6.44 us
  transfers between devices with their start and end apart: 9, of which 8 were waited for; matrix products, arithmetic and copies ran while one was open for 4% of the time, Pallas kernels for 0%

profile of v1, /device:TPU:8, one launch (start us, length us, event | category | flops | bytes accessed | tf_op | source)
XLA Modules:
  0.0 232.7 jit_solution(17030259267126819215)
XLA Ops:
  0.6 6.5 %collective-permute-start.1 = (bf16[32,3584]{1,0:T(8,128)(2,1)}, bf16[32,3584]{1,0:T(8,128)(2,1)S(1)}, u32[]{:S(2)}, u32[]{:S(2)}) collective-permute-start(bf16[32,3584]{1,0:T(8,128)(2,1)} %bitcast.80), channel_id=1, source_target_pairs={{64,0},{128,64},{192,128},{256,192},{320,256},{384,320},{448,384},... | collective-permute-start | bytes 688136 | tf_op jit(solution)/shard_map/ppermute | solution.py:14
  7.2 1.9 collective-permute-start
  9.1 0.7 fusion.26
  9.9 0.8 select_reduce_fusion
  10.7 0.7 fusion.29
  11.4 0.7 compare_and_fusion
  12.1 0.7 scatter_custom_fusion.1
  12.8 0.7 fusion.27
  13.6 0.8 select_reduce_fusion.1
  14.4 0.7 fusion.28
  15.1 0.7 compare_and_fusion.1
  15.7 0.7 scatter_custom_fusion
  16.5 0.6 copy-done.7
  17.2 0.8 gather_fusion.1
  18.0 0.5 reshape.132
  18.5 1.4 collective-permute-done
  20.0 0.7 copy-done.5
  20.7 0.8 gather_fusion
  21.5 0.5 reshape.131
  22.1 1.7 copy.48
  23.8 17.1 %all-to-all-start = ((bf16[64,2,6,448]{3,1,2,0:T(2,128)(2,1)}), bf16[64,2,6,448]{3,1,2,0:T(2,128)(2,1)S(1)}, u32[]{:S(2)}, u32[]{:S(2)}) async-start(bf16[64,2,6,448]{3,1,2,0:T(2,128)(2,1)} %copy.48), calls=%async_computation | async-start | bytes 1572864 | tf_op jit(solution)/shard_map/all_to_all | solution.py:173
  41.0 44.8 %all-to-all-done = bf16[64,2,6,448]{3,1,2,0:T(2,128)(2,1)S(1)} async-done(((bf16[64,2,6,448]{3,1,2,0:T(2,128)(2,1)}), bf16[64,2,6,448]{3,1,2,0:T(2,128)(2,1)S(1)}, u32[]{:S(2)}, u32[]{:S(2)}) %all-to-all-start) | async-done | bytes 688160 | tf_op jit(solution)/shard_map/all_to_all | solution.py:173
  85.8 1.9 slice_reduce_fusion.1
  87.7 0.6 constant_dynamic-update-slice_fusion.7
  88.6 2.2 slice_reduce_fusion
  90.8 1.0 reshape_squeeze.11
  91.8 0.6 constant_dynamic-update-slice_fusion.6
  92.4 0.6 constant_dynamic-update-slice_fusion.5
  93.0 0.6 constant_dynamic-update-slice_fusion.4
  93.6 0.6 constant_dynamic-update-slice_fusion.3
  94.3 0.6 constant_dynamic-update-slice_fusion.2
  94.9 0.6 constant_dynamic-update-slice_fusion.1
  95.5 0.6 constant_dynamic-update-slice_fusion
  96.1 1.9 fusion.12
  98.0 1.0 fusion.3
  99.0 1.9 broadcast_select_fusion
  101.4 1.9 collective-permute-start.2
  103.3 4.8 %collective-permute-done.2 = f32[192,3072]{1,0:T(8,128)} collective-permute-done((f32[192,3072]{1,0:T(8,128)}, f32[192,3072]{1,0:T(8,128)}, u32[]{:S(2)}, u32[]{:S(2)}) %collective-permute-start.2) | collective-permute-done | bytes 2359328 | tf_op jit(solution)/shard_map/ppermute | solution.py:95
  108.1 3.1 %select_add_fusion = f32[192,3072]{1,0:T(8,128)S(1)} fusion(f32[192,3072]{1,0:T(8,128)} %collective-permute-done.2, pred[]{:T(512)S(6)} %eq.55, f32[384,1024]{1,0:T(8,128)S(1)} %fusion.12, f32[384,2048]{1,0:T(8,128)} %copy-done.1), kind=kLoop, calls=%fused_computation.11 | loop fusion | flops 2359296 | bytes 9437185 | tf_op jit(solution)/shard_map/add | solution.py:95
  111.2 1.4 copy-done.2
  112.6 1.1 slice_select_fusion
  113.7 2.4 %collective-permute-start.3 = (f32[96,3072]{1,0:T(8,128)}, f32[96,3072]{1,0:T(8,128)S(1)}, u32[]{:S(2)}, u32[]{:S(2)}) collective-permute-start(f32[96,3072]{1,0:T(8,128)} %slice_select_fusion), channel_id=1, source_target_pairs={{0,2},{1,5},{2,0},{3,7},{4,6},{5,1},{6,4},{7,3},{8,10},{9,13},{10,... | collective-permute-start | bytes 3538952 | tf_op jit(solution)/shard_map/ppermute | solution.py:95
  116.2 15.8 %collective-permute-done.3 = f32[96,3072]{1,0:T(8,128)S(1)} collective-permute-done((f32[96,3072]{1,0:T(8,128)}, f32[96,3072]{1,0:T(8,128)S(1)}, u32[]{:S(2)}, u32[]{:S(2)}) %collective-permute-start.3) | collective-permute-done | bytes 1179680 | tf_op jit(solution)/shard_map/ppermute | solution.py:95
  132.0 1.8 select_add_fusion.1
  133.9 2.1 collective-permute-start.4
  136.0 9.7 %collective-permute-done.4 = f32[48,3072]{1,0:T(8,128)S(1)} collective-permute-done((f32[48,3072]{1,0:T(8,128)S(1)}, f32[48,3072]{1,0:T(8,128)S(1)}, u32[]{:S(2)}, u32[]{:S(2)}) %collective-permute-start.4) | collective-permute-done | bytes 589856 | tf_op jit(solution)/shard_map/ppermute | solution.py:95
  146.0 1.9 collective-permute-start.5
  148.0 6.7 %collective-permute-done.5 = bf16[48,3072]{1,0:T(8,128)(2,1)S(1)} collective-permute-done((bf16[48,3072]{1,0:T(8,128)(2,1)S(1)}, bf16[48,3072]{1,0:T(8,128)(2,1)S(1)}, u32[]{:S(2)}, u32[]{:S(2)}) %collective-permute-start.5) | collective-permute-done | bytes 294944 | tf_op jit(solution)/shard_map/ppermute | solution.py:103
  154.8 2.4 %collective-permute-start.6 = (bf16[96,3072]{1,0:T(8,128)(2,1)S(1)}, bf16[96,3072]{1,0:T(8,128)(2,1)S(1)}, u32[]{:S(2)}, u32[]{:S(2)}) collective-permute-start(bf16[96,3072]{1,0:T(8,128)(2,1)S(1)} %maximum_select_fusion.2), channel_id=1, source_target_pairs={{0,2},{1,5},{2,0},{3,7},{4,6},{5,1},{6,4},{7,3},{8,10},{9,13},{10,... | collective-permute-start | bytes 1769480 | tf_op jit(solution)/shard_map/ppermute | solution.py:103
  157.2 9.3 %collective-permute-done.6 = bf16[96,3072]{1,0:T(8,128)(2,1)S(1)} collective-permute-done((bf16[96,3072]{1,0:T(8,128)(2,1)S(1)}, bf16[96,3072]{1,0:T(8,128)(2,1)S(1)}, u32[]{:S(2)}, u32[]{:S(2)}) %collective-permute-start.6) | collective-permute-done | bytes 589856 | tf_op jit(solution)/shard_map/ppermute | solution.py:103
  166.8 1.9 collective-permute-start.7
  168.7 2.8 %collective-permute-done.7 = bf16[192,3072]{1,0:T(8,128)(2,1)S(1)} collective-permute-done((bf16[192,3072]{1,0:T(8,128)(2,1)S(1)}, bf16[192,3072]{1,0:T(8,128)(2,1)S(1)}, u32[]{:S(2)}, u32[]{:S(2)}) %collective-permute-start.7) | collective-permute-done | bytes 1179680 | tf_op jit(solution)/shard_map/ppermute | solution.py:103
  171.5 0.9 maximum_select_fusion
  172.5 1.1 fusion.6
  173.6 1.4 convolution_convert_fusion
  175.3 0.5 concatenate.50
  176.2 1.1 copy.49
  177.8 0.8 copy.51
  178.6 48.7 %all_to_all.10 = bf16[64,2,6,448]{3,1,2,0:T(2,128)(2,1)S(1)} all-to-all(bf16[64,2,6,448]{3,1,2,0:T(2,128)(2,1)S(1)} %copy.51), channel_id=1, replica_groups=mesh['pipe'=8,'expert'=64] {'expert'}, dimensions={0} | all-to-all | bytes 1376256 | tf_op jit(solution)/shard_map/all_to_all | solution.py:211
  227.4 1.1 fusion.34
  229.6 0.7 gather_fusion.3
  230.3 0.7 gather_fusion.2
  231.0 0.8 fusion.16
  231.9 0.8 fusion.15
  (64 shorter events, 4.3 us)
Async XLA Ops:
  0.6 97.4 %copy-start = (bf16[1,1,448,2048]{3,2,1,0:T(8,128)(2,1)S(1)}, bf16[1,1,448,2048]{3,2,1,0:T(8,128)(2,1)}, u32[]{:S(2)}) copy-start(bf16[1,1,448,2048]{3,2,1,0:T(8,128)(2,1)} %param.19) | copy-start | bytes 5505028
  0.6 15.8 %collective-permute-start.1 = (bf16[32,3584]{1,0:T(8,128)(2,1)}, bf16[32,3584]{1,0:T(8,128)(2,1)S(1)}, u32[]{:S(2)}, u32[]{:S(2)}) collective-permute-start(bf16[32,3584]{1,0:T(8,128)(2,1)} %bitcast.80), channel_id=1, source_target_pairs={{64,0},{128,64},{192,128},{256,192},{320,256},{384,320},{448,384},... | collective-permute-start | bytes 688136 | tf_op jit(solution)/shard_map/ppermute | solution.py:14
  7.2 12.8 %collective-permute-start = (bf16[32,3584]{1,0:T(8,128)(2,1)}, bf16[32,3584]{1,0:T(8,128)(2,1)S(1)}, u32[]{:S(2)}, u32[]{:S(2)}) collective-permute-start(bf16[32,3584]{1,0:T(8,128)(2,1)} %bitcast.81), channel_id=1, source_target_pairs={{448,0},{0,64},{64,128},{128,192},{192,256},{256,320},{320,384},{3... | collective-permute-start | bytes 688136 | tf_op jit(solution)/shard_map/ppermute | solution.py:14
  16.5 0.7 copy-start.7
  20.0 0.7 copy-start.5
  23.8 62.0 %all-to-all-start = ((bf16[64,2,6,448]{3,1,2,0:T(2,128)(2,1)}), bf16[64,2,6,448]{3,1,2,0:T(2,128)(2,1)S(1)}, u32[]{:S(2)}, u32[]{:S(2)}) async-start(bf16[64,2,6,448]{3,1,2,0:T(2,128)(2,1)} %copy.48), calls=%async_computation | async-start | bytes 1572864 | tf_op jit(solution)/shard_map/all_to_all | solution.py:173
  91.8 6.2 %copy-start.3 = (bf16[384,448]{1,0:T(8,128)(2,1)S(1)}, bf16[384,448]{1,0:T(8,128)(2,1)}, u32[]{:S(2)}) copy-start(bf16[384,448]{1,0:T(8,128)(2,1)} %reshape_squeeze.11) | copy-start | bytes 1032196
  99.0 2.4 %copy-start.1 = (f32[384,2048]{1,0:T(8,128)}, f32[384,2048]{1,0:T(8,128)S(1)}, u32[]{:S(2)}) copy-start(f32[384,2048]{1,0:T(8,128)S(1)} %fusion.3) | copy-start | bytes 9437188
  101.4 6.8 %collective-permute-start.2 = (f32[192,3072]{1,0:T(8,128)}, f32[192,3072]{1,0:T(8,128)}, u32[]{:S(2)}, u32[]{:S(2)}) collective-permute-start(f32[192,3072]{1,0:T(8,128)} %broadcast_select_fusion), channel_id=1, source_target_pairs={{0,1},{1,0},{2,3},{3,2},{4,5},{5,4},{6,7},{7,6},{8,9},{9,8},{10,11... | collective-permute-start | bytes 7077896 | tf_op jit(solution)/shard_map/ppermute | solution.py:95
  111.2 1.4 copy-start.2
  113.7 18.3 %collective-permute-start.3 = (f32[96,3072]{1,0:T(8,128)}, f32[96,3072]{1,0:T(8,128)S(1)}, u32[]{:S(2)}, u32[]{:S(2)}) collective-permute-start(f32[96,3072]{1,0:T(8,128)} %slice_select_fusion), channel_id=1, source_target_pairs={{0,2},{1,5},{2,0},{3,7},{4,6},{5,1},{6,4},{7,3},{8,10},{9,13},{10,... | collective-permute-start | bytes 3538952 | tf_op jit(solution)/shard_map/ppermute | solution.py:95
  133.8 12.0 %copy-start.9 = (bf16[1,1,48,2048]{3,2,1,0:T(8,128)(2,1)S(1)}, bf16[1,1,48,2048]{3,2,1,0:T(8,128)(2,1)}, u32[]{:S(2)}) copy-start(bf16[1,1,48,2048]{3,2,1,0:T(8,128)(2,1)} %param.21) | copy-start | bytes 589828
  133.9 11.8 %collective-permute-start.4 = (f32[48,3072]{1,0:T(8,128)S(1)}, f32[48,3072]{1,0:T(8,128)S(1)}, u32[]{:S(2)}, u32[]{:S(2)}) collective-permute-start(f32[48,3072]{1,0:T(8,128)S(1)} %slice_select_fusion.1), channel_id=1, source_target_pairs={{0,4},{1,3},{2,6},{3,1},{4,0},{5,7},{6,2},{7,5},{8,12},{9,11},{10,... | collective-permute-start | bytes 1769480 | tf_op jit(solution)/shard_map/ppermute | solution.py:95
  146.0 8.6 %collective-permute-start.5 = (bf16[48,3072]{1,0:T(8,128)(2,1)S(1)}, bf16[48,3072]{1,0:T(8,128)(2,1)S(1)}, u32[]{:S(2)}, u32[]{:S(2)}) collective-permute-start(bf16[48,3072]{1,0:T(8,128)(2,1)S(1)} %pad_maximum_fusion.3), channel_id=1, source_target_pairs={{0,4},{1,3},{2,6},{3,1},{4,0},{5,7},{6,2},{7,5},{8,12},{9,11},{10,... | collective-permute-start | bytes 884744 | tf_op jit(solution)/shard_map/ppermute | solution.py:103
  154.8 11.8 %collective-permute-start.6 = (bf16[96,3072]{1,0:T(8,128)(2,1)S(1)}, bf16[96,3072]{1,0:T(8,128)(2,1)S(1)}, u32[]{:S(2)}, u32[]{:S(2)}) collective-permute-start(bf16[96,3072]{1,0:T(8,128)(2,1)S(1)} %maximum_select_fusion.2), channel_id=1, source_target_pairs={{0,2},{1,5},{2,0},{3,7},{4,6},{5,1},{6,4},{7,3},{8,10},{9,13},{10,... | collective-permute-start | bytes 1769480 | tf_op jit(solution)/shard_map/ppermute | solution.py:103
  166.8 4.7 %collective-permute-start.7 = (bf16[192,3072]{1,0:T(8,128)(2,1)S(1)}, bf16[192,3072]{1,0:T(8,128)(2,1)S(1)}, u32[]{:S(2)}, u32[]{:S(2)}) collective-permute-start(bf16[192,3072]{1,0:T(8,128)(2,1)S(1)} %maximum_select_fusion.1), channel_id=1, source_target_pairs={{0,1},{1,0},{2,3},{3,2},{4,5},{5,4},{6,7},{7,6},{8,9},{9,8},{10,11... | collective-permute-start | bytes 3538952 | tf_op jit(solution)/shard_map/ppermute | solution.py:103
  172.5 1.2 copy-start.4
  229.2 1.8 copy-start.8
  229.2 1.8 copy-start.10
  229.6 2.3 copy-start.6
  229.6 2.3 copy-start.11

commit v2 on v1

v2 whole, which is shorter than its diff:
```python
import numpy as np
import jax
import jax.numpy as jnp
from jax import lax
from jax.sharding import PartitionSpec as P

EXPERTS = 8
MOST = 6


def shifted(block, axis, distance):
    devices = range(lax.axis_size(axis))
    route = [((i - distance) % len(devices), i) for i in devices]
    return lax.ppermute(block, axis, route)


def slot_tables(routes, experts, capacity):
    paths, tok_rows, top_count = routes.shape
    flat = routes.reshape(paths, tok_rows * top_count)
    pairs = flat.shape[1]
    earlier = jnp.arange(pairs)[None, :] < jnp.arange(pairs)[:, None]
    same = (flat[:, :, None] == flat[:, None, :]) & earlier[None]
    rank_within = jnp.sum(same.astype(jnp.int32), axis=2)
    return (flat * capacity + rank_within).reshape(paths, tok_rows, top_count)


def stage_bits(member_bits):
    core = member_bits[0]
    return [0, 1 if core == 0 else 2, 2 if core == 0 else 1]


def member_bits_of(member, group_size):
    return [member >> b & 1 for b in range(group_size.bit_length() - 1)]


def stage_route(axis_count, group_size, stage):
    route = []
    for index in range(axis_count):
        bits = member_bits_of(index % group_size, group_size)
        bit = stage_bits(bits)[stage]
        route.append((index, index ^ (1 << bit)))
    return route


def block_order(group_size):
    order = [0] * group_size
    for member in range(group_size):
        bits = member_bits_of(member, group_size)
        pos = 0
        for bit in stage_bits(bits):
            pos = pos * 2 + bits[bit]
        order[pos] = member
    return order


def own_stage_bit(index, group_size, stage):
    member = index % group_size
    core = member & 1
    if stage == 0:
        bit = 0
    elif stage == 1:
        bit = jnp.where(core == 0, 1, 2)
    else:
        bit = jnp.where(core == 0, 2, 1)
    return (member >> bit & 1).astype(jnp.int32)


def body(
    acts_down,
    routes_down,
    gates_down,
    grads_up,
    routes_up,
    gates_up,
    weight_in,
    weight_out,
    saved_pre,
):
    devices = lax.axis_size("expert")
    group_size = devices // EXPERTS
    levels = group_size.bit_length() - 1
    index = lax.axis_index("expert")
    model_width = acts_down.shape[2]
    share_width = model_width // group_size
    slot_count = EXPERTS * MOST
    proj_in = weight_in[0, 0]
    proj_out = weight_out[0, 0]
    hidden_units = proj_out.shape[0]
    order = block_order(group_size)

    saved_route = [
        (i, (i // group_size) * group_size + order[i % group_size]) for i in range(devices)
    ]
    saved = lax.ppermute(saved_pre[0, 0], "expert", saved_route)

    arrived = shifted(acts_down[0], "pipe", 1)
    incoming = shifted(grads_up[0], "pipe", -1)
    tokens = jnp.stack([arrived, incoming])
    routes = jnp.stack([routes_down[0], routes_up[0]])
    gates = jnp.stack([gates_down[0], gates_up[0]]).astype(jnp.float32)
    slots = slot_tables(routes, EXPERTS, MOST)
    onehot = (
        slots.transpose(0, 2, 1)[:, :, None, :]
        == jnp.arange(slot_count, dtype=jnp.int32)[None, None, :, None]
    ).astype(jnp.bfloat16)
    dispatch = jnp.sum(onehot, axis=1).reshape(2, EXPERTS, MOST, -1)
    token_parts = tokens.reshape(2, tokens.shape[1], group_size, share_width)
    sent = jnp.einsum(
        "prjt,pthc->rhpjc", dispatch, token_parts, preferred_element_type=jnp.float32
    ).astype(jnp.bfloat16)
    sent = sent.reshape(devices, 2, MOST, share_width)
    got = lax.all_to_all(sent, "expert", split_axis=0, concat_axis=0, tiled=True)
    rows_down = got[:, 0].reshape(-1, share_width)
    rows_up = got[:, 1].reshape(-1, share_width)

    def first_partial(start, count):
        part_down = lax.dynamic_slice_in_dim(rows_down, start, count, axis=0)
        part_up = lax.dynamic_slice_in_dim(rows_up, start, count, axis=0)
        pre = jnp.dot(part_down, proj_in, preferred_element_type=jnp.float32)
        grad = lax.dot_general(
            part_up, proj_out, (((1,), (1,)), ((), ())), preferred_element_type=jnp.float32
        )
        return jnp.concatenate([pre, grad], axis=1)

    half = rows_down.shape[0] // 2
    bit = own_stage_bit(index, group_size, 0)
    send_part = first_partial((1 - bit) * half, half)
    received = lax.ppermute(send_part, "expert", stage_route(devices, group_size, 0))
    current = first_partial(bit * half, half) + received
    for stage in range(1, levels):
        half = current.shape[0] // 2
        bit = own_stage_bit(index, group_size, stage)
        kept = lax.dynamic_slice_in_dim(current, bit * half, half, axis=0)
        send_part = lax.dynamic_slice_in_dim(current, (1 - bit) * half, half, axis=0)
        received = lax.ppermute(send_part, "expert", stage_route(devices, group_size, stage))
        current = kept + received

    pre_share = current[:, : 2 * hidden_units]
    hidden_grad = current[:, 2 * hidden_units :]
    hidden_share = (
        jax.nn.silu(pre_share[:, :hidden_units]) * pre_share[:, hidden_units:]
    ).astype(jnp.bfloat16)
    gate_pre = saved[:, :hidden_units].astype(jnp.float32)
    up_pre = saved[:, hidden_units:].astype(jnp.float32)
    sigmoid_gate = jax.nn.sigmoid(gate_pre)
    gate_grad = hidden_grad * up_pre * sigmoid_gate * (1.0 + gate_pre * (1.0 - sigmoid_gate))
    up_grad = hidden_grad * gate_pre * sigmoid_gate
    current = jnp.concatenate([hidden_share, gate_grad.astype(jnp.bfloat16), up_grad.astype(jnp.bfloat16)], axis=1)

    for stage in reversed(range(1, levels)):
        bit = own_stage_bit(index, group_size, stage)
        partner = lax.ppermute(current, "expert", stage_route(devices, group_size, stage))
        current = jnp.where(
            bit == 1,
            jnp.concatenate([partner, current], axis=0),
            jnp.concatenate([current, partner], axis=0),
        )

    def last_matmul(block):
        out_down = jnp.dot(
            block[:, :hidden_units], proj_out, preferred_element_type=jnp.float32
        ).astype(jnp.bfloat16)
        out_up = lax.dot_general(
            block[:, hidden_units:], proj_in, (((1,), (1,)), ((), ())),
            preferred_element_type=jnp.float32,
        ).astype(jnp.bfloat16)
        return jnp.stack([out_down, out_up])

    bit = own_stage_bit(index, group_size, 0)
    partner = lax.ppermute(current, "expert", stage_route(devices, group_size, 0))
    own_out = last_matmul(current)
    partner_out = last_matmul(partner)
    result = jnp.where(
        bit == 1,
        jnp.concatenate([partner_out, own_out], axis=1),
        jnp.concatenate([own_out, partner_out], axis=1),
    )
    result = result.reshape(2, devices, MOST, share_width).transpose(1, 0, 2, 3)
    back = lax.all_to_all(result, "expert", split_axis=0, concat_axis=0, tiled=True)
    back = back.reshape(EXPERTS, group_size, 2, MOST, share_width)
    gathered = jnp.einsum(
        "pkrjt,rhpjc->ptkhc",
        onehot.reshape(2, -1, EXPERTS, MOST, onehot.shape[-1]),
        back,
        preferred_element_type=jnp.float32,
    )
    gathered = gathered.reshape(2, tokens.shape[1], -1, model_width)
    summed = tokens.astype(jnp.float32) + jnp.sum(gates[..., None] * gathered, axis=2)
    summed = summed.astype(jnp.bfloat16)
    return (summed[0][None], summed[1][None])


def solution(mesh):
    placed = (
        P("pipe", "expert", None),
        P("pipe", "expert", None),
        P("pipe", "expert", None),
        P("pipe", "expert", None),
        P("pipe", "expert", None),
        P("pipe", "expert", None),
        P("pipe", "expert", None, None),
        P("pipe", "expert", None, None),
        P("pipe", "expert", None, None),
    )
    return jax.shard_map(
        body,
        mesh=mesh,
        in_specs=placed,
        out_specs=(P("pipe", "expert", None), P("pipe", "expert", None)),
        check_vma=False,
    )
```

time: 233 us -> 231 us (level)
  blocking collectives: 48.7 us -> 0 us
  waiting for transfers between devices: 95.4 us -> 138 us
  starting transfers between devices: 38.3 us -> 50.3 us
  local copies, waits for them, and re-layouts: 26 us -> 17.4 us
  other arithmetic: 17.7 us -> 13.1 us
  matrix products: 5.36 us -> 9.84 us
    all_to_all x1 -> x0, blocking collectives: 48.7 us -> none  [body(): lax.all_to_all(result, 'expert', split_axis=0, concat_axis=0, tiled=True)]
    all_to_all x0 -> x1, waiting for transfers between devices: none -> 44.9 us  [body(): lax.all_to_all(result, 'expert', split_axis=0, concat_axis=0, tiled=True)]
    ppermute x6 -> x7, waiting for transfers between devices: 49.2 us -> 41.8 us  [the longest x2 25.2 us: body(): lax.ppermute(send_part, 'expert', stage_route(devices, group_size, stage))]
    all_to_all x0 -> x1, starting transfers between devices: none -> 6.1 us  [body(): lax.all_to_all(result, 'expert', split_axis=0, concat_axis=0, tiled=True)]
    ppermute x2, waiting for transfers between devices: 1.42 us -> 6.51 us  [shifted(): return lax.ppermute(block, axis, route)]
    ppermute x6 -> x7, starting transfers between devices: 12.7 us -> 17.5 us  [the longest x2 8.47 us: body(): lax.ppermute(current, 'expert', stage_route(devices, group_size, stage))]
    dot_general x4 -> x10, matrix products: 5.36 us -> 9.84 us  [the longest x2 3.6 us: last_matmul(): lax.dot_general(block[:, hidden_units:], proj_in, (((1,), (1,)), ((), ())...]
    unnamed x33 -> x24, local copies, waits for them, and re-layouts: 7.84 us -> 3.37 us
  transfers between devices with their start and end apart: 9 -> 11, of which waited for: 8 -> 9; matrix products, arithmetic and copies ran while one was open for 4% -> 3% of each run, Pallas kernels for 0% -> 0%
where the time goes in v2:
time: 231 us; the launch traced here: 230 us
  waiting for transfers between devices  138 us (60%)
  starting transfers between devices  50.3 us (22%)
  local copies, waits for them, and re-layouts  17.4 us (8%)
  other arithmetic  13.1 us (6%)
  matrix products  9.84 us (4%)
    all_to_all x1, waiting for transfers between devices, body(): lax.all_to_all(result, 'expert', split_axis=0, concat_axis=0, tiled=True)  44.9 us
    all_to_all x1, waiting for transfers between devices, body(): lax.all_to_all(sent, 'expert', split_axis=0, concat_axis=0, tiled=True)  44.8 us
    ppermute x2, waiting for transfers between devices, body(): lax.ppermute(send_part, 'expert', stage_route(devices, group_size, stage))  25.2 us
    all_to_all x1, starting transfers between devices, body(): lax.all_to_all(sent, 'expert', split_axis=0, concat_axis=0, tiled=True)  17.1 us
    ppermute x2, waiting for transfers between devices, body(): lax.ppermute(current, 'expert', stage_route(devices, group_size, stage))  12.7 us
    ppermute x2, starting transfers between devices, shifted(): return lax.ppermute(block, axis, route)  9.59 us
    ppermute x2, starting transfers between devices, body(): lax.ppermute(current, 'expert', stage_route(devices, group_size, stage))  8.47 us
    ppermute x2, waiting for transfers between devices, shifted(): return lax.ppermute(block, axis, route)  6.51 us
  transfers between devices with their start and end apart: 11, of which 9 were waited for; matrix products, arithmetic and copies ran while one was open for 3% of the time, Pallas kernels for 0%

profile of v2, /device:TPU:8, one launch (start us, length us, event | category | flops | bytes accessed | tf_op | source)
XLA Modules:
  0.0 229.7 jit_solution(8892186118910994563)
XLA Ops:
  0.6 0.0 copy-start
  0.6 4.3 %collective-permute-start = (bf16[32,3584]{1,0:T(8,128)(2,1)}, bf16[32,3584]{1,0:T(8,128)(2,1)S(1)}, u32[]{:S(2)}, u32[]{:S(2)}) collective-permute-start(bf16[32,3584]{1,0:T(8,128)(2,1)} %bitcast.79), channel_id=1, source_target_pairs={{448,0},{0,64},{64,128},{128,192},{192,256},{256,320},{320,384},{3... | collective-permute-start | bytes 688136 | tf_op jit(solution)/shard_map/ppermute | solution.py:14
  5.0 5.3 %collective-permute-start.1 = (bf16[32,3584]{1,0:T(8,128)(2,1)}, bf16[32,3584]{1,0:T(8,128)(2,1)S(1)}, u32[]{:S(2)}, u32[]{:S(2)}) collective-permute-start(bf16[32,3584]{1,0:T(8,128)(2,1)} %bitcast.80), channel_id=1, source_target_pairs={{64,0},{128,64},{192,128},{256,192},{320,256},{384,320},{448,384},... | collective-permute-start | bytes 688136 | tf_op jit(solution)/shard_map/ppermute | solution.py:14
  10.3 0.7 pad_add_fusion
  10.9 0.2 convert_reduce_fusion
  11.1 2.8 %collective-permute-done = bf16[32,3584]{1,0:T(8,128)(2,1)S(1)} collective-permute-done((bf16[32,3584]{1,0:T(8,128)(2,1)}, bf16[32,3584]{1,0:T(8,128)(2,1)S(1)}, u32[]{:S(2)}, u32[]{:S(2)}) %collective-permute-start) | collective-permute-done | bytes 229408 | tf_op jit(solution)/shard_map/ppermute | solution.py:14
  13.9 0.7 copy-done.4
  14.6 0.3 stack.43
  14.9 0.1 copy.36
  15.0 3.7 %collective-permute-done.1 = bf16[32,3584]{1,0:T(8,128)(2,1)S(1)} collective-permute-done((bf16[32,3584]{1,0:T(8,128)(2,1)}, bf16[32,3584]{1,0:T(8,128)(2,1)S(1)}, u32[]{:S(2)}, u32[]{:S(2)}) %collective-permute-start.1) | collective-permute-done | bytes 229408 | tf_op jit(solution)/shard_map/ppermute | solution.py:14
  18.8 0.3 stack.44
  19.1 0.1 copy.37
  19.2 0.4 fusion.8
  19.6 0.4 copy.54
  20.0 1.7 copy.39
  21.7 17.1 %all-to-all-start = ((bf16[64,2,6,448]{3,1,2,0:T(2,128)(2,1)}), bf16[64,2,6,448]{3,1,2,0:T(2,128)(2,1)S(1)}, u32[]{:S(2)}, u32[]{:S(2)}) async-start(bf16[64,2,6,448]{3,1,2,0:T(2,128)(2,1)} %copy.39), calls=%async_computation | async-start | bytes 1572864 | tf_op jit(solution)/shard_map/all_to_all | solution.py:112
  38.9 44.8 %all-to-all-done = bf16[64,2,6,448]{3,1,2,0:T(2,128)(2,1)S(1)} async-done(((bf16[64,2,6,448]{3,1,2,0:T(2,128)(2,1)}), bf16[64,2,6,448]{3,1,2,0:T(2,128)(2,1)S(1)}, u32[]{:S(2)}, u32[]{:S(2)}) %all-to-all-start) | async-done | bytes 688160 | tf_op jit(solution)/shard_map/all_to_all | solution.py:112
  83.7 4.2 %slice_reduce_fusion.1 = (bf16[64,6,448]{2,1,0:T(8,128)(2,1)}, bf16[64,6,448]{2,1,0:T(8,128)(2,1)S(1)}) fusion(bf16[64,2,6,448]{3,1,2,0:T(2,128)(2,1)S(1)} %all-to-all-done), kind=kLoop, calls=%fused_computation.33 | loop fusion | bytes 1376256 | tf_op jit(solution)/shard_map/slice | solution.py:113
  87.9 1.3 reshape_squeeze.6
  89.2 0.2 reshape_squeeze.7
  89.4 0.0 copy-start.2
  89.4 0.6 fusion.4
  90.0 0.6 copy-done.2
  90.6 0.4 fusion.25
  91.0 1.6 pad_maximum_fusion
  92.6 1.9 collective-permute-start.2
  94.5 0.4 fusion.27
  94.9 0.6 fusion.6
  95.4 3.9 %collective-permute-done.2 = f32[192,3072]{1,0:T(8,128)} collective-permute-done((f32[192,3072]{1,0:T(8,128)}, f32[192,3072]{1,0:T(8,128)}, u32[]{:S(2)}, u32[]{:S(2)}) %collective-permute-start.2) | collective-permute-done | bytes 2359328 | tf_op jit(solution)/shard_map/ppermute | solution.py:128
  99.3 1.9 maximum_add_fusion
  101.2 1.4 copy-done.1
  102.7 0.1 constant_dynamic-slice_fusion.1
  102.7 2.4 %collective-permute-start.3 = (f32[96,3072]{1,0:T(8,128)S(1)}, f32[96,3072]{1,0:T(8,128)}, u32[]{:S(2)}, u32[]{:S(2)}) collective-permute-start(f32[96,3072]{1,0:T(8,128)S(1)} %constant_dynamic-slice_fusion.1), channel_id=1, source_target_pairs={{0,2},{1,5},{2,0},{3,7},{4,6},{5,1},{6,4},{7,3},{8,10},{9,13},{10,... | collective-permute-start | bytes 3538952 | tf_op jit(solution)/shard_map/ppermute | solution.py:135
  105.2 15.7 %collective-permute-done.3 = f32[96,3072]{1,0:T(8,128)} collective-permute-done((f32[96,3072]{1,0:T(8,128)S(1)}, f32[96,3072]{1,0:T(8,128)}, u32[]{:S(2)}, u32[]{:S(2)}) %collective-permute-start.3) | collective-permute-done | bytes 1179680 | tf_op jit(solution)/shard_map/ppermute | solution.py:135
  121.0 1.7 dynamic-slice_add_fusion
  122.7 0.9 constant_dynamic-slice_fusion
  123.6 1.9 collective-permute-start.4
  125.5 0.7 collective-permute-start.5
  126.2 9.5 %collective-permute-done.4 = f32[48,3072]{1,0:T(8,128)} collective-permute-done((f32[48,3072]{1,0:T(8,128)}, f32[48,3072]{1,0:T(8,128)}, u32[]{:S(2)}, u32[]{:S(2)}) %collective-permute-start.4) | collective-permute-done | bytes 589856 | tf_op jit(solution)/shard_map/ppermute | solution.py:135
  135.7 1.1 dynamic-slice_add_fusion.1
  136.8 0.2 fusion.41
  137.0 0.6 copy-done.8
  137.6 4.0 %collective-permute-start.6 = (bf16[48,3072]{1,0:T(8,128)(2,1)S(1)}, bf16[48,3072]{1,0:T(8,128)(2,1)}, u32[]{:S(2)}, u32[]{:S(2)}) collective-permute-start(bf16[48,3072]{1,0:T(8,128)(2,1)S(1)} %pad_maximum_fusion.1), channel_id=1, source_target_pairs={{0,4},{1,3},{2,6},{3,1},{4,0},{5,7},{6,2},{7,5},{8,12},{9,11},{10,... | collective-permute-start | bytes 884744 | tf_op jit(solution)/shard_map/ppermute | solution.py:152
  141.7 4.8 %collective-permute-done.6 = bf16[48,3072]{1,0:T(8,128)(2,1)} collective-permute-done((bf16[48,3072]{1,0:T(8,128)(2,1)S(1)}, bf16[48,3072]{1,0:T(8,128)(2,1)}, u32[]{:S(2)}, u32[]{:S(2)}) %collective-permute-start.6) | collective-permute-done | bytes 294944 | tf_op jit(solution)/shard_map/ppermute | solution.py:152
  146.4 1.3 maximum_select_fusion.2
  147.7 4.4 %collective-permute-start.7 = (bf16[96,3072]{1,0:T(8,128)(2,1)S(1)}, bf16[96,3072]{1,0:T(8,128)(2,1)}, u32[]{:S(2)}, u32[]{:S(2)}) collective-permute-start(bf16[96,3072]{1,0:T(8,128)(2,1)S(1)} %maximum_select_fusion.2), channel_id=1, source_target_pairs={{0,2},{1,5},{2,0},{3,7},{4,6},{5,1},{6,4},{7,3},{8,10},{9,13},{10,... | collective-permute-start | bytes 1769480 | tf_op jit(solution)/shard_map/ppermute | solution.py:152
  152.2 8.0 %collective-permute-done.7 = bf16[96,3072]{1,0:T(8,128)(2,1)} collective-permute-done((bf16[96,3072]{1,0:T(8,128)(2,1)S(1)}, bf16[96,3072]{1,0:T(8,128)(2,1)}, u32[]{:S(2)}, u32[]{:S(2)}) %collective-permute-start.7) | collective-permute-done | bytes 589856 | tf_op jit(solution)/shard_map/ppermute | solution.py:152
  160.1 2.7 %maximum_select_fusion = bf16[192,3072]{1,0:T(8,128)(2,1)} fusion(bf16[96,3072]{1,0:T(8,128)(2,1)S(1)} %maximum_select_fusion.2, bf16[96,3072]{1,0:T(8,128)(2,1)} %collective-permute-done.7, pred[]{:T(512)S(6)} %eq.63), kind=kLoop, calls=%fused_computation.13 | loop fusion | flops 5308416 | bytes 2359297 | tf_op jit(solution)/shard_map/jit(_where)/select_n | solution.py:153
  162.8 2.1 collective-permute-start.8
  165.0 1.4 fusion.22
  166.4 1.8 fusion.15
  168.2 1.8 fusion.18
  170.0 1.4 fusion.21
  171.5 0.3 maximum_select_fusion.1
  171.8 0.0 copy-start.9
  171.8 0.0 copy-start.10
  171.8 1.7 copy.40
  173.5 6.1 %all-to-all-start.1 = ((bf16[64,2,6,448]{3,1,2,0:T(2,128)(2,1)}), bf16[64,2,6,448]{3,1,2,0:T(2,128)(2,1)S(1)}, u32[]{:S(2)}, u32[]{:S(2)}) async-start(bf16[64,2,6,448]{3,1,2,0:T(2,128)(2,1)} %bitcast.20), calls=%async_computation.1 | async-start | bytes 1572864 | tf_op jit(solution)/shard_map/all_to_all | solution.py:179
  179.6 44.9 %all-to-all-done.1 = bf16[64,2,6,448]{3,1,2,0:T(2,128)(2,1)S(1)} async-done(((bf16[64,2,6,448]{3,1,2,0:T(2,128)(2,1)}), bf16[64,2,6,448]{3,1,2,0:T(2,128)(2,1)S(1)}, u32[]{:S(2)}, u32[]{:S(2)}) %all-to-all-start.1) | async-done | bytes 688160 | tf_op jit(solution)/shard_map/all_to_all | solution.py:179
  224.5 1.1 convolution_bitcast_fusion
  225.6 0.6 copy.43
  226.2 1.3 reshape.71
  227.6 1.4 add_convert_fusion
  228.9 0.8 fusion.62
  (23 shorter events, 0.1 us)
Async XLA Ops:
  0.6 88.8 %copy-start = (bf16[1,1,448,2048]{3,2,1,0:T(8,128)(2,1)S(1)}, bf16[1,1,448,2048]{3,2,1,0:T(8,128)(2,1)}, u32[]{:S(2)}) copy-start(bf16[1,1,448,2048]{3,2,1,0:T(8,128)(2,1)} %param.15) | copy-start | bytes 5505028
  0.6 13.3 %collective-permute-start = (bf16[32,3584]{1,0:T(8,128)(2,1)}, bf16[32,3584]{1,0:T(8,128)(2,1)S(1)}, u32[]{:S(2)}, u32[]{:S(2)}) collective-permute-start(bf16[32,3584]{1,0:T(8,128)(2,1)} %bitcast.79), channel_id=1, source_target_pairs={{448,0},{0,64},{64,128},{128,192},{192,256},{256,320},{320,384},{3... | collective-permute-start | bytes 688136 | tf_op jit(solution)/shard_map/ppermute | solution.py:14
  5.0 13.8 %collective-permute-start.1 = (bf16[32,3584]{1,0:T(8,128)(2,1)}, bf16[32,3584]{1,0:T(8,128)(2,1)S(1)}, u32[]{:S(2)}, u32[]{:S(2)}) collective-permute-start(bf16[32,3584]{1,0:T(8,128)(2,1)} %bitcast.80), channel_id=1, source_target_pairs={{64,0},{128,64},{192,128},{256,192},{320,256},{384,320},{448,384},... | collective-permute-start | bytes 688136 | tf_op jit(solution)/shard_map/ppermute | solution.py:14
  13.9 0.7 copy-start.4
  18.8 1.3 copy-start.6
  21.7 61.9 %all-to-all-start = ((bf16[64,2,6,448]{3,1,2,0:T(2,128)(2,1)}), bf16[64,2,6,448]{3,1,2,0:T(2,128)(2,1)S(1)}, u32[]{:S(2)}, u32[]{:S(2)}) async-start(bf16[64,2,6,448]{3,1,2,0:T(2,128)(2,1)} %copy.39), calls=%async_computation | async-start | bytes 1572864 | tf_op jit(solution)/shard_map/all_to_all | solution.py:112
  89.4 1.2 copy-start.2
  92.6 6.8 %collective-permute-start.2 = (f32[192,3072]{1,0:T(8,128)}, f32[192,3072]{1,0:T(8,128)}, u32[]{:S(2)}, u32[]{:S(2)}) collective-permute-start(f32[192,3072]{1,0:T(8,128)} %pad_maximum_fusion), channel_id=1, source_target_pairs={{0,1},{1,0},{2,3},{3,2},{4,5},{5,4},{6,7},{7,6},{8,9},{9,8},{10,11... | collective-permute-start | bytes 7077896 | tf_op jit(solution)/shard_map/ppermute | solution.py:128
  101.2 1.4 copy-start.1
  102.7 18.2 %collective-permute-start.3 = (f32[96,3072]{1,0:T(8,128)S(1)}, f32[96,3072]{1,0:T(8,128)}, u32[]{:S(2)}, u32[]{:S(2)}) collective-permute-start(f32[96,3072]{1,0:T(8,128)S(1)} %constant_dynamic-slice_fusion.1), channel_id=1, source_target_pairs={{0,2},{1,5},{2,0},{3,7},{4,6},{5,1},{6,4},{7,3},{8,10},{9,13},{10,... | collective-permute-start | bytes 3538952 | tf_op jit(solution)/shard_map/ppermute | solution.py:135
  105.2 20.3 %copy-start.11 = (bf16[1,1,48,2048]{3,2,1,0:T(8,128)(2,1)S(1)}, bf16[1,1,48,2048]{3,2,1,0:T(8,128)(2,1)}, u32[]{:S(2)}) copy-start(bf16[1,1,48,2048]{3,2,1,0:T(8,128)(2,1)} %param.17) | copy-start | bytes 589828
  123.6 12.1 %collective-permute-start.4 = (f32[48,3072]{1,0:T(8,128)}, f32[48,3072]{1,0:T(8,128)}, u32[]{:S(2)}, u32[]{:S(2)}) collective-permute-start(f32[48,3072]{1,0:T(8,128)} %constant_dynamic-slice_fusion), channel_id=1, source_target_pairs={{0,4},{1,3},{2,6},{3,1},{4,0},{5,7},{6,2},{7,5},{8,12},{9,11},{10,... | collective-permute-start | bytes 1769480 | tf_op jit(solution)/shard_map/ppermute | solution.py:135
  125.5 11.3 %collective-permute-start.5 = (bf16[48,2048]{1,0:T(8,128)(2,1)S(1)}, bf16[48,2048]{1,0:T(8,128)(2,1)S(1)}, u32[]{:S(2)}, u32[]{:S(2)}) collective-permute-start(bf16[48,2048]{1,0:T(8,128)(2,1)S(1)} %bitcast.81), channel_id=1, source_target_pairs={{0,0},{1,4},{2,2},{3,6},{4,1},{5,3},{6,5},{7,7},{8,8},{9,12},{10,1... | collective-permute-start | bytes 589832 | tf_op jit(solution)/shard_map/ppermute | solution.py:94
  137.0 0.6 copy-start.8
  137.6 8.8 %collective-permute-start.6 = (bf16[48,3072]{1,0:T(8,128)(2,1)S(1)}, bf16[48,3072]{1,0:T(8,128)(2,1)}, u32[]{:S(2)}, u32[]{:S(2)}) collective-permute-start(bf16[48,3072]{1,0:T(8,128)(2,1)S(1)} %pad_maximum_fusion.1), channel_id=1, source_target_pairs={{0,4},{1,3},{2,6},{3,1},{4,0},{5,7},{6,2},{7,5},{8,12},{9,11},{10,... | collective-permute-start | bytes 884744 | tf_op jit(solution)/shard_map/ppermute | solution.py:152
  141.7 23.3 %copy-start.3 = (bf16[1,1,1024,448]{2,3,1,0:T(8,128)(2,1)S(1)}, bf16[1,1,1024,448]{2,3,1,0:T(8,128)(2,1)}, u32[]{:S(2)}) copy-start(bf16[1,1,1024,448]{2,3,1,0:T(8,128)(2,1)} %param.16) | copy-start | bytes 2752516
  147.7 12.4 %collective-permute-start.7 = (bf16[96,3072]{1,0:T(8,128)(2,1)S(1)}, bf16[96,3072]{1,0:T(8,128)(2,1)}, u32[]{:S(2)}, u32[]{:S(2)}) collective-permute-start(bf16[96,3072]{1,0:T(8,128)(2,1)S(1)} %maximum_select_fusion.2), channel_id=1, source_target_pairs={{0,2},{1,5},{2,0},{3,7},{4,6},{5,1},{6,4},{7,3},{8,10},{9,13},{10,... | collective-permute-start | bytes 1769480 | tf_op jit(solution)/shard_map/ppermute | solution.py:152
  162.8 5.4 %collective-permute-start.8 = (bf16[192,3072]{1,0:T(8,128)(2,1)}, bf16[192,3072]{1,0:T(8,128)(2,1)}, u32[]{:S(2)}, u32[]{:S(2)}) collective-permute-start(bf16[192,3072]{1,0:T(8,128)(2,1)} %maximum_select_fusion), channel_id=1, source_target_pairs={{0,1},{1,0},{2,3},{3,2},{4,5},{5,4},{6,7},{7,6},{8,9},{9,8},{10,11... | collective-permute-start | bytes 3538952 | tf_op jit(solution)/shard_map/ppermute | solution.py:170
  171.8 7.8 %copy-start.9 = (f32[1,32,1]{1,2,0:T(1,128)S(1)}, f32[1,32,1]{1,2,0:T(1,128)}, u32[]{:S(2)}) copy-start(f32[1,32,1]{1,2,0:T(1,128)} %param.14) | copy-start | bytes 388
  171.8 7.8 %copy-start.10 = (f32[1,32,1]{1,2,0:T(1,128)S(1)}, f32[1,32,1]{1,2,0:T(1,128)}, u32[]{:S(2)}) copy-start(f32[1,32,1]{1,2,0:T(1,128)} %param.11) | copy-start | bytes 388
  173.5 51.0 %all-to-all-start.1 = ((bf16[64,2,6,448]{3,1,2,0:T(2,128)(2,1)}), bf16[64,2,6,448]{3,1,2,0:T(2,128)(2,1)S(1)}, u32[]{:S(2)}, u32[]{:S(2)}) async-start(bf16[64,2,6,448]{3,1,2,0:T(2,128)(2,1)} %bitcast.20), calls=%async_computation.1 | async-start | bytes 1572864 | tf_op jit(solution)/shard_map/all_to_all | solution.py:179
  225.6 2.0 copy-start.5
  225.6 2.0 copy-start.7

commit v3 on v2

--- a/solution.py
+++ b/solution.py
@@ -124,16 +124,17 @@
 
     half = rows_down.shape[0] // 2
     bit = own_stage_bit(index, group_size, 0)
-    send_part = first_partial((1 - bit) * half, half)
+    send_part = first_partial((1 - bit) * half, half).astype(jnp.bfloat16)
     received = lax.ppermute(send_part, "expert", stage_route(devices, group_size, 0))
-    current = first_partial(bit * half, half) + received
+    current = first_partial(bit * half, half) + received.astype(jnp.float32)
     for stage in range(1, levels):
         half = current.shape[0] // 2
         bit = own_stage_bit(index, group_size, stage)
         kept = lax.dynamic_slice_in_dim(current, bit * half, half, axis=0)
         send_part = lax.dynamic_slice_in_dim(current, (1 - bit) * half, half, axis=0)
+        send_part = send_part.astype(jnp.bfloat16)
         received = lax.ppermute(send_part, "expert", stage_route(devices, group_size, stage))
-        current = kept + received
+        current = kept + received.astype(jnp.float32)
 
     pre_share = current[:, : 2 * hidden_units]
     hidden_grad = current[:, 2 * hidden_units :]

time: 231 us -> 220 us (0.952)
  waiting for transfers between devices: 138 us -> 127 us
    ppermute x2, waiting for transfers between devices: 25.2 us -> 14.8 us  [body(): lax.ppermute(send_part, 'expert', stage_route(devices, group_size, stage))]
where the time goes in v3:
time: 220 us; the launch traced here: 219 us
  waiting for transfers between devices  127 us (58%)
  starting transfers between devices  49.9 us (23%)
  local copies, waits for them, and re-layouts  17.1 us (8%)
  other arithmetic  13 us (6%)
  matrix products  10.9 us (5%)
    all_to_all x1, waiting for transfers between devices, body(): lax.all_to_all(result, 'expert', split_axis=0, concat_axis=0, tiled=True)  44.9 us
    all_to_all x1, waiting for transfers between devices, body(): lax.all_to_all(sent, 'expert', split_axis=0, concat_axis=0, tiled=True)  44.8 us
    all_to_all x1, starting transfers between devices, body(): lax.all_to_all(sent, 'expert', split_axis=0, concat_axis=0, tiled=True)  17.1 us
    ppermute x2, waiting for transfers between devices, body(): lax.ppermute(send_part, 'expert', stage_route(devices, group_size, stage))  14.8 us
    ppermute x2, waiting for transfers between devices, body(): lax.ppermute(current, 'expert', stage_route(devices, group_size, stage))  13.5 us
    ppermute x2, starting transfers between devices, shifted(): return lax.ppermute(block, axis, route)  9.59 us
    ppermute x2, starting transfers between devices, body(): lax.ppermute(current, 'expert', stage_route(devices, group_size, stage))  7.32 us
    ppermute x2, waiting for transfers between devices, shifted(): return lax.ppermute(block, axis, route)  6.51 us
  transfers between devices with their start and end apart: 11, of which 9 were waited for; matrix products, arithmetic and copies ran while one was open for 3% of the time, Pallas kernels for 0%

profile of v3, /device:TPU:8, one launch (start us, length us, event | category | flops | bytes accessed | tf_op | source)
XLA Modules:
  0.0 218.6 jit_solution(18309671041447855307)
XLA Ops:
  0.6 0.0 copy-start
  0.6 4.3 %collective-permute-start = (bf16[32,3584]{1,0:T(8,128)(2,1)}, bf16[32,3584]{1,0:T(8,128)(2,1)S(1)}, u32[]{:S(2)}, u32[]{:S(2)}) collective-permute-start(bf16[32,3584]{1,0:T(8,128)(2,1)} %bitcast.79), channel_id=1, source_target_pairs={{448,0},{0,64},{64,128},{128,192},{192,256},{256,320},{320,384},{3... | collective-permute-start | bytes 688136 | tf_op jit(solution)/shard_map/ppermute | solution.py:14
  5.0 5.3 %collective-permute-start.1 = (bf16[32,3584]{1,0:T(8,128)(2,1)}, bf16[32,3584]{1,0:T(8,128)(2,1)S(1)}, u32[]{:S(2)}, u32[]{:S(2)}) collective-permute-start(bf16[32,3584]{1,0:T(8,128)(2,1)} %bitcast.80), channel_id=1, source_target_pairs={{64,0},{128,64},{192,128},{256,192},{320,256},{384,320},{448,384},... | collective-permute-start | bytes 688136 | tf_op jit(solution)/shard_map/ppermute | solution.py:14
  10.3 0.7 pad_add_fusion
  10.9 0.2 convert_reduce_fusion
  11.1 2.8 %collective-permute-done = bf16[32,3584]{1,0:T(8,128)(2,1)S(1)} collective-permute-done((bf16[32,3584]{1,0:T(8,128)(2,1)}, bf16[32,3584]{1,0:T(8,128)(2,1)S(1)}, u32[]{:S(2)}, u32[]{:S(2)}) %collective-permute-start) | collective-permute-done | bytes 229408 | tf_op jit(solution)/shard_map/ppermute | solution.py:14
  13.9 0.7 copy-done.5
  14.6 0.3 stack.43
  14.9 0.1 copy.36
  15.0 3.7 %collective-permute-done.1 = bf16[32,3584]{1,0:T(8,128)(2,1)S(1)} collective-permute-done((bf16[32,3584]{1,0:T(8,128)(2,1)}, bf16[32,3584]{1,0:T(8,128)(2,1)S(1)}, u32[]{:S(2)}, u32[]{:S(2)}) %collective-permute-start.1) | collective-permute-done | bytes 229408 | tf_op jit(solution)/shard_map/ppermute | solution.py:14
  18.8 0.3 stack.44
  19.1 0.1 copy.37
  19.2 0.4 fusion.7
  19.6 0.4 copy.54
  20.0 1.7 copy.39
  21.7 17.1 %all-to-all-start = ((bf16[64,2,6,448]{3,1,2,0:T(2,128)(2,1)}), bf16[64,2,6,448]{3,1,2,0:T(2,128)(2,1)S(1)}, u32[]{:S(2)}, u32[]{:S(2)}) async-start(bf16[64,2,6,448]{3,1,2,0:T(2,128)(2,1)} %copy.39), calls=%async_computation | async-start | bytes 1572864 | tf_op jit(solution)/shard_map/all_to_all | solution.py:112
  38.9 44.8 %all-to-all-done = bf16[64,2,6,448]{3,1,2,0:T(2,128)(2,1)S(1)} async-done(((bf16[64,2,6,448]{3,1,2,0:T(2,128)(2,1)}), bf16[64,2,6,448]{3,1,2,0:T(2,128)(2,1)S(1)}, u32[]{:S(2)}, u32[]{:S(2)}) %all-to-all-start) | async-done | bytes 688160 | tf_op jit(solution)/shard_map/all_to_all | solution.py:112
  83.7 4.2 %slice_reduce_fusion.1 = (bf16[64,6,448]{2,1,0:T(8,128)(2,1)}, bf16[64,6,448]{2,1,0:T(8,128)(2,1)S(1)}) fusion(bf16[64,2,6,448]{3,1,2,0:T(2,128)(2,1)S(1)} %all-to-all-done), kind=kLoop, calls=%fused_computation.34 | loop fusion | bytes 1376256 | tf_op jit(solution)/shard_map/slice | solution.py:113
  87.9 2.0 reshape_squeeze.6
  89.9 0.2 reshape_squeeze.7
  90.2 0.0 copy-start.2
  90.2 1.6 convolution_convert_fusion
  91.8 0.4 convolution_convert_fusion.2
  92.2 1.1 pad_maximum_fusion
  93.3 2.0 collective-permute-start.2
  95.4 0.4 fusion.25
  95.8 0.6 fusion.5
  96.3 2.2 collective-permute-done.2
  98.5 1.6 maximum_add_fusion
  100.1 1.4 copy-done.1
  101.6 0.1 dynamic-slice_convert_fusion
  101.6 2.4 %collective-permute-start.3 = (bf16[96,3072]{1,0:T(8,128)(2,1)S(1)}, bf16[96,3072]{1,0:T(8,128)(2,1)}, u32[]{:S(2)}, u32[]{:S(2)}) collective-permute-start(bf16[96,3072]{1,0:T(8,128)(2,1)S(1)} %dynamic-slice_convert_fusion), channel_id=1, source_target_pairs={{0,2},{1,5},{2,0},{3,7},{4,6},{5,1},{6,4},{7,3},{8,10},{9,13},{10,... | collective-permute-start | bytes 1769480 | tf_op jit(solution)/shard_map/ppermute | solution.py:136
  104.1 0.0 copy-start.12
  104.1 9.4 %collective-permute-done.3 = bf16[96,3072]{1,0:T(8,128)(2,1)} collective-permute-done((bf16[96,3072]{1,0:T(8,128)(2,1)S(1)}, bf16[96,3072]{1,0:T(8,128)(2,1)}, u32[]{:S(2)}, u32[]{:S(2)}) %collective-permute-start.3) | collective-permute-done | bytes 589856 | tf_op jit(solution)/shard_map/ppermute | solution.py:136
  113.5 1.6 convert_add_fusion
  115.1 1.0 copy-done.3
  116.2 1.9 collective-permute-start.4
  118.1 1.3 collective-permute-start.5
  119.4 5.4 %collective-permute-done.4 = bf16[48,3072]{1,0:T(8,128)(2,1)S(1)} collective-permute-done((bf16[48,3072]{1,0:T(8,128)(2,1)S(1)}, bf16[48,3072]{1,0:T(8,128)(2,1)S(1)}, u32[]{:S(2)}, u32[]{:S(2)}) %collective-permute-start.4) | collective-permute-done | bytes 294944 | tf_op jit(solution)/shard_map/ppermute | solution.py:136
  124.8 1.1 convert_add_fusion.1
  125.9 1.1 fusion.39
  127.0 3.2 %collective-permute-start.6 = (bf16[48,3072]{1,0:T(8,128)(2,1)S(1)}, bf16[48,3072]{1,0:T(8,128)(2,1)}, u32[]{:S(2)}, u32[]{:S(2)}) collective-permute-start(bf16[48,3072]{1,0:T(8,128)(2,1)S(1)} %pad_maximum_fusion.1), channel_id=1, source_target_pairs={{0,4},{1,3},{2,6},{3,1},{4,0},{5,7},{6,2},{7,5},{8,12},{9,11},{10,... | collective-permute-start | bytes 884744 | tf_op jit(solution)/shard_map/ppermute | solution.py:153
  130.3 5.5 %collective-permute-done.6 = bf16[48,3072]{1,0:T(8,128)(2,1)} collective-permute-done((bf16[48,3072]{1,0:T(8,128)(2,1)S(1)}, bf16[48,3072]{1,0:T(8,128)(2,1)}, u32[]{:S(2)}, u32[]{:S(2)}) %collective-permute-start.6) | collective-permute-done | bytes 294944 | tf_op jit(solution)/shard_map/ppermute | solution.py:153
  135.8 1.3 maximum_select_fusion.2
  137.1 4.1 %collective-permute-start.7 = (bf16[96,3072]{1,0:T(8,128)(2,1)S(1)}, bf16[96,3072]{1,0:T(8,128)(2,1)}, u32[]{:S(2)}, u32[]{:S(2)}) collective-permute-start(bf16[96,3072]{1,0:T(8,128)(2,1)S(1)} %maximum_select_fusion.2), channel_id=1, source_target_pairs={{0,2},{1,5},{2,0},{3,7},{4,6},{5,1},{6,4},{7,3},{8,10},{9,13},{10,... | collective-permute-start | bytes 1769480 | tf_op jit(solution)/shard_map/ppermute | solution.py:153
  141.2 8.0 %collective-permute-done.7 = bf16[96,3072]{1,0:T(8,128)(2,1)} collective-permute-done((bf16[96,3072]{1,0:T(8,128)(2,1)S(1)}, bf16[96,3072]{1,0:T(8,128)(2,1)}, u32[]{:S(2)}, u32[]{:S(2)}) %collective-permute-start.7) | collective-permute-done | bytes 589856 | tf_op jit(solution)/shard_map/ppermute | solution.py:153
  149.1 2.6 %maximum_select_fusion = bf16[192,3072]{1,0:T(8,128)(2,1)} fusion(bf16[96,3072]{1,0:T(8,128)(2,1)S(1)} %maximum_select_fusion.2, bf16[96,3072]{1,0:T(8,128)(2,1)} %collective-permute-done.7, pred[]{:T(512)S(6)} %eq.63), kind=kLoop, calls=%fused_computation.14 | loop fusion | flops 5308416 | bytes 2359297 | tf_op jit(solution)/shard_map/jit(_where)/select_n | solution.py:154
  151.7 2.1 collective-permute-start.8
  153.8 1.4 fusion.21
  155.3 1.8 fusion.14
  157.1 1.8 fusion.17
  158.9 1.4 fusion.20
  160.4 0.3 maximum_select_fusion.1
  160.7 0.0 copy-start.10
  160.7 0.0 copy-start.11
  160.7 1.7 copy.40
  162.4 6.1 %all-to-all-start.1 = ((bf16[64,2,6,448]{3,1,2,0:T(2,128)(2,1)}), bf16[64,2,6,448]{3,1,2,0:T(2,128)(2,1)S(1)}, u32[]{:S(2)}, u32[]{:S(2)}) async-start(bf16[64,2,6,448]{3,1,2,0:T(2,128)(2,1)} %bitcast.20), calls=%async_computation.1 | async-start | bytes 1572864 | tf_op jit(solution)/shard_map/all_to_all | solution.py:180
  168.5 44.9 %all-to-all-done.1 = bf16[64,2,6,448]{3,1,2,0:T(2,128)(2,1)S(1)} async-done(((bf16[64,2,6,448]{3,1,2,0:T(2,128)(2,1)}), bf16[64,2,6,448]{3,1,2,0:T(2,128)(2,1)S(1)}, u32[]{:S(2)}, u32[]{:S(2)}) %all-to-all-start.1) | async-done | bytes 688160 | tf_op jit(solution)/shard_map/all_to_all | solution.py:180
  213.4 1.1 convolution_bitcast_fusion
  214.5 0.0 copy-start.8
  214.5 0.6 copy.43
  215.1 1.3 reshape.71
  216.5 1.4 add_convert_fusion
  217.8 0.8 fusion.60
  (25 shorter events, 0.1 us)
Async XLA Ops:
  0.6 89.5 %copy-start = (bf16[1,1,448,2048]{3,2,1,0:T(8,128)(2,1)S(1)}, bf16[1,1,448,2048]{3,2,1,0:T(8,128)(2,1)}, u32[]{:S(2)}) copy-start(bf16[1,1,448,2048]{3,2,1,0:T(8,128)(2,1)} %param.15) | copy-start | bytes 5505028
  0.6 13.3 %collective-permute-start = (bf16[32,3584]{1,0:T(8,128)(2,1)}, bf16[32,3584]{1,0:T(8,128)(2,1)S(1)}, u32[]{:S(2)}, u32[]{:S(2)}) collective-permute-start(bf16[32,3584]{1,0:T(8,128)(2,1)} %bitcast.79), channel_id=1, source_target_pairs={{448,0},{0,64},{64,128},{128,192},{192,256},{256,320},{320,384},{3... | collective-permute-start | bytes 688136 | tf_op jit(solution)/shard_map/ppermute | solution.py:14
  5.0 13.8 %collective-permute-start.1 = (bf16[32,3584]{1,0:T(8,128)(2,1)}, bf16[32,3584]{1,0:T(8,128)(2,1)S(1)}, u32[]{:S(2)}, u32[]{:S(2)}) collective-permute-start(bf16[32,3584]{1,0:T(8,128)(2,1)} %bitcast.80), channel_id=1, source_target_pairs={{64,0},{128,64},{192,128},{256,192},{320,256},{384,320},{448,384},... | collective-permute-start | bytes 688136 | tf_op jit(solution)/shard_map/ppermute | solution.py:14
  13.9 0.7 copy-start.5
  18.8 1.3 copy-start.7
  21.7 61.9 %all-to-all-start = ((bf16[64,2,6,448]{3,1,2,0:T(2,128)(2,1)}), bf16[64,2,6,448]{3,1,2,0:T(2,128)(2,1)S(1)}, u32[]{:S(2)}, u32[]{:S(2)}) async-start(bf16[64,2,6,448]{3,1,2,0:T(2,128)(2,1)} %copy.39), calls=%async_computation | async-start | bytes 1572864 | tf_op jit(solution)/shard_map/all_to_all | solution.py:112
  90.2 1.6 copy-start.2
  93.3 2.4 %copy-start.4 = (bf16[384,448]{1,0:T(8,128)(2,1)S(1)}, bf16[384,448]{1,0:T(8,128)(2,1)}, u32[]{:S(2)}) copy-start(bf16[384,448]{1,0:T(8,128)(2,1)} %reshape_squeeze.6) | copy-start | bytes 1032196
  93.3 5.2 %collective-permute-start.2 = (bf16[192,3072]{1,0:T(8,128)(2,1)}, bf16[192,3072]{1,0:T(8,128)(2,1)}, u32[]{:S(2)}, u32[]{:S(2)}) collective-permute-start(bf16[192,3072]{1,0:T(8,128)(2,1)} %pad_maximum_fusion), channel_id=1, source_target_pairs={{0,1},{1,0},{2,3},{3,2},{4,5},{5,4},{6,7},{7,6},{8,9},{9,8},{10,11... | collective-permute-start | bytes 3538952 | tf_op jit(solution)/shard_map/ppermute | solution.py:128
  100.1 1.4 copy-start.1
  101.6 11.9 %collective-permute-start.3 = (bf16[96,3072]{1,0:T(8,128)(2,1)S(1)}, bf16[96,3072]{1,0:T(8,128)(2,1)}, u32[]{:S(2)}, u32[]{:S(2)}) collective-permute-start(bf16[96,3072]{1,0:T(8,128)(2,1)S(1)} %dynamic-slice_convert_fusion), channel_id=1, source_target_pairs={{0,2},{1,5},{2,0},{3,7},{4,6},{5,1},{6,4},{7,3},{8,10},{9,13},{10,... | collective-permute-start | bytes 1769480 | tf_op jit(solution)/shard_map/ppermute | solution.py:136
  104.1 14.0 %copy-start.12 = (bf16[1,1,48,2048]{3,2,1,0:T(8,128)(2,1)S(1)}, bf16[1,1,48,2048]{3,2,1,0:T(8,128)(2,1)}, u32[]{:S(2)}) copy-start(bf16[1,1,48,2048]{3,2,1,0:T(8,128)(2,1)} %param.17) | copy-start | bytes 589828
  115.1 1.0 copy-start.3
  116.2 8.6 %collective-permute-start.4 = (bf16[48,3072]{1,0:T(8,128)(2,1)S(1)}, bf16[48,3072]{1,0:T(8,128)(2,1)S(1)}, u32[]{:S(2)}, u32[]{:S(2)}) collective-permute-start(bf16[48,3072]{1,0:T(8,128)(2,1)S(1)} %dynamic-slice_convert_fusion.1), channel_id=1, source_target_pairs={{0,4},{1,3},{2,6},{3,1},{4,0},{5,7},{6,2},{7,5},{8,12},{9,11},{10,... | collective-permute-start | bytes 884744 | tf_op jit(solution)/shard_map/ppermute | solution.py:136
  118.1 7.8 %collective-permute-start.5 = (bf16[48,2048]{1,0:T(8,128)(2,1)S(1)}, bf16[48,2048]{1,0:T(8,128)(2,1)}, u32[]{:S(2)}, u32[]{:S(2)}) collective-permute-start(bf16[48,2048]{1,0:T(8,128)(2,1)S(1)} %bitcast.81), channel_id=1, source_target_pairs={{0,0},{1,4},{2,2},{3,6},{4,1},{5,3},{6,5},{7,7},{8,8},{9,12},{10,1... | collective-permute-start | bytes 589832 | tf_op jit(solution)/shard_map/ppermute | solution.py:94
  127.0 3.3 %copy-start.9 = (bf16[48,1024]{1,0:T(8,128)(2,1)}, bf16[48,1024]{1,0:T(8,128)(2,1)S(1)}, u32[]{:S(2)}) copy-start(bf16[48,1024]{1,0:T(8,128)(2,1)S(1)} %get-tuple-element.6) | copy-start | bytes 294916
  127.0 8.7 %collective-permute-start.6 = (bf16[48,3072]{1,0:T(8,128)(2,1)S(1)}, bf16[48,3072]{1,0:T(8,128)(2,1)}, u32[]{:S(2)}, u32[]{:S(2)}) collective-permute-start(bf16[48,3072]{1,0:T(8,128)(2,1)S(1)} %pad_maximum_fusion.1), channel_id=1, source_target_pairs={{0,4},{1,3},{2,6},{3,1},{4,0},{5,7},{6,2},{7,5},{8,12},{9,11},{10,... | collective-permute-start | bytes 884744 | tf_op jit(solution)/shard_map/ppermute | solution.py:153
  137.1 12.1 %collective-permute-start.7 = (bf16[96,3072]{1,0:T(8,128)(2,1)S(1)}, bf16[96,3072]{1,0:T(8,128)(2,1)}, u32[]{:S(2)}, u32[]{:S(2)}) collective-permute-start(bf16[96,3072]{1,0:T(8,128)(2,1)S(1)} %maximum_select_fusion.2), channel_id=1, source_target_pairs={{0,2},{1,5},{2,0},{3,7},{4,6},{5,1},{6,4},{7,3},{8,10},{9,13},{10,... | collective-permute-start | bytes 1769480 | tf_op jit(solution)/shard_map/ppermute | solution.py:153
  151.7 5.4 %collective-permute-start.8 = (bf16[192,3072]{1,0:T(8,128)(2,1)}, bf16[192,3072]{1,0:T(8,128)(2,1)}, u32[]{:S(2)}, u32[]{:S(2)}) collective-permute-start(bf16[192,3072]{1,0:T(8,128)(2,1)} %maximum_select_fusion), channel_id=1, source_target_pairs={{0,1},{1,0},{2,3},{3,2},{4,5},{5,4},{6,7},{7,6},{8,9},{9,8},{10,11... | collective-permute-start | bytes 3538952 | tf_op jit(solution)/shard_map/ppermute | solution.py:171
  160.7 7.8 %copy-start.10 = (f32[1,32,1]{1,2,0:T(1,128)S(1)}, f32[1,32,1]{1,2,0:T(1,128)}, u32[]{:S(2)}) copy-start(f32[1,32,1]{1,2,0:T(1,128)} %param.14) | copy-start | bytes 388
  160.7 7.8 %copy-start.11 = (f32[1,32,1]{1,2,0:T(1,128)S(1)}, f32[1,32,1]{1,2,0:T(1,128)}, u32[]{:S(2)}) copy-start(f32[1,32,1]{1,2,0:T(1,128)} %param.11) | copy-start | bytes 388
  162.4 51.0 %all-to-all-start.1 = ((bf16[64,2,6,448]{3,1,2,0:T(2,128)(2,1)}), bf16[64,2,6,448]{3,1,2,0:T(2,128)(2,1)S(1)}, u32[]{:S(2)}, u32[]{:S(2)}) async-start(bf16[64,2,6,448]{3,1,2,0:T(2,128)(2,1)} %bitcast.20), calls=%async_computation.1 | async-start | bytes 1572864 | tf_op jit(solution)/shard_map/all_to_all | solution.py:180
  214.5 2.0 copy-start.6
  214.5 2.0 copy-start.8

commit v4 on v2

--- a/solution.py
+++ b/solution.py
@@ -63,6 +63,19 @@
     else:
         bit = jnp.where(core == 0, 2, 1)
     return (member >> bit & 1).astype(jnp.int32)
+
+
+def encode_rows(values, lanes):
+    largest = jnp.maximum(jnp.max(jnp.abs(values), axis=1, keepdims=True), 1e-30)
+    exponent = jnp.floor(jnp.log2(largest)) - 13.0
+    coded = jnp.round(values * jnp.exp2(-exponent)).astype(jnp.int16)
+    tail = jnp.broadcast_to(exponent.astype(jnp.int16), (values.shape[0], lanes))
+    return jnp.concatenate([coded, tail], axis=1)
+
+
+def decode_rows(coded, width):
+    exponent = coded[:, width : width + 1].astype(jnp.float32)
+    return coded[:, :width].astype(jnp.float32) * jnp.exp2(exponent)
 
 
 def body(
@@ -132,8 +145,11 @@
         bit = own_stage_bit(index, group_size, stage)
         kept = lax.dynamic_slice_in_dim(current, bit * half, half, axis=0)
         send_part = lax.dynamic_slice_in_dim(current, (1 - bit) * half, half, axis=0)
-        received = lax.ppermute(send_part, "expert", stage_route(devices, group_size, stage))
-        current = kept + received
+        width = send_part.shape[1]
+        received = lax.ppermute(
+            encode_rows(send_part, 128), "expert", stage_route(devices, group_size, stage)
+        )
+        current = kept + decode_rows(received, width)
 
     pre_share = current[:, : 2 * hidden_units]
     hidden_grad = current[:, 2 * hidden_units :]

time: 231 us -> 222 us (0.961)
  waiting for transfers between devices: 138 us -> 128 us
    ppermute x2, waiting for transfers between devices: 25.2 us -> 15.3 us  [body(): lax.ppermute(encode_rows(send_part, 128), 'expert', stage_route(devices,...]
where the time goes in v4:
time: 222 us; the launch traced here: 221 us
  waiting for transfers between devices  128 us (58%)
  starting transfers between devices  50.8 us (23%)
  local copies, waits for them, and re-layouts  16.8 us (8%)
  other arithmetic  14.6 us (7%)
  matrix products  9.84 us (4%)
    all_to_all x1, waiting for transfers between devices, body(): lax.all_to_all(result, 'expert', split_axis=0, concat_axis=0, tiled=True)  44.9 us
    all_to_all x1, waiting for transfers between devices, body(): lax.all_to_all(sent, 'expert', split_axis=0, concat_axis=0, tiled=True)  44.8 us
    all_to_all x1, starting transfers between devices, body(): lax.all_to_all(sent, 'expert', split_axis=0, concat_axis=0, tiled=True)  17.1 us
    ppermute x2, waiting for transfers between devices, body(): lax.ppermute(encode_rows(send_part, 128), 'expert', stage_route(devices,...  15.3 us
    ppermute x2, waiting for transfers between devices, body(): lax.ppermute(current, 'expert', stage_route(devices, group_size, stage))  12.6 us
    ppermute x2, starting transfers between devices, shifted(): return lax.ppermute(block, axis, route)  9.59 us
    ppermute x2, starting transfers between devices, body(): lax.ppermute(current, 'expert', stage_route(devices, group_size, stage))  8.52 us
    ppermute x2, waiting for transfers between devices, shifted(): return lax.ppermute(block, axis, route)  6.51 us
  transfers between devices with their start and end apart: 11, of which 9 were waited for; matrix products, arithmetic and copies ran while one was open for 3% of the time, Pallas kernels for 0%

profile of v4, /device:TPU:8, one launch (start us, length us, event | category | flops | bytes accessed | tf_op | source)
XLA Modules:
  0.0 221.2 jit_solution(195950469926977966)
XLA Ops:
  0.6 4.3 %collective-permute-start = (bf16[32,3584]{1,0:T(8,128)(2,1)}, bf16[32,3584]{1,0:T(8,128)(2,1)S(1)}, u32[]{:S(2)}, u32[]{:S(2)}) collective-permute-start(bf16[32,3584]{1,0:T(8,128)(2,1)} %bitcast.79), channel_id=1, source_target_pairs={{448,0},{0,64},{64,128},{128,192},{192,256},{256,320},{320,384},{3... | collective-permute-start | bytes 688136 | tf_op jit(solution)/shard_map/ppermute | solution.py:14
  5.0 5.3 %collective-permute-start.1 = (bf16[32,3584]{1,0:T(8,128)(2,1)}, bf16[32,3584]{1,0:T(8,128)(2,1)S(1)}, u32[]{:S(2)}, u32[]{:S(2)}) collective-permute-start(bf16[32,3584]{1,0:T(8,128)(2,1)} %bitcast.80), channel_id=1, source_target_pairs={{64,0},{128,64},{192,128},{256,192},{320,256},{384,320},{448,384},... | collective-permute-start | bytes 688136 | tf_op jit(solution)/shard_map/ppermute | solution.py:14
  10.3 0.7 pad_add_fusion.2
  10.9 0.2 convert_reduce_fusion
  11.1 2.8 %collective-permute-done = bf16[32,3584]{1,0:T(8,128)(2,1)S(1)} collective-permute-done((bf16[32,3584]{1,0:T(8,128)(2,1)}, bf16[32,3584]{1,0:T(8,128)(2,1)S(1)}, u32[]{:S(2)}, u32[]{:S(2)}) %collective-permute-start) | collective-permute-done | bytes 229408 | tf_op jit(solution)/shard_map/ppermute | solution.py:14
  13.9 0.7 copy-done.4
  14.6 0.3 stack.43
  15.0 3.7 %collective-permute-done.1 = bf16[32,3584]{1,0:T(8,128)(2,1)S(1)} collective-permute-done((bf16[32,3584]{1,0:T(8,128)(2,1)}, bf16[32,3584]{1,0:T(8,128)(2,1)S(1)}, u32[]{:S(2)}, u32[]{:S(2)}) %collective-permute-start.1) | collective-permute-done | bytes 229408 | tf_op jit(solution)/shard_map/ppermute | solution.py:14
  18.8 0.3 stack.44
  19.2 0.4 fusion.8
  19.6 0.4 copy.54
  20.0 1.7 copy.39
  21.7 17.1 %all-to-all-start = ((bf16[64,2,6,448]{3,1,2,0:T(2,128)(2,1)}), bf16[64,2,6,448]{3,1,2,0:T(2,128)(2,1)S(1)}, u32[]{:S(2)}, u32[]{:S(2)}) async-start(bf16[64,2,6,448]{3,1,2,0:T(2,128)(2,1)} %copy.39), calls=%async_computation | async-start | bytes 1572864 | tf_op jit(solution)/shard_map/all_to_all | solution.py:125
  38.9 44.8 %all-to-all-done = bf16[64,2,6,448]{3,1,2,0:T(2,128)(2,1)S(1)} async-done(((bf16[64,2,6,448]{3,1,2,0:T(2,128)(2,1)}), bf16[64,2,6,448]{3,1,2,0:T(2,128)(2,1)S(1)}, u32[]{:S(2)}, u32[]{:S(2)}) %all-to-all-start) | async-done | bytes 688160 | tf_op jit(solution)/shard_map/all_to_all | solution.py:125
  83.7 4.2 %slice_reduce_fusion.1 = (bf16[64,6,448]{2,1,0:T(8,128)(2,1)}, bf16[64,6,448]{2,1,0:T(8,128)(2,1)S(1)}) fusion(bf16[64,2,6,448]{3,1,2,0:T(2,128)(2,1)S(1)} %all-to-all-done), kind=kLoop, calls=%fused_computation.35 | loop fusion | bytes 1376256 | tf_op jit(solution)/shard_map/slice | solution.py:126
  87.9 1.3 reshape_squeeze.6
  89.1 0.2 reshape_squeeze.7
  89.4 0.6 fusion.4
  90.0 0.6 copy-done.2
  90.6 0.4 fusion.25
  91.0 1.6 pad_maximum_fusion
  92.5 1.9 collective-permute-start.2
  94.5 0.4 fusion.27
  94.8 0.6 fusion.6
  95.4 3.9 %collective-permute-done.2 = f32[192,3072]{1,0:T(8,128)} collective-permute-done((f32[192,3072]{1,0:T(8,128)}, f32[192,3072]{1,0:T(8,128)}, u32[]{:S(2)}, u32[]{:S(2)}) %collective-permute-start.2) | collective-permute-done | bytes 2359328 | tf_op jit(solution)/shard_map/ppermute | solution.py:141
  99.3 1.9 maximum_add_fusion
  101.2 0.2 abs_reduce_fusion
  101.4 0.3 round-nearest-even_convert_fusion
  101.8 0.8 copy-done.1
  102.6 2.4 %collective-permute-start.3 = (s16[96,3200]{1,0:T(8,128)(2,1)S(1)}, s16[96,3200]{1,0:T(8,128)(2,1)S(1)}, u32[]{:S(2)}, u32[]{:S(2)}) collective-permute-start(s16[96,3200]{1,0:T(8,128)(2,1)S(1)} %pad_add_fusion), channel_id=1, source_target_pairs={{0,2},{1,5},{2,0},{3,7},{4,6},{5,1},{6,4},{7,3},{8,10},{9,13},{10,... | collective-permute-start | bytes 1843208 | tf_op jit(solution)/shard_map/ppermute | solution.py:149
  105.1 9.6 %collective-permute-done.3 = s16[96,3200]{1,0:T(8,128)(2,1)S(1)} collective-permute-done((s16[96,3200]{1,0:T(8,128)(2,1)S(1)}, s16[96,3200]{1,0:T(8,128)(2,1)S(1)}, u32[]{:S(2)}, u32[]{:S(2)}) %collective-permute-start.3) | collective-permute-done | bytes 614432 | tf_op jit(solution)/shard_map/ppermute | solution.py:149
  114.6 0.8 copy-done.9
  115.5 0.1 exponential_reduce_fusion
  115.6 1.7 multiply_add_fusion
  117.3 0.1 abs_reduce_fusion.1
  117.5 0.2 round-nearest-even_convert_fusion.1
  117.7 0.7 pad_add_fusion.1
  118.5 1.9 collective-permute-start.4
  120.4 1.3 collective-permute-start.5
  121.7 5.7 %collective-permute-done.4 = s16[48,3200]{1,0:T(8,128)(2,1)S(1)} collective-permute-done((s16[48,3200]{1,0:T(8,128)(2,1)}, s16[48,3200]{1,0:T(8,128)(2,1)S(1)}, u32[]{:S(2)}, u32[]{:S(2)}) %collective-permute-start.4) | collective-permute-done | bytes 307232 | tf_op jit(solution)/shard_map/ppermute | solution.py:149
  127.4 0.1 exponential_reduce_fusion.1
  127.5 0.1 multiply_add_fusion.1
  127.7 1.1 fusion.41
  128.8 0.6 copy-done.8
  129.4 3.9 %collective-permute-start.6 = (bf16[48,3072]{1,0:T(8,128)(2,1)S(1)}, bf16[48,3072]{1,0:T(8,128)(2,1)}, u32[]{:S(2)}, u32[]{:S(2)}) collective-permute-start(bf16[48,3072]{1,0:T(8,128)(2,1)S(1)} %pad_maximum_fusion.1), channel_id=1, source_target_pairs={{0,4},{1,3},{2,6},{3,1},{4,0},{5,7},{6,2},{7,5},{8,12},{9,11},{10,... | collective-permute-start | bytes 884744 | tf_op jit(solution)/shard_map/ppermute | solution.py:168
  133.3 4.8 %collective-permute-done.6 = bf16[48,3072]{1,0:T(8,128)(2,1)} collective-permute-done((bf16[48,3072]{1,0:T(8,128)(2,1)S(1)}, bf16[48,3072]{1,0:T(8,128)(2,1)}, u32[]{:S(2)}, u32[]{:S(2)}) %collective-permute-start.6) | collective-permute-done | bytes 294944 | tf_op jit(solution)/shard_map/ppermute | solution.py:168
  138.2 1.3 maximum_select_fusion.2
  139.5 4.7 %collective-permute-start.7 = (bf16[96,3072]{1,0:T(8,128)(2,1)S(1)}, bf16[96,3072]{1,0:T(8,128)(2,1)}, u32[]{:S(2)}, u32[]{:S(2)}) collective-permute-start(bf16[96,3072]{1,0:T(8,128)(2,1)S(1)} %maximum_select_fusion.2), channel_id=1, source_target_pairs={{0,2},{1,5},{2,0},{3,7},{4,6},{5,1},{6,4},{7,3},{8,10},{9,13},{10,... | collective-permute-start | bytes 1769480 | tf_op jit(solution)/shard_map/ppermute | solution.py:168
  144.1 7.8 %collective-permute-done.7 = bf16[96,3072]{1,0:T(8,128)(2,1)} collective-permute-done((bf16[96,3072]{1,0:T(8,128)(2,1)S(1)}, bf16[96,3072]{1,0:T(8,128)(2,1)}, u32[]{:S(2)}, u32[]{:S(2)}) %collective-permute-start.7) | collective-permute-done | bytes 589856 | tf_op jit(solution)/shard_map/ppermute | solution.py:168
  151.9 2.6 %maximum_select_fusion = bf16[192,3072]{1,0:T(8,128)(2,1)} fusion(bf16[96,3072]{1,0:T(8,128)(2,1)S(1)} %maximum_select_fusion.2, bf16[96,3072]{1,0:T(8,128)(2,1)} %collective-permute-done.7, pred[]{:T(512)S(6)} %eq.63), kind=kLoop, calls=%fused_computation.13 | loop fusion | flops 5308416 | bytes 2359297 | tf_op jit(solution)/shard_map/jit(_where)/select_n | solution.py:169
  154.5 2.0 collective-permute-start.8
  156.5 1.4 fusion.22
  158.0 1.8 fusion.15
  159.8 1.8 fusion.18
  161.6 1.4 fusion.21
  163.0 0.3 maximum_select_fusion.1
  163.4 1.7 copy.40
  165.0 6.0 %all-to-all-start.1 = ((bf16[64,2,6,448]{3,1,2,0:T(2,128)(2,1)}), bf16[64,2,6,448]{3,1,2,0:T(2,128)(2,1)S(1)}, u32[]{:S(2)}, u32[]{:S(2)}) async-start(bf16[64,2,6,448]{3,1,2,0:T(2,128)(2,1)} %bitcast.20), calls=%async_computation.1 | async-start | bytes 1572864 | tf_op jit(solution)/shard_map/all_to_all | solution.py:195
  171.1 44.9 %all-to-all-done.1 = bf16[64,2,6,448]{3,1,2,0:T(2,128)(2,1)S(1)} async-done(((bf16[64,2,6,448]{3,1,2,0:T(2,128)(2,1)}), bf16[64,2,6,448]{3,1,2,0:T(2,128)(2,1)S(1)}, u32[]{:S(2)}, u32[]{:S(2)}) %all-to-all-start.1) | async-done | bytes 688160 | tf_op jit(solution)/shard_map/all_to_all | solution.py:195
  216.0 1.1 convolution_bitcast_fusion
  217.1 0.6 copy.43
  217.7 1.3 reshape.115
  219.0 1.4 add_convert_fusion
  220.4 0.8 fusion.64
  (35 shorter events, 0.5 us)
Async XLA Ops:
  0.6 88.8 %copy-start = (bf16[1,1,448,2048]{3,2,1,0:T(8,128)(2,1)S(1)}, bf16[1,1,448,2048]{3,2,1,0:T(8,128)(2,1)}, u32[]{:S(2)}) copy-start(bf16[1,1,448,2048]{3,2,1,0:T(8,128)(2,1)} %param.15) | copy-start | bytes 5505028
  0.6 13.3 %collective-permute-start = (bf16[32,3584]{1,0:T(8,128)(2,1)}, bf16[32,3584]{1,0:T(8,128)(2,1)S(1)}, u32[]{:S(2)}, u32[]{:S(2)}) collective-permute-start(bf16[32,3584]{1,0:T(8,128)(2,1)} %bitcast.79), channel_id=1, source_target_pairs={{448,0},{0,64},{64,128},{128,192},{192,256},{256,320},{320,384},{3... | collective-permute-start | bytes 688136 | tf_op jit(solution)/shard_map/ppermute | solution.py:14
  5.0 13.8 %collective-permute-start.1 = (bf16[32,3584]{1,0:T(8,128)(2,1)}, bf16[32,3584]{1,0:T(8,128)(2,1)S(1)}, u32[]{:S(2)}, u32[]{:S(2)}) collective-permute-start(bf16[32,3584]{1,0:T(8,128)(2,1)} %bitcast.80), channel_id=1, source_target_pairs={{64,0},{128,64},{192,128},{256,192},{320,256},{384,320},{448,384},... | collective-permute-start | bytes 688136 | tf_op jit(solution)/shard_map/ppermute | solution.py:14
  13.9 0.7 copy-start.4
  18.8 1.3 copy-start.6
  21.7 61.9 %all-to-all-start = ((bf16[64,2,6,448]{3,1,2,0:T(2,128)(2,1)}), bf16[64,2,6,448]{3,1,2,0:T(2,128)(2,1)S(1)}, u32[]{:S(2)}, u32[]{:S(2)}) async-start(bf16[64,2,6,448]{3,1,2,0:T(2,128)(2,1)} %copy.39), calls=%async_computation | async-start | bytes 1572864 | tf_op jit(solution)/shard_map/all_to_all | solution.py:125
  89.4 1.2 copy-start.2
  92.5 6.8 %collective-permute-start.2 = (f32[192,3072]{1,0:T(8,128)}, f32[192,3072]{1,0:T(8,128)}, u32[]{:S(2)}, u32[]{:S(2)}) collective-permute-start(f32[192,3072]{1,0:T(8,128)} %pad_maximum_fusion), channel_id=1, source_target_pairs={{0,1},{1,0},{2,3},{3,2},{4,5},{5,4},{6,7},{7,6},{8,9},{9,8},{10,11... | collective-permute-start | bytes 7077896 | tf_op jit(solution)/shard_map/ppermute | solution.py:141
  101.2 1.4 copy-start.1
  102.6 12.0 %collective-permute-start.3 = (s16[96,3200]{1,0:T(8,128)(2,1)S(1)}, s16[96,3200]{1,0:T(8,128)(2,1)S(1)}, u32[]{:S(2)}, u32[]{:S(2)}) collective-permute-start(s16[96,3200]{1,0:T(8,128)(2,1)S(1)} %pad_add_fusion), channel_id=1, source_target_pairs={{0,2},{1,5},{2,0},{3,7},{4,6},{5,1},{6,4},{7,3},{8,10},{9,13},{10,... | collective-permute-start | bytes 1843208 | tf_op jit(solution)/shard_map/ppermute | solution.py:149
  114.6 0.8 copy-start.9
  117.3 3.1 %copy-start.12 = (bf16[1,1,48,2048]{3,2,1,0:T(8,128)(2,1)S(1)}, bf16[1,1,48,2048]{3,2,1,0:T(8,128)(2,1)}, u32[]{:S(2)}) copy-start(bf16[1,1,48,2048]{3,2,1,0:T(8,128)(2,1)} %param.17) | copy-start | bytes 589828
  118.5 8.9 %collective-permute-start.4 = (s16[48,3200]{1,0:T(8,128)(2,1)}, s16[48,3200]{1,0:T(8,128)(2,1)S(1)}, u32[]{:S(2)}, u32[]{:S(2)}) collective-permute-start(s16[48,3200]{1,0:T(8,128)(2,1)} %pad_add_fusion.1), channel_id=1, source_target_pairs={{0,4},{1,3},{2,6},{3,1},{4,0},{5,7},{6,2},{7,5},{8,12},{9,11},{10,... | collective-permute-start | bytes 921608 | tf_op jit(solution)/shard_map/ppermute | solution.py:149
  120.4 7.3 %collective-permute-start.5 = (bf16[48,2048]{1,0:T(8,128)(2,1)S(1)}, bf16[48,2048]{1,0:T(8,128)(2,1)}, u32[]{:S(2)}, u32[]{:S(2)}) collective-permute-start(bf16[48,2048]{1,0:T(8,128)(2,1)S(1)} %bitcast.81), channel_id=1, source_target_pairs={{0,0},{1,4},{2,2},{3,6},{4,1},{5,3},{6,5},{7,7},{8,8},{9,12},{10,1... | collective-permute-start | bytes 589832 | tf_op jit(solution)/shard_map/ppermute | solution.py:107
  128.8 0.6 copy-start.8
  129.4 8.7 %collective-permute-start.6 = (bf16[48,3072]{1,0:T(8,128)(2,1)S(1)}, bf16[48,3072]{1,0:T(8,128)(2,1)}, u32[]{:S(2)}, u32[]{:S(2)}) collective-permute-start(bf16[48,3072]{1,0:T(8,128)(2,1)S(1)} %pad_maximum_fusion.1), channel_id=1, source_target_pairs={{0,4},{1,3},{2,6},{3,1},{4,0},{5,7},{6,2},{7,5},{8,12},{9,11},{10,... | collective-permute-start | bytes 884744 | tf_op jit(solution)/shard_map/ppermute | solution.py:168
  133.3 23.2 %copy-start.3 = (bf16[1,1,1024,448]{2,3,1,0:T(8,128)(2,1)S(1)}, bf16[1,1,1024,448]{2,3,1,0:T(8,128)(2,1)}, u32[]{:S(2)}) copy-start(bf16[1,1,1024,448]{2,3,1,0:T(8,128)(2,1)} %param.16) | copy-start | bytes 2752516
  139.5 12.4 %collective-permute-start.7 = (bf16[96,3072]{1,0:T(8,128)(2,1)S(1)}, bf16[96,3072]{1,0:T(8,128)(2,1)}, u32[]{:S(2)}, u32[]{:S(2)}) collective-permute-start(bf16[96,3072]{1,0:T(8,128)(2,1)S(1)} %maximum_select_fusion.2), channel_id=1, source_target_pairs={{0,2},{1,5},{2,0},{3,7},{4,6},{5,1},{6,4},{7,3},{8,10},{9,13},{10,... | collective-permute-start | bytes 1769480 | tf_op jit(solution)/shard_map/ppermute | solution.py:168
  154.5 5.3 %collective-permute-start.8 = (bf16[192,3072]{1,0:T(8,128)(2,1)}, bf16[192,3072]{1,0:T(8,128)(2,1)}, u32[]{:S(2)}, u32[]{:S(2)}) collective-permute-start(bf16[192,3072]{1,0:T(8,128)(2,1)} %maximum_select_fusion), channel_id=1, source_target_pairs={{0,1},{1,0},{2,3},{3,2},{4,5},{5,4},{6,7},{7,6},{8,9},{9,8},{10,11... | collective-permute-start | bytes 3538952 | tf_op jit(solution)/shard_map/ppermute | solution.py:186
  163.3 7.7 %copy-start.10 = (f32[1,32,1]{1,2,0:T(1,128)S(1)}, f32[1,32,1]{1,2,0:T(1,128)}, u32[]{:S(2)}) copy-start(f32[1,32,1]{1,2,0:T(1,128)} %param.14) | copy-start | bytes 388
  163.3 7.7 %copy-start.11 = (f32[1,32,1]{1,2,0:T(1,128)S(1)}, f32[1,32,1]{1,2,0:T(1,128)}, u32[]{:S(2)}) copy-start(f32[1,32,1]{1,2,0:T(1,128)} %param.11) | copy-start | bytes 388
  165.0 51.0 %all-to-all-start.1 = ((bf16[64,2,6,448]{3,1,2,0:T(2,128)(2,1)}), bf16[64,2,6,448]{3,1,2,0:T(2,128)(2,1)S(1)}, u32[]{:S(2)}, u32[]{:S(2)}) async-start(bf16[64,2,6,448]{3,1,2,0:T(2,128)(2,1)} %bitcast.20), calls=%async_computation.1 | async-start | bytes 1572864 | tf_op jit(solution)/shard_map/all_to_all | solution.py:195
  217.1 2.0 copy-start.5
  217.1 2.0 copy-start.7

commit v5 on v4

--- a/solution.py
+++ b/solution.py
@@ -163,34 +163,27 @@
     up_grad = hidden_grad * gate_pre * sigmoid_gate
     current = jnp.concatenate([hidden_share, gate_grad.astype(jnp.bfloat16), up_grad.astype(jnp.bfloat16)], axis=1)
 
+    for stage in reversed(range(levels)):
+        partner = lax.ppermute(current, "expert", stage_route(devices, group_size, stage))
+        current = jnp.concatenate([current, partner], axis=0)
+    out_down = jnp.dot(
+        current[:, :hidden_units], proj_out, preferred_element_type=jnp.float32
+    ).astype(jnp.bfloat16)
+    out_up = lax.dot_general(
+        current[:, hidden_units:], proj_in, (((1,), (1,)), ((), ())),
+        preferred_element_type=jnp.float32,
+    ).astype(jnp.bfloat16)
+    result = jnp.stack([out_down, out_up])
+    view = result.reshape((2,) + (2,) * levels + (-1, share_width))
+    neighbour = index ^ 1
     for stage in reversed(range(1, levels)):
-        bit = own_stage_bit(index, group_size, stage)
-        partner = lax.ppermute(current, "expert", stage_route(devices, group_size, stage))
-        current = jnp.where(
-            bit == 1,
-            jnp.concatenate([partner, current], axis=0),
-            jnp.concatenate([current, partner], axis=0),
-        )
-
-    def last_matmul(block):
-        out_down = jnp.dot(
-            block[:, :hidden_units], proj_out, preferred_element_type=jnp.float32
-        ).astype(jnp.bfloat16)
-        out_up = lax.dot_general(
-            block[:, hidden_units:], proj_in, (((1,), (1,)), ((), ())),
-            preferred_element_type=jnp.float32,
-        ).astype(jnp.bfloat16)
-        return jnp.stack([out_down, out_up])
-
-    bit = own_stage_bit(index, group_size, 0)
-    partner = lax.ppermute(current, "expert", stage_route(devices, group_size, 0))
-    own_out = last_matmul(current)
-    partner_out = last_matmul(partner)
-    result = jnp.where(
-        bit == 1,
-        jnp.concatenate([partner_out, own_out], axis=1),
-        jnp.concatenate([own_out, partner_out], axis=1),
-    )
+        flags = jnp.stack(
+            [own_stage_bit(index, group_size, stage), own_stage_bit(neighbour, group_size, stage)]
+        ).reshape((1, 2) + (1,) * (levels + 1))
+        view = jnp.where(flags == 1, jnp.flip(view, axis=1 + stage), view)
+    top = own_stage_bit(index, group_size, 0)
+    view = jnp.where(top == 1, jnp.flip(view, axis=1), view)
+    result = view.reshape(2, -1, share_width)
     result = result.reshape(2, devices, MOST, share_width).transpose(1, 0, 2, 3)
     back = lax.all_to_all(result, "expert", split_axis=0, concat_axis=0, tiled=True)
     back = back.reshape(EXPERTS, group_size, 2, MOST, share_width)

time: 222 us -> 223 us (level)
  waiting for transfers between devices: 128 us -> 131 us
  other arithmetic: 14.6 us -> 11.7 us
  local copies, waits for them, and re-layouts: 16.8 us -> 19.3 us
    select_n x3, other arithmetic: 4.17 us -> 0.86 us  [the longest x2 0.71 us: body(): view = jnp.where(flags == 1, jnp.flip(view, axis=1 + stage), view)]
    ppermute x2 -> x3, waiting for transfers between devices: 12.6 us -> 15.4 us  [body(): lax.ppermute(current, 'expert', stage_route(devices, group_size, stage))]
    convert_element_type x0 -> x2, local copies, waits for them, and re-layouts: none -> 2.29 us  [the longest x1 1.15 us: body(): out_down = jnp.dot(current[:, :hidden_units], proj_out, preferred_element...]
    ppermute x2 -> x3, starting transfers between devices: 8.52 us -> 10.4 us  [body(): lax.ppermute(current, 'expert', stage_route(devices, group_size, stage))]
    dot_general x4 -> x2, matrix products: 6.49 us -> 5.57 us  [the longest x1 3.12 us: body(): lax.dot_general(current[:, hidden_units:], proj_in, (((1,), (1,)), ((), (...]
  transfers between devices with their start and end apart: 11 -> 11, of which waited for: 9 -> 10; matrix products, arithmetic and copies ran while one was open for 3% -> 1% of each run, Pallas kernels for 0% -> 0%
where the time goes in v5:
time: 223 us
  waiting for transfers between devices  131 us (59%)
  starting transfers between devices  51 us (23%)
  local copies, waits for them, and re-layouts  19.3 us (9%)
  other arithmetic  11.7 us (5%)
  matrix products  8.92 us (4%)
    all_to_all x1, waiting for transfers between devices, body(): lax.all_to_all(result, 'expert', split_axis=0, concat_axis=0, tiled=True)  44.9 us
    all_to_all x1, waiting for transfers between devices, body(): lax.all_to_all(sent, 'expert', split_axis=0, concat_axis=0, tiled=True)  44.8 us
    all_to_all x1, starting transfers between devices, body(): lax.all_to_all(sent, 'expert', split_axis=0, concat_axis=0, tiled=True)  17.1 us
    ppermute x3, waiting for transfers between devices, body(): lax.ppermute(current, 'expert', stage_route(devices, group_size, stage))  15.4 us
    ppermute x2, waiting for transfers between devices, body(): lax.ppermute(encode_rows(send_part, 128), 'expert', stage_route(devices,...  15 us
    ppermute x3, starting transfers between devices, body(): lax.ppermute(current, 'expert', stage_route(devices, group_size, stage))  10.4 us
    ppermute x2, starting transfers between devices, shifted(): return lax.ppermute(block, axis, route)  9.59 us
    ppermute x2, waiting for transfers between devices, shifted(): return lax.ppermute(block, axis, route)  6.51 us
  transfers between devices with their start and end apart: 11, of which 10 were waited for; matrix products, arithmetic and copies ran while one was open for 1% of the time, Pallas kernels for 0%

profile of v5, /device:TPU:8, one launch (start us, length us, event | category | flops | bytes accessed | tf_op | source)
XLA Modules:
  0.0 222.6 jit_solution(10199437911518051012)
XLA Ops:
  0.6 4.3 %collective-permute-start = (bf16[32,3584]{1,0:T(8,128)(2,1)}, bf16[32,3584]{1,0:T(8,128)(2,1)S(1)}, u32[]{:S(2)}, u32[]{:S(2)}) collective-permute-start(bf16[32,3584]{1,0:T(8,128)(2,1)} %bitcast.69), channel_id=1, source_target_pairs={{448,0},{0,64},{64,128},{128,192},{192,256},{256,320},{320,384},{3... | collective-permute-start | bytes 688136 | tf_op jit(solution)/shard_map/ppermute | solution.py:14
  5.0 5.3 %collective-permute-start.1 = (bf16[32,3584]{1,0:T(8,128)(2,1)}, bf16[32,3584]{1,0:T(8,128)(2,1)S(1)}, u32[]{:S(2)}, u32[]{:S(2)}) collective-permute-start(bf16[32,3584]{1,0:T(8,128)(2,1)} %bitcast.70), channel_id=1, source_target_pairs={{64,0},{128,64},{192,128},{256,192},{320,256},{384,320},{448,384},... | collective-permute-start | bytes 688136 | tf_op jit(solution)/shard_map/ppermute | solution.py:14
  10.3 0.7 pad_add_fusion.2
  10.9 0.2 convert_reduce_fusion
  11.1 2.8 %collective-permute-done = bf16[32,3584]{1,0:T(8,128)(2,1)S(1)} collective-permute-done((bf16[32,3584]{1,0:T(8,128)(2,1)}, bf16[32,3584]{1,0:T(8,128)(2,1)S(1)}, u32[]{:S(2)}, u32[]{:S(2)}) %collective-permute-start) | collective-permute-done | bytes 229408 | tf_op jit(solution)/shard_map/ppermute | solution.py:14
  13.9 0.7 copy-done.4
  14.6 0.3 stack.58
  15.0 3.7 %collective-permute-done.1 = bf16[32,3584]{1,0:T(8,128)(2,1)S(1)} collective-permute-done((bf16[32,3584]{1,0:T(8,128)(2,1)}, bf16[32,3584]{1,0:T(8,128)(2,1)S(1)}, u32[]{:S(2)}, u32[]{:S(2)}) %collective-permute-start.1) | collective-permute-done | bytes 229408 | tf_op jit(solution)/shard_map/ppermute | solution.py:14
  18.8 0.3 stack.59
  19.2 0.4 fusion.7
  19.6 0.4 copy.62
  20.0 1.7 copy.45
  21.7 17.1 %all-to-all-start = ((bf16[64,2,6,448]{3,1,2,0:T(2,128)(2,1)}), bf16[64,2,6,448]{3,1,2,0:T(2,128)(2,1)S(1)}, u32[]{:S(2)}, u32[]{:S(2)}) async-start(bf16[64,2,6,448]{3,1,2,0:T(2,128)(2,1)} %copy.45), calls=%async_computation | async-start | bytes 1572864 | tf_op jit(solution)/shard_map/all_to_all | solution.py:125
  38.9 44.8 %all-to-all-done = bf16[64,2,6,448]{3,1,2,0:T(2,128)(2,1)S(1)} async-done(((bf16[64,2,6,448]{3,1,2,0:T(2,128)(2,1)}), bf16[64,2,6,448]{3,1,2,0:T(2,128)(2,1)S(1)}, u32[]{:S(2)}, u32[]{:S(2)}) %all-to-all-start) | async-done | bytes 688160 | tf_op jit(solution)/shard_map/all_to_all | solution.py:125
  83.7 4.2 %slice_reduce_fusion.1 = (bf16[64,6,448]{2,1,0:T(8,128)(2,1)}, bf16[64,6,448]{2,1,0:T(8,128)(2,1)S(1)}) fusion(bf16[64,2,6,448]{3,1,2,0:T(2,128)(2,1)S(1)} %all-to-all-done), kind=kLoop, calls=%fused_computation.44 | loop fusion | bytes 1376256 | tf_op jit(solution)/shard_map/slice | solution.py:126
  87.9 1.3 reshape_squeeze.6
  89.1 0.2 reshape_squeeze.7
  89.4 0.6 fusion.2
  90.0 0.6 copy-done.2
  90.6 0.4 fusion.12
  91.0 1.6 pad_maximum_fusion
  92.5 1.9 collective-permute-start.2
  94.5 0.4 fusion.14
  94.8 0.6 fusion.4
  95.4 3.9 %collective-permute-done.2 = f32[192,3072]{1,0:T(8,128)} collective-permute-done((f32[192,3072]{1,0:T(8,128)}, f32[192,3072]{1,0:T(8,128)}, u32[]{:S(2)}, u32[]{:S(2)}) %collective-permute-start.2) | collective-permute-done | bytes 2359328 | tf_op jit(solution)/shard_map/ppermute | solution.py:141
  99.3 1.9 maximum_add_fusion
  101.2 0.2 abs_reduce_fusion
  101.4 0.3 round-nearest-even_convert_fusion
  101.8 0.8 copy-done.1
  102.6 2.4 %collective-permute-start.3 = (s16[96,3200]{1,0:T(8,128)(2,1)S(1)}, s16[96,3200]{1,0:T(8,128)(2,1)S(1)}, u32[]{:S(2)}, u32[]{:S(2)}) collective-permute-start(s16[96,3200]{1,0:T(8,128)(2,1)S(1)} %pad_add_fusion), channel_id=1, source_target_pairs={{0,2},{1,5},{2,0},{3,7},{4,6},{5,1},{6,4},{7,3},{8,10},{9,13},{10,... | collective-permute-start | bytes 1843208 | tf_op jit(solution)/shard_map/ppermute | solution.py:149
  105.1 9.6 %collective-permute-done.3 = s16[96,3200]{1,0:T(8,128)(2,1)S(1)} collective-permute-done((s16[96,3200]{1,0:T(8,128)(2,1)S(1)}, s16[96,3200]{1,0:T(8,128)(2,1)S(1)}, u32[]{:S(2)}, u32[]{:S(2)}) %collective-permute-start.3) | collective-permute-done | bytes 614432 | tf_op jit(solution)/shard_map/ppermute | solution.py:149
  114.6 0.8 copy-done.8
  115.6 1.7 multiply_add_fusion
  117.3 0.1 abs_reduce_fusion.1
  117.5 0.2 round-nearest-even_convert_fusion.1
  117.7 0.7 pad_add_fusion.1
  118.4 1.9 collective-permute-start.4
  120.4 1.6 collective-permute-start.5
  121.9 5.4 %collective-permute-done.4 = s16[48,3200]{1,0:T(8,128)(2,1)S(1)} collective-permute-done((s16[48,3200]{1,0:T(8,128)(2,1)}, s16[48,3200]{1,0:T(8,128)(2,1)S(1)}, u32[]{:S(2)}, u32[]{:S(2)}) %collective-permute-start.4) | collective-permute-done | bytes 307232 | tf_op jit(solution)/shard_map/ppermute | solution.py:149
  127.5 0.1 multiply_add_fusion.1
  127.7 0.2 fusion.35
  127.9 3.9 %collective-permute-start.6 = (bf16[48,3072]{1,0:T(8,128)(2,1)S(1)}, bf16[48,3072]{1,0:T(8,128)(2,1)S(1)}, u32[]{:S(2)}, u32[]{:S(2)}) collective-permute-start(bf16[48,3072]{1,0:T(8,128)(2,1)S(1)} %pad_maximum_fusion.16), channel_id=1, source_target_pairs={{0,4},{1,3},{2,6},{3,1},{4,0},{5,7},{6,2},{7,5},{8,12},{9,11},{10,... | collective-permute-start | bytes 884744 | tf_op jit(solution)/shard_map/ppermute | solution.py:167
  131.8 4.8 %collective-permute-done.6 = bf16[48,3072]{1,0:T(8,128)(2,1)S(1)} collective-permute-done((bf16[48,3072]{1,0:T(8,128)(2,1)S(1)}, bf16[48,3072]{1,0:T(8,128)(2,1)S(1)}, u32[]{:S(2)}, u32[]{:S(2)}) %collective-permute-start.6) | collective-permute-done | bytes 294944 | tf_op jit(solution)/shard_map/ppermute | solution.py:167
  136.7 4.3 %collective-permute-start.7 = (bf16[96,3072]{1,0:T(8,128)(2,1)S(1)}, bf16[96,3072]{1,0:T(8,128)(2,1)S(1)}, u32[]{:S(2)}, u32[]{:S(2)}) collective-permute-start(bf16[96,3072]{1,0:T(8,128)(2,1)S(1)} %pad_maximum_fusion.15), channel_id=1, source_target_pairs={{0,2},{1,5},{2,0},{3,7},{4,6},{5,1},{6,4},{7,3},{8,10},{9,13},{10,... | collective-permute-start | bytes 1769480 | tf_op jit(solution)/shard_map/ppermute | solution.py:167
  140.9 7.8 %collective-permute-done.7 = bf16[96,3072]{1,0:T(8,128)(2,1)S(1)} collective-permute-done((bf16[96,3072]{1,0:T(8,128)(2,1)S(1)}, bf16[96,3072]{1,0:T(8,128)(2,1)S(1)}, u32[]{:S(2)}, u32[]{:S(2)}) %collective-permute-start.7) | collective-permute-done | bytes 589856 | tf_op jit(solution)/shard_map/ppermute | solution.py:167
  148.8 0.8 copy-done.9
  149.6 1.1 pad_maximum_fusion.13
  150.7 2.2 collective-permute-start.8
  153.0 2.8 %collective-permute-done.8 = bf16[192,3072]{1,0:T(8,128)(2,1)} collective-permute-done((bf16[192,3072]{1,0:T(8,128)(2,1)}, bf16[192,3072]{1,0:T(8,128)(2,1)}, u32[]{:S(2)}, u32[]{:S(2)}) %collective-permute-start.8) | collective-permute-done | bytes 1179680 | tf_op jit(solution)/shard_map/ppermute | solution.py:167
  155.8 2.5 %convolution_convert_fusion.1 = bf16[384,448]{0,1:T(8,128)(2,1)} fusion(bf16[1,1,1024,448]{2,3,1,0:T(8,128)(2,1)S(1)} %copy-done.3, bf16[192,3072]{1,0:T(8,128)(2,1)} %collective-permute-done.8, bf16[96,3072]{1,0:T(8,128)(2,1)} %copy-done.9, bf16[48,3072]{1,0:T(8,128)(2,1)S(1)} %collective-permute-done.6, bf16[48,1024]{1,0:T(8,128)(2,1)S(1)} %get-tuple-element.5, ...), kind=kOutput, calls=%fused_computation.17 | convolution fusion | flops 357212160 | bytes 3620864 | tf_op jit(solution)/shard_map/dot_general | solution.py:169
  158.3 1.1 copy.46
  159.4 3.1 %fusion.8 = bf16[384,448]{0,1:T(8,128)(2,1)} fusion(bf16[1,1,448,2048]{3,2,1,0:T(8,128)(2,1)S(1)} %copy-done, bf16[192,3072]{1,0:T(8,128)(2,1)} %collective-permute-done.8, bf16[96,3072]{1,0:T(8,128)(2,1)} %copy-done.9, bf16[48,3072]{1,0:T(8,128)(2,1)S(1)} %collective-permute-done.6, bf16[48,1024]{1,0:T(8,128)(2,1)S(1)} %get-tuple-element.5, ...), kind=kOutput, calls=%fused_computation.18 | convolution fusion | flops 714252288 | bytes 4538368 | tf_op jit(solution)/shard_map/dot_general | solution.py:172
  162.5 1.1 copy.47
  163.8 0.4 reverse_select_fusion.2
  164.1 0.4 reverse_select_fusion.1
  164.5 0.2 reverse_select_fusion
  164.7 1.7 copy.48
  166.4 6.1 %all-to-all-start.1 = ((bf16[64,2,6,448]{3,1,2,0:T(2,128)(2,1)}), bf16[64,2,6,448]{3,1,2,0:T(2,128)(2,1)S(1)}, u32[]{:S(2)}, u32[]{:S(2)}) async-start(bf16[64,2,6,448]{3,1,2,0:T(2,128)(2,1)} %bitcast.22), calls=%async_computation.1 | async-start | bytes 1572864 | tf_op jit(solution)/shard_map/all_to_all | solution.py:188
  172.5 44.9 %all-to-all-done.1 = bf16[64,2,6,448]{3,1,2,0:T(2,128)(2,1)S(1)} async-done(((bf16[64,2,6,448]{3,1,2,0:T(2,128)(2,1)}), bf16[64,2,6,448]{3,1,2,0:T(2,128)(2,1)S(1)}, u32[]{:S(2)}, u32[]{:S(2)}) %all-to-all-start.1) | async-done | bytes 688160 | tf_op jit(solution)/shard_map/all_to_all | solution.py:188
  217.4 1.1 convolution_bitcast_fusion
  218.5 0.6 copy.51
  219.1 1.3 reshape.153
  220.5 1.4 add_convert_fusion
  221.8 0.8 fusion.60
  (37 shorter events, 0.9 us)
Async XLA Ops:
  0.6 88.8 %copy-start = (bf16[1,1,448,2048]{3,2,1,0:T(8,128)(2,1)S(1)}, bf16[1,1,448,2048]{3,2,1,0:T(8,128)(2,1)}, u32[]{:S(2)}) copy-start(bf16[1,1,448,2048]{3,2,1,0:T(8,128)(2,1)} %param.15) | copy-start | bytes 5505028
  0.6 13.3 %collective-permute-start = (bf16[32,3584]{1,0:T(8,128)(2,1)}, bf16[32,3584]{1,0:T(8,128)(2,1)S(1)}, u32[]{:S(2)}, u32[]{:S(2)}) collective-permute-start(bf16[32,3584]{1,0:T(8,128)(2,1)} %bitcast.69), channel_id=1, source_target_pairs={{448,0},{0,64},{64,128},{128,192},{192,256},{256,320},{320,384},{3... | collective-permute-start | bytes 688136 | tf_op jit(solution)/shard_map/ppermute | solution.py:14
  5.0 13.8 %collective-permute-start.1 = (bf16[32,3584]{1,0:T(8,128)(2,1)}, bf16[32,3584]{1,0:T(8,128)(2,1)S(1)}, u32[]{:S(2)}, u32[]{:S(2)}) collective-permute-start(bf16[32,3584]{1,0:T(8,128)(2,1)} %bitcast.70), channel_id=1, source_target_pairs={{64,0},{128,64},{192,128},{256,192},{320,256},{384,320},{448,384},... | collective-permute-start | bytes 688136 | tf_op jit(solution)/shard_map/ppermute | solution.py:14
  13.9 0.7 copy-start.4
  18.8 1.3 copy-start.6
  21.7 61.9 %all-to-all-start = ((bf16[64,2,6,448]{3,1,2,0:T(2,128)(2,1)}), bf16[64,2,6,448]{3,1,2,0:T(2,128)(2,1)S(1)}, u32[]{:S(2)}, u32[]{:S(2)}) async-start(bf16[64,2,6,448]{3,1,2,0:T(2,128)(2,1)} %copy.45), calls=%async_computation | async-start | bytes 1572864 | tf_op jit(solution)/shard_map/all_to_all | solution.py:125
  89.4 1.2 copy-start.2
  92.5 6.8 %collective-permute-start.2 = (f32[192,3072]{1,0:T(8,128)}, f32[192,3072]{1,0:T(8,128)}, u32[]{:S(2)}, u32[]{:S(2)}) collective-permute-start(f32[192,3072]{1,0:T(8,128)} %pad_maximum_fusion), channel_id=1, source_target_pairs={{0,1},{1,0},{2,3},{3,2},{4,5},{5,4},{6,7},{7,6},{8,9},{9,8},{10,11... | collective-permute-start | bytes 7077896 | tf_op jit(solution)/shard_map/ppermute | solution.py:141
  101.2 1.4 copy-start.1
  102.6 12.0 %collective-permute-start.3 = (s16[96,3200]{1,0:T(8,128)(2,1)S(1)}, s16[96,3200]{1,0:T(8,128)(2,1)S(1)}, u32[]{:S(2)}, u32[]{:S(2)}) collective-permute-start(s16[96,3200]{1,0:T(8,128)(2,1)S(1)} %pad_add_fusion), channel_id=1, source_target_pairs={{0,2},{1,5},{2,0},{3,7},{4,6},{5,1},{6,4},{7,3},{8,10},{9,13},{10,... | collective-permute-start | bytes 1843208 | tf_op jit(solution)/shard_map/ppermute | solution.py:149
  114.6 0.8 copy-start.8
  118.4 8.9 %collective-permute-start.4 = (s16[48,3200]{1,0:T(8,128)(2,1)}, s16[48,3200]{1,0:T(8,128)(2,1)S(1)}, u32[]{:S(2)}, u32[]{:S(2)}) collective-permute-start(s16[48,3200]{1,0:T(8,128)(2,1)} %pad_add_fusion.1), channel_id=1, source_target_pairs={{0,4},{1,3},{2,6},{3,1},{4,0},{5,7},{6,2},{7,5},{8,12},{9,11},{10,... | collective-permute-start | bytes 921608 | tf_op jit(solution)/shard_map/ppermute | solution.py:149
  120.4 7.3 %collective-permute-start.5 = (bf16[48,2048]{1,0:T(8,128)(2,1)}, bf16[48,2048]{1,0:T(8,128)(2,1)S(1)}, u32[]{:S(2)}, u32[]{:S(2)}) collective-permute-start(bf16[48,2048]{1,0:T(8,128)(2,1)} %bitcast.18), channel_id=1, source_target_pairs={{0,0},{1,4},{2,2},{3,6},{4,1},{5,3},{6,5},{7,7},{8,8},{9,12},{10,1... | collective-permute-start | bytes 589832 | tf_op jit(solution)/shard_map/ppermute | solution.py:107
  127.9 27.9 %copy-start.3 = (bf16[1,1,1024,448]{2,3,1,0:T(8,128)(2,1)S(1)}, bf16[1,1,1024,448]{2,3,1,0:T(8,128)(2,1)}, u32[]{:S(2)}) copy-start(bf16[1,1,1024,448]{2,3,1,0:T(8,128)(2,1)} %param.16) | copy-start | bytes 2752516
  127.9 8.7 %collective-permute-start.6 = (bf16[48,3072]{1,0:T(8,128)(2,1)S(1)}, bf16[48,3072]{1,0:T(8,128)(2,1)S(1)}, u32[]{:S(2)}, u32[]{:S(2)}) collective-permute-start(bf16[48,3072]{1,0:T(8,128)(2,1)S(1)} %pad_maximum_fusion.16), channel_id=1, source_target_pairs={{0,4},{1,3},{2,6},{3,1},{4,0},{5,7},{6,2},{7,5},{8,12},{9,11},{10,... | collective-permute-start | bytes 884744 | tf_op jit(solution)/shard_map/ppermute | solution.py:167
  136.7 12.1 %collective-permute-start.7 = (bf16[96,3072]{1,0:T(8,128)(2,1)S(1)}, bf16[96,3072]{1,0:T(8,128)(2,1)S(1)}, u32[]{:S(2)}, u32[]{:S(2)}) collective-permute-start(bf16[96,3072]{1,0:T(8,128)(2,1)S(1)} %pad_maximum_fusion.15), channel_id=1, source_target_pairs={{0,2},{1,5},{2,0},{3,7},{4,6},{5,1},{6,4},{7,3},{8,10},{9,13},{10,... | collective-permute-start | bytes 1769480 | tf_op jit(solution)/shard_map/ppermute | solution.py:167
  148.8 0.8 copy-start.9
  150.7 5.1 %collective-permute-start.8 = (bf16[192,3072]{1,0:T(8,128)(2,1)}, bf16[192,3072]{1,0:T(8,128)(2,1)}, u32[]{:S(2)}, u32[]{:S(2)}) collective-permute-start(bf16[192,3072]{1,0:T(8,128)(2,1)} %pad_maximum_fusion.13), channel_id=1, source_target_pairs={{0,1},{1,0},{2,3},{3,2},{4,5},{5,4},{6,7},{7,6},{8,9},{9,8},{10,11... | collective-permute-start | bytes 3538952 | tf_op jit(solution)/shard_map/ppermute | solution.py:167
  164.7 7.8 %copy-start.10 = (f32[1,32,1]{1,2,0:T(1,128)S(1)}, f32[1,32,1]{1,2,0:T(1,128)}, u32[]{:S(2)}) copy-start(f32[1,32,1]{1,2,0:T(1,128)} %param.14) | copy-start | bytes 388
  164.7 7.8 %copy-start.11 = (f32[1,32,1]{1,2,0:T(1,128)S(1)}, f32[1,32,1]{1,2,0:T(1,128)}, u32[]{:S(2)}) copy-start(f32[1,32,1]{1,2,0:T(1,128)} %param.11) | copy-start | bytes 388
  166.4 51.0 %all-to-all-start.1 = ((bf16[64,2,6,448]{3,1,2,0:T(2,128)(2,1)}), bf16[64,2,6,448]{3,1,2,0:T(2,128)(2,1)S(1)}, u32[]{:S(2)}, u32[]{:S(2)}) async-start(bf16[64,2,6,448]{3,1,2,0:T(2,128)(2,1)} %bitcast.22), calls=%async_computation.1 | async-start | bytes 1572864 | tf_op jit(solution)/shard_map/all_to_all | solution.py:188
  218.5 2.0 copy-start.5
  218.5 2.0 copy-start.7

commit v6 on v5

--- a/solution.py
+++ b/solution.py
@@ -163,17 +163,23 @@
     up_grad = hidden_grad * gate_pre * sigmoid_gate
     current = jnp.concatenate([hidden_share, gate_grad.astype(jnp.bfloat16), up_grad.astype(jnp.bfloat16)], axis=1)
 
-    for stage in reversed(range(levels)):
+    for stage in reversed(range(1, levels)):
         partner = lax.ppermute(current, "expert", stage_route(devices, group_size, stage))
         current = jnp.concatenate([current, partner], axis=0)
-    out_down = jnp.dot(
-        current[:, :hidden_units], proj_out, preferred_element_type=jnp.float32
-    ).astype(jnp.bfloat16)
-    out_up = lax.dot_general(
-        current[:, hidden_units:], proj_in, (((1,), (1,)), ((), ())),
-        preferred_element_type=jnp.float32,
-    ).astype(jnp.bfloat16)
-    result = jnp.stack([out_down, out_up])
+
+    def last_matmul(block):
+        out_down = jnp.dot(
+            block[:, :hidden_units], proj_out, preferred_element_type=jnp.float32
+        ).astype(jnp.bfloat16)
+        out_up = lax.dot_general(
+            block[:, hidden_units:], proj_in, (((1,), (1,)), ((), ())),
+            preferred_element_type=jnp.float32,
+        ).astype(jnp.bfloat16)
+        return jnp.stack([out_down, out_up])
+
+    partner = lax.ppermute(current, "expert", stage_route(devices, group_size, 0))
+    own_out = last_matmul(current)
+    result = jnp.concatenate([own_out, last_matmul(partner)], axis=1)
     view = result.reshape((2,) + (2,) * levels + (-1, share_width))
     neighbour = index ^ 1
     for stage in reversed(range(1, levels)):

time: 223 us -> 220 us (0.987)
  local copies, waits for them, and re-layouts: 19.3 us -> 15.3 us
  waiting for transfers between devices: 131 us -> 128 us
    ppermute x3 -> x2, waiting for transfers between devices: 15.4 us -> 12.6 us  [body(): lax.ppermute(current, 'expert', stage_route(devices, group_size, stage))]
    convert_element_type x2 -> x0, local copies, waits for them, and re-layouts: 2.29 us -> none  [the longest x1 1.15 us: body(): out_down = jnp.dot(current[:, :hidden_units], proj_out, preferred_element...]
    ppermute x3 -> x2, starting transfers between devices: 10.4 us -> 8.21 us  [body(): lax.ppermute(current, 'expert', stage_route(devices, group_size, stage))]
    dot_general x2 -> x4, matrix products: 5.57 us -> 6.49 us  [the longest x2 3.6 us: last_matmul(): lax.dot_general(block[:, hidden_units:], proj_in, (((1,), (1,)), ((), ())...]
  transfers between devices with their start and end apart: 11 -> 11, of which waited for: 10 -> 9; matrix products, arithmetic and copies ran while one was open for 1% -> 3% of each run, Pallas kernels for 0% -> 0%
where the time goes in v6:
time: 220 us; the launch traced here: 219 us
  waiting for transfers between devices  128 us (58%)
  starting transfers between devices  50.9 us (23%)
  local copies, waits for them, and re-layouts  15.3 us (7%)
  other arithmetic  13.8 us (6%)
  matrix products  9.84 us (4%)
    all_to_all x1, waiting for transfers between devices, body(): lax.all_to_all(result, 'expert', split_axis=0, concat_axis=0, tiled=True)  44.9 us
    all_to_all x1, waiting for transfers between devices, body(): lax.all_to_all(sent, 'expert', split_axis=0, concat_axis=0, tiled=True)  44.8 us
    all_to_all x1, starting transfers between devices, body(): lax.all_to_all(sent, 'expert', split_axis=0, concat_axis=0, tiled=True)  17.1 us
    ppermute x2, waiting for transfers between devices, body(): lax.ppermute(encode_rows(send_part, 128), 'expert', stage_route(devices,...  15 us
    ppermute x2, waiting for transfers between devices, body(): lax.ppermute(current, 'expert', stage_route(devices, group_size, stage))  12.6 us
    ppermute x2, starting transfers between devices, shifted(): return lax.ppermute(block, axis, route)  9.59 us
    ppermute x2, starting transfers between devices, body(): lax.ppermute(current, 'expert', stage_route(devices, group_size, stage))  8.21 us
    ppermute x2, waiting for transfers between devices, shifted(): return lax.ppermute(block, axis, route)  6.51 us
  transfers between devices with their start and end apart: 11, of which 9 were waited for; matrix products, arithmetic and copies ran while one was open for 3% of the time, Pallas kernels for 0%

profile of v6, /device:TPU:8, one launch (start us, length us, event | category | flops | bytes accessed | tf_op | source)
XLA Modules:
  0.0 218.9 jit_solution(6288773170019062937)
XLA Ops:
  0.6 4.3 %collective-permute-start = (bf16[32,3584]{1,0:T(8,128)(2,1)}, bf16[32,3584]{1,0:T(8,128)(2,1)S(1)}, u32[]{:S(2)}, u32[]{:S(2)}) collective-permute-start(bf16[32,3584]{1,0:T(8,128)(2,1)} %bitcast.85), channel_id=1, source_target_pairs={{448,0},{0,64},{64,128},{128,192},{192,256},{256,320},{320,384},{3... | collective-permute-start | bytes 688136 | tf_op jit(solution)/shard_map/ppermute | solution.py:14
  5.0 5.3 %collective-permute-start.1 = (bf16[32,3584]{1,0:T(8,128)(2,1)}, bf16[32,3584]{1,0:T(8,128)(2,1)S(1)}, u32[]{:S(2)}, u32[]{:S(2)}) collective-permute-start(bf16[32,3584]{1,0:T(8,128)(2,1)} %bitcast.86), channel_id=1, source_target_pairs={{64,0},{128,64},{192,128},{256,192},{320,256},{384,320},{448,384},... | collective-permute-start | bytes 688136 | tf_op jit(solution)/shard_map/ppermute | solution.py:14
  10.3 0.7 pad_add_fusion.2
  10.9 0.2 convert_reduce_fusion
  11.1 2.8 %collective-permute-done = bf16[32,3584]{1,0:T(8,128)(2,1)S(1)} collective-permute-done((bf16[32,3584]{1,0:T(8,128)(2,1)}, bf16[32,3584]{1,0:T(8,128)(2,1)S(1)}, u32[]{:S(2)}, u32[]{:S(2)}) %collective-permute-start) | collective-permute-done | bytes 229408 | tf_op jit(solution)/shard_map/ppermute | solution.py:14
  13.9 0.7 copy-done.4
  14.6 0.3 stack.67
  15.0 3.7 %collective-permute-done.1 = bf16[32,3584]{1,0:T(8,128)(2,1)S(1)} collective-permute-done((bf16[32,3584]{1,0:T(8,128)(2,1)}, bf16[32,3584]{1,0:T(8,128)(2,1)S(1)}, u32[]{:S(2)}, u32[]{:S(2)}) %collective-permute-start.1) | collective-permute-done | bytes 229408 | tf_op jit(solution)/shard_map/ppermute | solution.py:14
  18.8 0.3 stack.68
  19.2 0.4 fusion.8
  19.6 0.4 copy.58
  20.0 1.7 copy.42
  21.7 17.1 %all-to-all-start = ((bf16[64,2,6,448]{3,1,2,0:T(2,128)(2,1)}), bf16[64,2,6,448]{3,1,2,0:T(2,128)(2,1)S(1)}, u32[]{:S(2)}, u32[]{:S(2)}) async-start(bf16[64,2,6,448]{3,1,2,0:T(2,128)(2,1)} %copy.42), calls=%async_computation | async-start | bytes 1572864 | tf_op jit(solution)/shard_map/all_to_all | solution.py:125
  38.9 44.8 %all-to-all-done = bf16[64,2,6,448]{3,1,2,0:T(2,128)(2,1)S(1)} async-done(((bf16[64,2,6,448]{3,1,2,0:T(2,128)(2,1)}), bf16[64,2,6,448]{3,1,2,0:T(2,128)(2,1)S(1)}, u32[]{:S(2)}, u32[]{:S(2)}) %all-to-all-start) | async-done | bytes 688160 | tf_op jit(solution)/shard_map/all_to_all | solution.py:125
  83.7 4.2 %slice_reduce_fusion.1 = (bf16[64,6,448]{2,1,0:T(8,128)(2,1)}, bf16[64,6,448]{2,1,0:T(8,128)(2,1)S(1)}) fusion(bf16[64,2,6,448]{3,1,2,0:T(2,128)(2,1)S(1)} %all-to-all-done), kind=kLoop, calls=%fused_computation.38 | loop fusion | bytes 1376256 | tf_op jit(solution)/shard_map/slice | solution.py:126
  87.9 1.3 reshape_squeeze.6
  89.2 0.2 reshape_squeeze.7
  89.4 0.6 fusion.4
  90.0 0.6 copy-done.2
  90.6 0.4 fusion.25
  91.0 1.6 pad_maximum_fusion
  92.5 1.9 collective-permute-start.2
  94.5 0.4 fusion.27
  94.8 0.6 fusion.6
  95.4 3.9 %collective-permute-done.2 = f32[192,3072]{1,0:T(8,128)} collective-permute-done((f32[192,3072]{1,0:T(8,128)}, f32[192,3072]{1,0:T(8,128)}, u32[]{:S(2)}, u32[]{:S(2)}) %collective-permute-start.2) | collective-permute-done | bytes 2359328 | tf_op jit(solution)/shard_map/ppermute | solution.py:141
  99.3 1.9 maximum_add_fusion
  101.2 0.2 abs_reduce_fusion
  101.4 0.3 round-nearest-even_convert_fusion
  101.8 0.8 copy-done.1
  102.6 2.4 %collective-permute-start.3 = (s16[96,3200]{1,0:T(8,128)(2,1)S(1)}, s16[96,3200]{1,0:T(8,128)(2,1)S(1)}, u32[]{:S(2)}, u32[]{:S(2)}) collective-permute-start(s16[96,3200]{1,0:T(8,128)(2,1)S(1)} %pad_add_fusion), channel_id=1, source_target_pairs={{0,2},{1,5},{2,0},{3,7},{4,6},{5,1},{6,4},{7,3},{8,10},{9,13},{10,... | collective-permute-start | bytes 1843208 | tf_op jit(solution)/shard_map/ppermute | solution.py:149
  105.1 9.6 %collective-permute-done.3 = s16[96,3200]{1,0:T(8,128)(2,1)S(1)} collective-permute-done((s16[96,3200]{1,0:T(8,128)(2,1)S(1)}, s16[96,3200]{1,0:T(8,128)(2,1)S(1)}, u32[]{:S(2)}, u32[]{:S(2)}) %collective-permute-start.3) | collective-permute-done | bytes 614432 | tf_op jit(solution)/shard_map/ppermute | solution.py:149
  114.7 0.8 copy-done.8
  115.5 0.1 exponential_reduce_fusion
  115.6 1.7 multiply_add_fusion
  117.3 0.1 abs_reduce_fusion.1
  117.5 0.2 round-nearest-even_convert_fusion.1
  117.7 0.7 pad_add_fusion.1
  118.5 1.9 collective-permute-start.4
  120.4 1.6 collective-permute-start.5
  122.0 5.4 %collective-permute-done.4 = s16[48,3200]{1,0:T(8,128)(2,1)S(1)} collective-permute-done((s16[48,3200]{1,0:T(8,128)(2,1)}, s16[48,3200]{1,0:T(8,128)(2,1)S(1)}, u32[]{:S(2)}, u32[]{:S(2)}) %collective-permute-start.4) | collective-permute-done | bytes 307232 | tf_op jit(solution)/shard_map/ppermute | solution.py:149
  127.4 0.1 exponential_reduce_fusion.1
  127.5 0.1 multiply_add_fusion.1
  127.7 0.2 fusion.41
  127.9 3.9 %collective-permute-start.6 = (bf16[48,3072]{1,0:T(8,128)(2,1)S(1)}, bf16[48,3072]{1,0:T(8,128)(2,1)S(1)}, u32[]{:S(2)}, u32[]{:S(2)}) collective-permute-start(bf16[48,3072]{1,0:T(8,128)(2,1)S(1)} %pad_maximum_fusion.3), channel_id=1, source_target_pairs={{0,4},{1,3},{2,6},{3,1},{4,0},{5,7},{6,2},{7,5},{8,12},{9,11},{10,... | collective-permute-start | bytes 884744 | tf_op jit(solution)/shard_map/ppermute | solution.py:167
  131.9 4.8 %collective-permute-done.6 = bf16[48,3072]{1,0:T(8,128)(2,1)S(1)} collective-permute-done((bf16[48,3072]{1,0:T(8,128)(2,1)S(1)}, bf16[48,3072]{1,0:T(8,128)(2,1)S(1)}, u32[]{:S(2)}, u32[]{:S(2)}) %collective-permute-start.6) | collective-permute-done | bytes 294944 | tf_op jit(solution)/shard_map/ppermute | solution.py:167
  136.7 4.3 %collective-permute-start.7 = (bf16[96,3072]{1,0:T(8,128)(2,1)S(1)}, bf16[96,3072]{1,0:T(8,128)(2,1)S(1)}, u32[]{:S(2)}, u32[]{:S(2)}) collective-permute-start(bf16[96,3072]{1,0:T(8,128)(2,1)S(1)} %pad_maximum_fusion.2), channel_id=1, source_target_pairs={{0,2},{1,5},{2,0},{3,7},{4,6},{5,1},{6,4},{7,3},{8,10},{9,13},{10,... | collective-permute-start | bytes 1769480 | tf_op jit(solution)/shard_map/ppermute | solution.py:167
  141.0 7.8 %collective-permute-done.7 = bf16[96,3072]{1,0:T(8,128)(2,1)S(1)} collective-permute-done((bf16[96,3072]{1,0:T(8,128)(2,1)S(1)}, bf16[96,3072]{1,0:T(8,128)(2,1)S(1)}, u32[]{:S(2)}, u32[]{:S(2)}) %collective-permute-start.7) | collective-permute-done | bytes 589856 | tf_op jit(solution)/shard_map/ppermute | solution.py:167
  148.8 1.1 pad_maximum_fusion.1
  149.9 2.2 %collective-permute-start.8 = (bf16[192,3072]{1,0:T(8,128)(2,1)}, bf16[192,3072]{1,0:T(8,128)(2,1)}, u32[]{:S(2)}, u32[]{:S(2)}) collective-permute-start(bf16[192,3072]{1,0:T(8,128)(2,1)} %pad_maximum_fusion.1), channel_id=1, source_target_pairs={{0,1},{1,0},{2,3},{3,2},{4,5},{5,4},{6,7},{7,6},{8,9},{9,8},{10,11... | collective-permute-start | bytes 3538952 | tf_op jit(solution)/shard_map/ppermute | solution.py:180
  152.2 1.4 fusion.21
  153.7 1.8 fusion.18
  155.5 1.8 fusion.15
  157.3 1.4 fusion.22
  158.9 0.8 copy.43
  159.7 0.8 broadcast_select_fusion
  160.5 0.7 broadcast_select_fusion.1
  161.2 1.5 broadcast_select_fusion.2
  162.7 6.0 %all-to-all-start.1 = ((bf16[64,2,6,448]{3,1,2,0:T(2,128)(2,1)}), bf16[64,2,6,448]{3,1,2,0:T(2,128)(2,1)S(1)}, u32[]{:S(2)}, u32[]{:S(2)}) async-start(bf16[64,2,6,448]{3,1,2,0:T(2,128)(2,1)} %bitcast.25), calls=%async_computation.1 | async-start | bytes 1572864 | tf_op jit(solution)/shard_map/all_to_all | solution.py:194
  168.8 44.9 %all-to-all-done.1 = bf16[64,2,6,448]{3,1,2,0:T(2,128)(2,1)S(1)} async-done(((bf16[64,2,6,448]{3,1,2,0:T(2,128)(2,1)}), bf16[64,2,6,448]{3,1,2,0:T(2,128)(2,1)S(1)}, u32[]{:S(2)}, u32[]{:S(2)}) %all-to-all-start.1) | async-done | bytes 688160 | tf_op jit(solution)/shard_map/all_to_all | solution.py:194
  213.7 1.1 convolution_bitcast_fusion
  214.7 0.6 copy.47
  215.4 1.3 reshape.152
  216.7 1.4 add_convert_fusion
  218.1 0.8 fusion.64
  (35 shorter events, 0.7 us)
Async XLA Ops:
  0.6 88.8 %copy-start = (bf16[1,1,448,2048]{3,2,1,0:T(8,128)(2,1)S(1)}, bf16[1,1,448,2048]{3,2,1,0:T(8,128)(2,1)}, u32[]{:S(2)}) copy-start(bf16[1,1,448,2048]{3,2,1,0:T(8,128)(2,1)} %param.15) | copy-start | bytes 5505028
  0.6 13.3 %collective-permute-start = (bf16[32,3584]{1,0:T(8,128)(2,1)}, bf16[32,3584]{1,0:T(8,128)(2,1)S(1)}, u32[]{:S(2)}, u32[]{:S(2)}) collective-permute-start(bf16[32,3584]{1,0:T(8,128)(2,1)} %bitcast.85), channel_id=1, source_target_pairs={{448,0},{0,64},{64,128},{128,192},{192,256},{256,320},{320,384},{3... | collective-permute-start | bytes 688136 | tf_op jit(solution)/shard_map/ppermute | solution.py:14
  5.0 13.8 %collective-permute-start.1 = (bf16[32,3584]{1,0:T(8,128)(2,1)}, bf16[32,3584]{1,0:T(8,128)(2,1)S(1)}, u32[]{:S(2)}, u32[]{:S(2)}) collective-permute-start(bf16[32,3584]{1,0:T(8,128)(2,1)} %bitcast.86), channel_id=1, source_target_pairs={{64,0},{128,64},{192,128},{256,192},{320,256},{384,320},{448,384},... | collective-permute-start | bytes 688136 | tf_op jit(solution)/shard_map/ppermute | solution.py:14
  13.9 0.7 copy-start.4
  18.8 1.3 copy-start.6
  21.7 61.9 %all-to-all-start = ((bf16[64,2,6,448]{3,1,2,0:T(2,128)(2,1)}), bf16[64,2,6,448]{3,1,2,0:T(2,128)(2,1)S(1)}, u32[]{:S(2)}, u32[]{:S(2)}) async-start(bf16[64,2,6,448]{3,1,2,0:T(2,128)(2,1)} %copy.42), calls=%async_computation | async-start | bytes 1572864 | tf_op jit(solution)/shard_map/all_to_all | solution.py:125
  89.4 1.2 copy-start.2
  92.5 6.8 %collective-permute-start.2 = (f32[192,3072]{1,0:T(8,128)}, f32[192,3072]{1,0:T(8,128)}, u32[]{:S(2)}, u32[]{:S(2)}) collective-permute-start(f32[192,3072]{1,0:T(8,128)} %pad_maximum_fusion), channel_id=1, source_target_pairs={{0,1},{1,0},{2,3},{3,2},{4,5},{5,4},{6,7},{7,6},{8,9},{9,8},{10,11... | collective-permute-start | bytes 7077896 | tf_op jit(solution)/shard_map/ppermute | solution.py:141
  101.2 1.4 copy-start.1
  102.6 12.0 %collective-permute-start.3 = (s16[96,3200]{1,0:T(8,128)(2,1)S(1)}, s16[96,3200]{1,0:T(8,128)(2,1)S(1)}, u32[]{:S(2)}, u32[]{:S(2)}) collective-permute-start(s16[96,3200]{1,0:T(8,128)(2,1)S(1)} %pad_add_fusion), channel_id=1, source_target_pairs={{0,2},{1,5},{2,0},{3,7},{4,6},{5,1},{6,4},{7,3},{8,10},{9,13},{10,... | collective-permute-start | bytes 1843208 | tf_op jit(solution)/shard_map/ppermute | solution.py:149
  114.7 0.8 copy-start.8
  118.5 8.9 %collective-permute-start.4 = (s16[48,3200]{1,0:T(8,128)(2,1)}, s16[48,3200]{1,0:T(8,128)(2,1)S(1)}, u32[]{:S(2)}, u32[]{:S(2)}) collective-permute-start(s16[48,3200]{1,0:T(8,128)(2,1)} %pad_add_fusion.1), channel_id=1, source_target_pairs={{0,4},{1,3},{2,6},{3,1},{4,0},{5,7},{6,2},{7,5},{8,12},{9,11},{10,... | collective-permute-start | bytes 921608 | tf_op jit(solution)/shard_map/ppermute | solution.py:149
  120.4 7.3 %collective-permute-start.5 = (bf16[48,2048]{1,0:T(8,128)(2,1)}, bf16[48,2048]{1,0:T(8,128)(2,1)S(1)}, u32[]{:S(2)}, u32[]{:S(2)}) collective-permute-start(bf16[48,2048]{1,0:T(8,128)(2,1)} %bitcast.18), channel_id=1, source_target_pairs={{0,0},{1,4},{2,2},{3,6},{4,1},{5,3},{6,5},{7,7},{8,8},{9,12},{10,1... | collective-permute-start | bytes 589832 | tf_op jit(solution)/shard_map/ppermute | solution.py:107
  127.9 24.3 %copy-start.3 = (bf16[1,1,1024,448]{2,3,1,0:T(8,128)(2,1)S(1)}, bf16[1,1,1024,448]{2,3,1,0:T(8,128)(2,1)}, u32[]{:S(2)}) copy-start(bf16[1,1,1024,448]{2,3,1,0:T(8,128)(2,1)} %param.16) | copy-start | bytes 2752516
  127.9 8.7 %collective-permute-start.6 = (bf16[48,3072]{1,0:T(8,128)(2,1)S(1)}, bf16[48,3072]{1,0:T(8,128)(2,1)S(1)}, u32[]{:S(2)}, u32[]{:S(2)}) collective-permute-start(bf16[48,3072]{1,0:T(8,128)(2,1)S(1)} %pad_maximum_fusion.3), channel_id=1, source_target_pairs={{0,4},{1,3},{2,6},{3,1},{4,0},{5,7},{6,2},{7,5},{8,12},{9,11},{10,... | collective-permute-start | bytes 884744 | tf_op jit(solution)/shard_map/ppermute | solution.py:167
  136.7 12.1 %collective-permute-start.7 = (bf16[96,3072]{1,0:T(8,128)(2,1)S(1)}, bf16[96,3072]{1,0:T(8,128)(2,1)S(1)}, u32[]{:S(2)}, u32[]{:S(2)}) collective-permute-start(bf16[96,3072]{1,0:T(8,128)(2,1)S(1)} %pad_maximum_fusion.2), channel_id=1, source_target_pairs={{0,2},{1,5},{2,0},{3,7},{4,6},{5,1},{6,4},{7,3},{8,10},{9,13},{10,... | collective-permute-start | bytes 1769480 | tf_op jit(solution)/shard_map/ppermute | solution.py:167
  149.9 5.6 %collective-permute-start.8 = (bf16[192,3072]{1,0:T(8,128)(2,1)}, bf16[192,3072]{1,0:T(8,128)(2,1)}, u32[]{:S(2)}, u32[]{:S(2)}) collective-permute-start(bf16[192,3072]{1,0:T(8,128)(2,1)} %pad_maximum_fusion.1), channel_id=1, source_target_pairs={{0,1},{1,0},{2,3},{3,2},{4,5},{5,4},{6,7},{7,6},{8,9},{9,8},{10,11... | collective-permute-start | bytes 3538952 | tf_op jit(solution)/shard_map/ppermute | solution.py:180
  161.2 7.5 %copy-start.9 = (f32[1,32,1]{1,2,0:T(1,128)S(1)}, f32[1,32,1]{1,2,0:T(1,128)}, u32[]{:S(2)}) copy-start(f32[1,32,1]{1,2,0:T(1,128)} %param.14) | copy-start | bytes 388
  161.2 7.5 %copy-start.10 = (f32[1,32,1]{1,2,0:T(1,128)S(1)}, f32[1,32,1]{1,2,0:T(1,128)}, u32[]{:S(2)}) copy-start(f32[1,32,1]{1,2,0:T(1,128)} %param.11) | copy-start | bytes 388
  162.7 50.9 %all-to-all-start.1 = ((bf16[64,2,6,448]{3,1,2,0:T(2,128)(2,1)}), bf16[64,2,6,448]{3,1,2,0:T(2,128)(2,1)S(1)}, u32[]{:S(2)}, u32[]{:S(2)}) async-start(bf16[64,2,6,448]{3,1,2,0:T(2,128)(2,1)} %bitcast.25), calls=%async_computation.1 | async-start | bytes 1572864 | tf_op jit(solution)/shard_map/all_to_all | solution.py:194
  214.7 2.0 copy-start.5
  214.7 2.0 copy-start.7

commit v7 on v6

--- a/solution.py
+++ b/solution.py
@@ -180,16 +180,22 @@
     partner = lax.ppermute(current, "expert", stage_route(devices, group_size, 0))
     own_out = last_matmul(current)
     result = jnp.concatenate([own_out, last_matmul(partner)], axis=1)
-    view = result.reshape((2,) + (2,) * levels + (-1, share_width))
     neighbour = index ^ 1
-    for stage in reversed(range(1, levels)):
-        flags = jnp.stack(
-            [own_stage_bit(index, group_size, stage), own_stage_bit(neighbour, group_size, stage)]
-        ).reshape((1, 2) + (1,) * (levels + 1))
-        view = jnp.where(flags == 1, jnp.flip(view, axis=1 + stage), view)
-    top = own_stage_bit(index, group_size, 0)
-    view = jnp.where(top == 1, jnp.flip(view, axis=1), view)
-    result = view.reshape(2, -1, share_width)
+    flags = [
+        [own_stage_bit(index, group_size, stage), own_stage_bit(neighbour, group_size, stage)]
+        for stage in range(levels)
+    ]
+    sources = []
+    for position in range(group_size):
+        wanted = [position >> (levels - 1 - level) & 1 for level in range(levels)]
+        first = wanted[0] ^ flags[0][0]
+        source = first
+        for level in range(1, levels):
+            flag = jnp.where(first == 1, flags[level][1], flags[level][0])
+            source = source * 2 + (wanted[level] ^ flag)
+        sources.append(source)
+    blocks = result.reshape(2, group_size, -1, share_width)
+    result = jnp.take(blocks, jnp.stack(sources), axis=1).reshape(2, -1, share_width)
     result = result.reshape(2, devices, MOST, share_width).transpose(1, 0, 2, 3)
     back = lax.all_to_all(result, "expert", split_axis=0, concat_axis=0, tiled=True)
     back = back.reshape(EXPERTS, group_size, 2, MOST, share_width)

time: 220 us -> 219 us (level)
    select_n x3 -> x1, other arithmetic: 3 us -> 0.01 us  [body(): jnp.take(blocks, jnp.stack(sources), axis=1).reshape(2, -1, share_width)]
where the time goes in v7:
time: 219 us
  waiting for transfers between devices  128 us (58%)
  starting transfers between devices  50.9 us (23%)
  local copies, waits for them, and re-layouts  16.3 us (7%)
  other arithmetic  12.5 us (6%)
  matrix products  9.84 us (4%)
    all_to_all x1, waiting for transfers between devices, body(): lax.all_to_all(result, 'expert', split_axis=0, concat_axis=0, tiled=True)  44.9 us
    all_to_all x1, waiting for transfers between devices, body(): lax.all_to_all(sent, 'expert', split_axis=0, concat_axis=0, tiled=True)  44.8 us
    all_to_all x1, starting transfers between devices, body(): lax.all_to_all(sent, 'expert', split_axis=0, concat_axis=0, tiled=True)  17.1 us
    ppermute x2, waiting for transfers between devices, body(): lax.ppermute(encode_rows(send_part, 128), 'expert', stage_route(devices,...  15 us
    ppermute x2, waiting for transfers between devices, body(): lax.ppermute(current, 'expert', stage_route(devices, group_size, stage))  12.6 us
    ppermute x2, starting transfers between devices, shifted(): return lax.ppermute(block, axis, route)  9.59 us
    ppermute x2, starting transfers between devices, body(): lax.ppermute(current, 'expert', stage_route(devices, group_size, stage))  8.2 us
    ppermute x2, waiting for transfers between devices, shifted(): return lax.ppermute(block, axis, route)  6.51 us
  transfers between devices with their start and end apart: 11, of which 9 were waited for; matrix products, arithmetic and copies ran while one was open for 3% of the time, Pallas kernels for 0%

profile of v7, /device:TPU:8, one launch (start us, length us, event | category | flops | bytes accessed | tf_op | source)
XLA Modules:
  0.0 218.5 jit_solution(7452651214061134863)
XLA Ops:
  0.6 4.3 %collective-permute-start = (bf16[32,3584]{1,0:T(8,128)(2,1)}, bf16[32,3584]{1,0:T(8,128)(2,1)S(1)}, u32[]{:S(2)}, u32[]{:S(2)}) collective-permute-start(bf16[32,3584]{1,0:T(8,128)(2,1)} %bitcast.102), channel_id=1, source_target_pairs={{448,0},{0,64},{64,128},{128,192},{192,256},{256,320},{320,384},{3... | collective-permute-start | bytes 688136 | tf_op jit(solution)/shard_map/ppermute | solution.py:14
  5.0 5.3 %collective-permute-start.1 = (bf16[32,3584]{1,0:T(8,128)(2,1)}, bf16[32,3584]{1,0:T(8,128)(2,1)S(1)}, u32[]{:S(2)}, u32[]{:S(2)}) collective-permute-start(bf16[32,3584]{1,0:T(8,128)(2,1)} %bitcast.103), channel_id=1, source_target_pairs={{64,0},{128,64},{192,128},{256,192},{320,256},{384,320},{448,384},... | collective-permute-start | bytes 688136 | tf_op jit(solution)/shard_map/ppermute | solution.py:14
  10.3 0.7 pad_add_fusion.2
  10.9 0.2 convert_reduce_fusion
  11.1 2.8 %collective-permute-done = bf16[32,3584]{1,0:T(8,128)(2,1)S(1)} collective-permute-done((bf16[32,3584]{1,0:T(8,128)(2,1)}, bf16[32,3584]{1,0:T(8,128)(2,1)S(1)}, u32[]{:S(2)}, u32[]{:S(2)}) %collective-permute-start) | collective-permute-done | bytes 229408 | tf_op jit(solution)/shard_map/ppermute | solution.py:14
  13.9 0.7 copy-done.4
  14.6 0.3 stack.97
  15.0 3.7 %collective-permute-done.1 = bf16[32,3584]{1,0:T(8,128)(2,1)S(1)} collective-permute-done((bf16[32,3584]{1,0:T(8,128)(2,1)}, bf16[32,3584]{1,0:T(8,128)(2,1)S(1)}, u32[]{:S(2)}, u32[]{:S(2)}) %collective-permute-start.1) | collective-permute-done | bytes 229408 | tf_op jit(solution)/shard_map/ppermute | solution.py:14
  18.8 0.3 stack.98
  19.2 0.4 fusion.8
  19.6 0.4 copy.62
  20.0 1.7 copy.47
  21.7 17.1 %all-to-all-start = ((bf16[64,2,6,448]{3,1,2,0:T(2,128)(2,1)}), bf16[64,2,6,448]{3,1,2,0:T(2,128)(2,1)S(1)}, u32[]{:S(2)}, u32[]{:S(2)}) async-start(bf16[64,2,6,448]{3,1,2,0:T(2,128)(2,1)} %copy.47), calls=%async_computation | async-start | bytes 1572864 | tf_op jit(solution)/shard_map/all_to_all | solution.py:125
  38.9 44.8 %all-to-all-done = bf16[64,2,6,448]{3,1,2,0:T(2,128)(2,1)S(1)} async-done(((bf16[64,2,6,448]{3,1,2,0:T(2,128)(2,1)}), bf16[64,2,6,448]{3,1,2,0:T(2,128)(2,1)S(1)}, u32[]{:S(2)}, u32[]{:S(2)}) %all-to-all-start) | async-done | bytes 688160 | tf_op jit(solution)/shard_map/all_to_all | solution.py:125
  83.7 4.2 %slice_reduce_fusion.1 = (bf16[64,6,448]{2,1,0:T(8,128)(2,1)}, bf16[64,6,448]{2,1,0:T(8,128)(2,1)S(1)}) fusion(bf16[64,2,6,448]{3,1,2,0:T(2,128)(2,1)S(1)} %all-to-all-done), kind=kLoop, calls=%fused_computation.37 | loop fusion | bytes 1376256 | tf_op jit(solution)/shard_map/slice | solution.py:126
  87.9 1.3 reshape_squeeze.6
  89.2 0.2 reshape_squeeze.7
  89.4 0.6 fusion.4
  90.0 0.6 copy-done.2
  90.6 0.4 fusion.25
  91.0 1.6 pad_maximum_fusion
  92.6 1.9 collective-permute-start.2
  94.5 0.4 fusion.27
  94.9 0.6 fusion.6
  95.4 3.9 %collective-permute-done.2 = f32[192,3072]{1,0:T(8,128)} collective-permute-done((f32[192,3072]{1,0:T(8,128)}, f32[192,3072]{1,0:T(8,128)}, u32[]{:S(2)}, u32[]{:S(2)}) %collective-permute-start.2) | collective-permute-done | bytes 2359328 | tf_op jit(solution)/shard_map/ppermute | solution.py:141
  99.3 1.9 maximum_add_fusion
  101.2 0.2 abs_reduce_fusion
  101.4 0.3 round-nearest-even_convert_fusion
  101.8 0.8 copy-done.1
  102.7 2.4 %collective-permute-start.3 = (s16[96,3200]{1,0:T(8,128)(2,1)S(1)}, s16[96,3200]{1,0:T(8,128)(2,1)S(1)}, u32[]{:S(2)}, u32[]{:S(2)}) collective-permute-start(s16[96,3200]{1,0:T(8,128)(2,1)S(1)} %pad_add_fusion), channel_id=1, source_target_pairs={{0,2},{1,5},{2,0},{3,7},{4,6},{5,1},{6,4},{7,3},{8,10},{9,13},{10,... | collective-permute-start | bytes 1843208 | tf_op jit(solution)/shard_map/ppermute | solution.py:149
  105.1 9.6 %collective-permute-done.3 = s16[96,3200]{1,0:T(8,128)(2,1)S(1)} collective-permute-done((s16[96,3200]{1,0:T(8,128)(2,1)S(1)}, s16[96,3200]{1,0:T(8,128)(2,1)S(1)}, u32[]{:S(2)}, u32[]{:S(2)}) %collective-permute-start.3) | collective-permute-done | bytes 614432 | tf_op jit(solution)/shard_map/ppermute | solution.py:149
  114.7 0.9 copy-done.8
  115.5 0.1 exponential_reduce_fusion
  115.7 1.7 multiply_add_fusion
  117.3 0.1 abs_reduce_fusion.1
  117.5 0.2 round-nearest-even_convert_fusion.1
  117.8 0.7 pad_add_fusion.1
  118.5 1.9 collective-permute-start.4
  120.4 1.6 collective-permute-start.5
  122.0 5.4 %collective-permute-done.4 = s16[48,3200]{1,0:T(8,128)(2,1)S(1)} collective-permute-done((s16[48,3200]{1,0:T(8,128)(2,1)}, s16[48,3200]{1,0:T(8,128)(2,1)S(1)}, u32[]{:S(2)}, u32[]{:S(2)}) %collective-permute-start.4) | collective-permute-done | bytes 307232 | tf_op jit(solution)/shard_map/ppermute | solution.py:149
  127.4 0.1 exponential_reduce_fusion.1
  127.6 0.1 multiply_add_fusion.1
  127.7 0.2 fusion.42
  127.9 3.9 %collective-permute-start.6 = (bf16[48,3072]{1,0:T(8,128)(2,1)S(1)}, bf16[48,3072]{1,0:T(8,128)(2,1)S(1)}, u32[]{:S(2)}, u32[]{:S(2)}) collective-permute-start(bf16[48,3072]{1,0:T(8,128)(2,1)S(1)} %pad_maximum_fusion.3), channel_id=1, source_target_pairs={{0,4},{1,3},{2,6},{3,1},{4,0},{5,7},{6,2},{7,5},{8,12},{9,11},{10,... | collective-permute-start | bytes 884744 | tf_op jit(solution)/shard_map/ppermute | solution.py:167
  131.9 4.8 %collective-permute-done.6 = bf16[48,3072]{1,0:T(8,128)(2,1)S(1)} collective-permute-done((bf16[48,3072]{1,0:T(8,128)(2,1)S(1)}, bf16[48,3072]{1,0:T(8,128)(2,1)S(1)}, u32[]{:S(2)}, u32[]{:S(2)}) %collective-permute-start.6) | collective-permute-done | bytes 294944 | tf_op jit(solution)/shard_map/ppermute | solution.py:167
  136.7 4.3 %collective-permute-start.7 = (bf16[96,3072]{1,0:T(8,128)(2,1)S(1)}, bf16[96,3072]{1,0:T(8,128)(2,1)S(1)}, u32[]{:S(2)}, u32[]{:S(2)}) collective-permute-start(bf16[96,3072]{1,0:T(8,128)(2,1)S(1)} %pad_maximum_fusion.2), channel_id=1, source_target_pairs={{0,2},{1,5},{2,0},{3,7},{4,6},{5,1},{6,4},{7,3},{8,10},{9,13},{10,... | collective-permute-start | bytes 1769480 | tf_op jit(solution)/shard_map/ppermute | solution.py:167
  141.0 7.8 %collective-permute-done.7 = bf16[96,3072]{1,0:T(8,128)(2,1)S(1)} collective-permute-done((bf16[96,3072]{1,0:T(8,128)(2,1)S(1)}, bf16[96,3072]{1,0:T(8,128)(2,1)S(1)}, u32[]{:S(2)}, u32[]{:S(2)}) %collective-permute-start.7) | collective-permute-done | bytes 589856 | tf_op jit(solution)/shard_map/ppermute | solution.py:167
  148.8 1.1 pad_maximum_fusion.1
  150.0 2.2 %collective-permute-start.8 = (bf16[192,3072]{1,0:T(8,128)(2,1)}, bf16[192,3072]{1,0:T(8,128)(2,1)}, u32[]{:S(2)}, u32[]{:S(2)}) collective-permute-start(bf16[192,3072]{1,0:T(8,128)(2,1)} %pad_maximum_fusion.1), channel_id=1, source_target_pairs={{0,1},{1,0},{2,3},{3,2},{4,5},{5,4},{6,7},{7,6},{8,9},{9,8},{10,11... | collective-permute-start | bytes 3538952 | tf_op jit(solution)/shard_map/ppermute | solution.py:180
  152.5 0.1 stack.115
  152.6 1.4 fusion.21
  154.1 1.8 fusion.18
  155.9 1.8 fusion.15
  157.7 1.4 fusion.22
  159.2 0.6 gather_fusion
  159.8 0.8 copy.48
  160.7 1.7 fusion.32
  162.4 6.0 %all-to-all-start.1 = ((bf16[64,2,6,448]{3,1,2,0:T(2,128)(2,1)}), bf16[64,2,6,448]{3,1,2,0:T(2,128)(2,1)S(1)}, u32[]{:S(2)}, u32[]{:S(2)}) async-start(bf16[64,2,6,448]{3,1,2,0:T(2,128)(2,1)} %fusion.32), calls=%async_computation.1 | async-start | bytes 1572864 | tf_op jit(solution)/shard_map/all_to_all | solution.py:200
  168.4 44.9 %all-to-all-done.1 = bf16[64,2,6,448]{3,1,2,0:T(2,128)(2,1)S(1)} async-done(((bf16[64,2,6,448]{3,1,2,0:T(2,128)(2,1)}), bf16[64,2,6,448]{3,1,2,0:T(2,128)(2,1)S(1)}, u32[]{:S(2)}, u32[]{:S(2)}) %all-to-all-start.1) | async-done | bytes 688160 | tf_op jit(solution)/shard_map/all_to_all | solution.py:200
  213.3 1.1 convolution_bitcast_fusion
  214.4 0.6 copy.51
  215.0 1.4 reshape.465
  216.4 1.4 add_convert_fusion
  217.7 0.8 fusion.66
  (40 shorter events, 0.9 us)
Async XLA Ops:
  0.6 88.8 %copy-start = (bf16[1,1,448,2048]{3,2,1,0:T(8,128)(2,1)S(1)}, bf16[1,1,448,2048]{3,2,1,0:T(8,128)(2,1)}, u32[]{:S(2)}) copy-start(bf16[1,1,448,2048]{3,2,1,0:T(8,128)(2,1)} %param.15) | copy-start | bytes 5505028
  0.6 13.3 %collective-permute-start = (bf16[32,3584]{1,0:T(8,128)(2,1)}, bf16[32,3584]{1,0:T(8,128)(2,1)S(1)}, u32[]{:S(2)}, u32[]{:S(2)}) collective-permute-start(bf16[32,3584]{1,0:T(8,128)(2,1)} %bitcast.102), channel_id=1, source_target_pairs={{448,0},{0,64},{64,128},{128,192},{192,256},{256,320},{320,384},{3... | collective-permute-start | bytes 688136 | tf_op jit(solution)/shard_map/ppermute | solution.py:14
  5.0 13.8 %collective-permute-start.1 = (bf16[32,3584]{1,0:T(8,128)(2,1)}, bf16[32,3584]{1,0:T(8,128)(2,1)S(1)}, u32[]{:S(2)}, u32[]{:S(2)}) collective-permute-start(bf16[32,3584]{1,0:T(8,128)(2,1)} %bitcast.103), channel_id=1, source_target_pairs={{64,0},{128,64},{192,128},{256,192},{320,256},{384,320},{448,384},... | collective-permute-start | bytes 688136 | tf_op jit(solution)/shard_map/ppermute | solution.py:14
  13.9 0.7 copy-start.4
  18.8 1.3 copy-start.6
  21.7 61.9 %all-to-all-start = ((bf16[64,2,6,448]{3,1,2,0:T(2,128)(2,1)}), bf16[64,2,6,448]{3,1,2,0:T(2,128)(2,1)S(1)}, u32[]{:S(2)}, u32[]{:S(2)}) async-start(bf16[64,2,6,448]{3,1,2,0:T(2,128)(2,1)} %copy.47), calls=%async_computation | async-start | bytes 1572864 | tf_op jit(solution)/shard_map/all_to_all | solution.py:125
  89.4 1.2 copy-start.2
  92.6 6.8 %collective-permute-start.2 = (f32[192,3072]{1,0:T(8,128)}, f32[192,3072]{1,0:T(8,128)}, u32[]{:S(2)}, u32[]{:S(2)}) collective-permute-start(f32[192,3072]{1,0:T(8,128)} %pad_maximum_fusion), channel_id=1, source_target_pairs={{0,1},{1,0},{2,3},{3,2},{4,5},{5,4},{6,7},{7,6},{8,9},{9,8},{10,11... | collective-permute-start | bytes 7077896 | tf_op jit(solution)/shard_map/ppermute | solution.py:141
  101.2 1.4 copy-start.1
  102.7 12.0 %collective-permute-start.3 = (s16[96,3200]{1,0:T(8,128)(2,1)S(1)}, s16[96,3200]{1,0:T(8,128)(2,1)S(1)}, u32[]{:S(2)}, u32[]{:S(2)}) collective-permute-start(s16[96,3200]{1,0:T(8,128)(2,1)S(1)} %pad_add_fusion), channel_id=1, source_target_pairs={{0,2},{1,5},{2,0},{3,7},{4,6},{5,1},{6,4},{7,3},{8,10},{9,13},{10,... | collective-permute-start | bytes 1843208 | tf_op jit(solution)/shard_map/ppermute | solution.py:149
  114.7 0.9 copy-start.8
  118.5 8.9 %collective-permute-start.4 = (s16[48,3200]{1,0:T(8,128)(2,1)}, s16[48,3200]{1,0:T(8,128)(2,1)S(1)}, u32[]{:S(2)}, u32[]{:S(2)}) collective-permute-start(s16[48,3200]{1,0:T(8,128)(2,1)} %pad_add_fusion.1), channel_id=1, source_target_pairs={{0,4},{1,3},{2,6},{3,1},{4,0},{5,7},{6,2},{7,5},{8,12},{9,11},{10,... | collective-permute-start | bytes 921608 | tf_op jit(solution)/shard_map/ppermute | solution.py:149
  120.4 7.3 %collective-permute-start.5 = (bf16[48,2048]{1,0:T(8,128)(2,1)}, bf16[48,2048]{1,0:T(8,128)(2,1)S(1)}, u32[]{:S(2)}, u32[]{:S(2)}) collective-permute-start(bf16[48,2048]{1,0:T(8,128)(2,1)} %bitcast.22), channel_id=1, source_target_pairs={{0,0},{1,4},{2,2},{3,6},{4,1},{5,3},{6,5},{7,7},{8,8},{9,12},{10,1... | collective-permute-start | bytes 589832 | tf_op jit(solution)/shard_map/ppermute | solution.py:107
  127.9 24.7 %copy-start.3 = (bf16[1,1,1024,448]{2,3,1,0:T(8,128)(2,1)S(1)}, bf16[1,1,1024,448]{2,3,1,0:T(8,128)(2,1)}, u32[]{:S(2)}) copy-start(bf16[1,1,1024,448]{2,3,1,0:T(8,128)(2,1)} %param.16) | copy-start | bytes 2752516
  127.9 8.7 %collective-permute-start.6 = (bf16[48,3072]{1,0:T(8,128)(2,1)S(1)}, bf16[48,3072]{1,0:T(8,128)(2,1)S(1)}, u32[]{:S(2)}, u32[]{:S(2)}) collective-permute-start(bf16[48,3072]{1,0:T(8,128)(2,1)S(1)} %pad_maximum_fusion.3), channel_id=1, source_target_pairs={{0,4},{1,3},{2,6},{3,1},{4,0},{5,7},{6,2},{7,5},{8,12},{9,11},{10,... | collective-permute-start | bytes 884744 | tf_op jit(solution)/shard_map/ppermute | solution.py:167
  136.7 12.1 %collective-permute-start.7 = (bf16[96,3072]{1,0:T(8,128)(2,1)S(1)}, bf16[96,3072]{1,0:T(8,128)(2,1)S(1)}, u32[]{:S(2)}, u32[]{:S(2)}) collective-permute-start(bf16[96,3072]{1,0:T(8,128)(2,1)S(1)} %pad_maximum_fusion.2), channel_id=1, source_target_pairs={{0,2},{1,5},{2,0},{3,7},{4,6},{5,1},{6,4},{7,3},{8,10},{9,13},{10,... | collective-permute-start | bytes 1769480 | tf_op jit(solution)/shard_map/ppermute | solution.py:167
  150.0 5.9 %collective-permute-start.8 = (bf16[192,3072]{1,0:T(8,128)(2,1)}, bf16[192,3072]{1,0:T(8,128)(2,1)}, u32[]{:S(2)}, u32[]{:S(2)}) collective-permute-start(bf16[192,3072]{1,0:T(8,128)(2,1)} %pad_maximum_fusion.1), channel_id=1, source_target_pairs={{0,1},{1,0},{2,3},{3,2},{4,5},{5,4},{6,7},{7,6},{8,9},{9,8},{10,11... | collective-permute-start | bytes 3538952 | tf_op jit(solution)/shard_map/ppermute | solution.py:180
  160.7 7.7 %copy-start.9 = (f32[1,32,1]{1,2,0:T(1,128)S(1)}, f32[1,32,1]{1,2,0:T(1,128)}, u32[]{:S(2)}) copy-start(f32[1,32,1]{1,2,0:T(1,128)} %param.14) | copy-start | bytes 388
  160.7 7.7 %copy-start.10 = (f32[1,32,1]{1,2,0:T(1,128)S(1)}, f32[1,32,1]{1,2,0:T(1,128)}, u32[]{:S(2)}) copy-start(f32[1,32,1]{1,2,0:T(1,128)} %param.11) | copy-start | bytes 388
  162.4 50.9 %all-to-all-start.1 = ((bf16[64,2,6,448]{3,1,2,0:T(2,128)(2,1)}), bf16[64,2,6,448]{3,1,2,0:T(2,128)(2,1)S(1)}, u32[]{:S(2)}, u32[]{:S(2)}) async-start(bf16[64,2,6,448]{3,1,2,0:T(2,128)(2,1)} %fusion.32), calls=%async_computation.1 | async-start | bytes 1572864 | tf_op jit(solution)/shard_map/all_to_all | solution.py:200
  214.4 2.0 copy-start.5
  214.4 2.0 copy-start.7

commit v8 on v7

--- a/solution.py
+++ b/solution.py
@@ -122,6 +122,7 @@
         "prjt,pthc->rhpjc", dispatch, token_parts, preferred_element_type=jnp.float32
     ).astype(jnp.bfloat16)
     sent = sent.reshape(devices, 2, MOST, share_width)
+    saved, sent = lax.optimization_barrier((saved, sent))
     got = lax.all_to_all(sent, "expert", split_axis=0, concat_axis=0, tiled=True)
     rows_down = got[:, 0].reshape(-1, share_width)
     rows_up = got[:, 1].reshape(-1, share_width)

time: 219 us -> 219 us (level)
  starting transfers between devices: 50.9 us -> 46.8 us
  waiting for transfers between devices: 128 us -> 131 us
    ppermute x2, starting transfers between devices: 8.2 us -> 4.49 us  [body(): lax.ppermute(current, 'expert', stage_route(devices, group_size, stage))]
    ppermute x2, waiting for transfers between devices: 12.6 us -> 16 us  [body(): lax.ppermute(current, 'expert', stage_route(devices, group_size, stage))]
where the time goes in v8:
time: 219 us; the launch traced here: 218 us
  waiting for transfers between devices  131 us (60%)
  starting transfers between devices  46.8 us (21%)
  local copies, waits for them, and re-layouts  16.3 us (7%)
  other arithmetic  12.5 us (6%)
  matrix products  9.84 us (4%)
    all_to_all x1, waiting for transfers between devices, body(): lax.all_to_all(result, 'expert', split_axis=0, concat_axis=0, tiled=True)  44.9 us
    all_to_all x1, waiting for transfers between devices, body(): lax.all_to_all(sent, 'expert', split_axis=0, concat_axis=0, tiled=True)  44.8 us
    all_to_all x1, starting transfers between devices, body(): lax.all_to_all(sent, 'expert', split_axis=0, concat_axis=0, tiled=True)  18.2 us
    ppermute x2, waiting for transfers between devices, body(): lax.ppermute(encode_rows(send_part, 128), 'expert', stage_route(devices,...  16.6 us
    ppermute x2, waiting for transfers between devices, body(): lax.ppermute(current, 'expert', stage_route(devices, group_size, stage))  16 us
    ppermute x2, starting transfers between devices, shifted(): return lax.ppermute(block, axis, route)  9.59 us
    ppermute x2, waiting for transfers between devices, shifted(): return lax.ppermute(block, axis, route)  4.93 us
    all_to_all x1, starting transfers between devices, body(): lax.all_to_all(result, 'expert', split_axis=0, concat_axis=0, tiled=True)  4.61 us
  transfers between devices with their start and end apart: 11, of which 9 were waited for; matrix products, arithmetic and copies ran while one was open for 3% of the time, Pallas kernels for 0%

profile of v8, /device:TPU:8, one launch (start us, length us, event | category | flops | bytes accessed | tf_op | source)
XLA Modules:
  0.0 217.8 jit_solution(16363951580243025948)
XLA Ops:
  0.6 4.3 %collective-permute-start = (bf16[32,3584]{1,0:T(8,128)(2,1)}, bf16[32,3584]{1,0:T(8,128)(2,1)S(1)}, u32[]{:S(2)}, u32[]{:S(2)}) collective-permute-start(bf16[32,3584]{1,0:T(8,128)(2,1)} %bitcast.102), channel_id=1, source_target_pairs={{448,0},{0,64},{64,128},{128,192},{192,256},{256,320},{320,384},{3... | collective-permute-start | bytes 688136 | tf_op jit(solution)/shard_map/ppermute | solution.py:14
  5.0 5.3 %collective-permute-start.1 = (bf16[32,3584]{1,0:T(8,128)(2,1)}, bf16[32,3584]{1,0:T(8,128)(2,1)S(1)}, u32[]{:S(2)}, u32[]{:S(2)}) collective-permute-start(bf16[32,3584]{1,0:T(8,128)(2,1)} %bitcast.103), channel_id=1, source_target_pairs={{64,0},{128,64},{192,128},{256,192},{320,256},{384,320},{448,384},... | collective-permute-start | bytes 688136 | tf_op jit(solution)/shard_map/ppermute | solution.py:14
  10.2 1.6 collective-permute-start.2
  11.8 0.7 pad_add_fusion.2
  12.5 0.2 convert_reduce_fusion
  12.7 1.2 collective-permute-done
  13.9 0.7 copy-done.4
  14.6 0.3 stack.97
  15.0 3.7 %collective-permute-done.1 = bf16[32,3584]{1,0:T(8,128)(2,1)S(1)} collective-permute-done((bf16[32,3584]{1,0:T(8,128)(2,1)}, bf16[32,3584]{1,0:T(8,128)(2,1)S(1)}, u32[]{:S(2)}, u32[]{:S(2)}) %collective-permute-start.1) | collective-permute-done | bytes 229408 | tf_op jit(solution)/shard_map/ppermute | solution.py:14
  18.8 0.3 stack.98
  19.2 0.4 fusion.8
  19.6 0.4 copy.62
  20.1 1.7 copy.47
  21.7 18.2 %all-to-all-start = ((bf16[64,2,6,448]{3,1,2,0:T(2,128)(2,1)}), bf16[64,2,6,448]{3,1,2,0:T(2,128)(2,1)S(1)}, u32[]{:S(2)}, u32[]{:S(2)}) async-start(bf16[64,2,6,448]{3,1,2,0:T(2,128)(2,1)} %copy.47), calls=%async_computation | async-start | bytes 1572864 | tf_op jit(solution)/shard_map/all_to_all | solution.py:126
  40.0 44.8 %all-to-all-done = bf16[64,2,6,448]{3,1,2,0:T(2,128)(2,1)S(1)} async-done(((bf16[64,2,6,448]{3,1,2,0:T(2,128)(2,1)}), bf16[64,2,6,448]{3,1,2,0:T(2,128)(2,1)S(1)}, u32[]{:S(2)}, u32[]{:S(2)}) %all-to-all-start) | async-done | bytes 688160 | tf_op jit(solution)/shard_map/all_to_all | solution.py:126
  84.8 4.2 %slice_reduce_fusion.1 = (bf16[64,6,448]{2,1,0:T(8,128)(2,1)}, bf16[64,6,448]{2,1,0:T(8,128)(2,1)S(1)}) fusion(bf16[64,2,6,448]{3,1,2,0:T(2,128)(2,1)S(1)} %all-to-all-done), kind=kLoop, calls=%fused_computation.37 | loop fusion | bytes 1376256 | tf_op jit(solution)/shard_map/slice | solution.py:127
  89.0 1.3 reshape_squeeze.6
  90.3 0.2 reshape_squeeze.7
  90.6 0.6 fusion.4
  91.2 0.6 copy-done.2
  91.7 0.4 fusion.25
  92.1 1.6 pad_maximum_fusion
  93.7 1.9 collective-permute-start.3
  95.6 0.4 fusion.27
  96.0 0.6 fusion.6
  96.6 3.9 %collective-permute-done.3 = f32[192,3072]{1,0:T(8,128)} collective-permute-done((f32[192,3072]{1,0:T(8,128)}, f32[192,3072]{1,0:T(8,128)}, u32[]{:S(2)}, u32[]{:S(2)}) %collective-permute-start.3) | collective-permute-done | bytes 2359328 | tf_op jit(solution)/shard_map/ppermute | solution.py:142
  100.4 1.9 maximum_add_fusion
  102.4 0.2 abs_reduce_fusion
  102.6 0.3 round-nearest-even_convert_fusion
  103.0 0.8 copy-done.1
  103.8 2.4 %collective-permute-start.4 = (s16[96,3200]{1,0:T(8,128)(2,1)S(1)}, s16[96,3200]{1,0:T(8,128)(2,1)S(1)}, u32[]{:S(2)}, u32[]{:S(2)}) collective-permute-start(s16[96,3200]{1,0:T(8,128)(2,1)S(1)} %pad_add_fusion), channel_id=1, source_target_pairs={{0,2},{1,5},{2,0},{3,7},{4,6},{5,1},{6,4},{7,3},{8,10},{9,13},{10,... | collective-permute-start | bytes 1843208 | tf_op jit(solution)/shard_map/ppermute | solution.py:150
  106.2 9.6 %collective-permute-done.4 = s16[96,3200]{1,0:T(8,128)(2,1)S(1)} collective-permute-done((s16[96,3200]{1,0:T(8,128)(2,1)S(1)}, s16[96,3200]{1,0:T(8,128)(2,1)S(1)}, u32[]{:S(2)}, u32[]{:S(2)}) %collective-permute-start.4) | collective-permute-done | bytes 614432 | tf_op jit(solution)/shard_map/ppermute | solution.py:150
  115.8 0.8 copy-done.8
  116.6 0.1 exponential_reduce_fusion
  116.8 1.7 multiply_add_fusion
  118.4 0.1 abs_reduce_fusion.1
  118.6 0.2 round-nearest-even_convert_fusion.1
  118.9 0.7 pad_add_fusion.1
  119.6 1.9 collective-permute-start.5
  121.5 7.0 %collective-permute-done.5 = s16[48,3200]{1,0:T(8,128)(2,1)S(1)} collective-permute-done((s16[48,3200]{1,0:T(8,128)(2,1)}, s16[48,3200]{1,0:T(8,128)(2,1)S(1)}, u32[]{:S(2)}, u32[]{:S(2)}) %collective-permute-start.5) | collective-permute-done | bytes 307232 | tf_op jit(solution)/shard_map/ppermute | solution.py:150
  128.6 0.1 exponential_reduce_fusion.1
  128.7 0.1 multiply_add_fusion.1
  128.8 0.2 fusion.42
  129.0 2.1 collective-permute-start.6
  131.1 6.7 %collective-permute-done.6 = bf16[48,3072]{1,0:T(8,128)(2,1)S(1)} collective-permute-done((bf16[48,3072]{1,0:T(8,128)(2,1)S(1)}, bf16[48,3072]{1,0:T(8,128)(2,1)S(1)}, u32[]{:S(2)}, u32[]{:S(2)}) %collective-permute-start.6) | collective-permute-done | bytes 294944 | tf_op jit(solution)/shard_map/ppermute | solution.py:168
  137.8 2.4 %collective-permute-start.7 = (bf16[96,3072]{1,0:T(8,128)(2,1)S(1)}, bf16[96,3072]{1,0:T(8,128)(2,1)S(1)}, u32[]{:S(2)}, u32[]{:S(2)}) collective-permute-start(bf16[96,3072]{1,0:T(8,128)(2,1)S(1)} %pad_maximum_fusion.2), channel_id=1, source_target_pairs={{0,2},{1,5},{2,0},{3,7},{4,6},{5,1},{6,4},{7,3},{8,10},{9,13},{10,... | collective-permute-start | bytes 1769480 | tf_op jit(solution)/shard_map/ppermute | solution.py:168
  140.3 9.3 %collective-permute-done.7 = bf16[96,3072]{1,0:T(8,128)(2,1)S(1)} collective-permute-done((bf16[96,3072]{1,0:T(8,128)(2,1)S(1)}, bf16[96,3072]{1,0:T(8,128)(2,1)S(1)}, u32[]{:S(2)}, u32[]{:S(2)}) %collective-permute-start.7) | collective-permute-done | bytes 589856 | tf_op jit(solution)/shard_map/ppermute | solution.py:168
  149.6 1.1 pad_maximum_fusion.1
  150.7 2.1 collective-permute-start.8
  153.1 0.1 stack.115
  153.3 1.4 fusion.21
  154.7 1.8 fusion.18
  156.5 1.8 fusion.15
  158.3 1.4 fusion.22
  159.9 0.6 gather_fusion
  160.5 0.8 copy.48
  161.3 1.7 fusion.32
  163.0 4.6 %all-to-all-start.1 = ((bf16[64,2,6,448]{3,1,2,0:T(2,128)(2,1)}), bf16[64,2,6,448]{3,1,2,0:T(2,128)(2,1)S(1)}, u32[]{:S(2)}, u32[]{:S(2)}) async-start(bf16[64,2,6,448]{3,1,2,0:T(2,128)(2,1)} %fusion.32), calls=%async_computation.1 | async-start | bytes 1572864 | tf_op jit(solution)/shard_map/all_to_all | solution.py:201
  167.7 44.9 %all-to-all-done.1 = bf16[64,2,6,448]{3,1,2,0:T(2,128)(2,1)S(1)} async-done(((bf16[64,2,6,448]{3,1,2,0:T(2,128)(2,1)}), bf16[64,2,6,448]{3,1,2,0:T(2,128)(2,1)S(1)}, u32[]{:S(2)}, u32[]{:S(2)}) %all-to-all-start.1) | async-done | bytes 688160 | tf_op jit(solution)/shard_map/all_to_all | solution.py:201
  212.6 1.1 convolution_bitcast_fusion
  213.7 0.6 copy.51
  214.3 1.3 reshape.465
  215.6 1.4 add_convert_fusion
  217.0 0.8 fusion.66
  (44 shorter events, 0.9 us)
Async XLA Ops:
  0.6 89.9 %copy-start = (bf16[1,1,448,2048]{3,2,1,0:T(8,128)(2,1)S(1)}, bf16[1,1,448,2048]{3,2,1,0:T(8,128)(2,1)}, u32[]{:S(2)}) copy-start(bf16[1,1,448,2048]{3,2,1,0:T(8,128)(2,1)} %param.15) | copy-start | bytes 5505028
  0.6 13.3 %collective-permute-start = (bf16[32,3584]{1,0:T(8,128)(2,1)}, bf16[32,3584]{1,0:T(8,128)(2,1)S(1)}, u32[]{:S(2)}, u32[]{:S(2)}) collective-permute-start(bf16[32,3584]{1,0:T(8,128)(2,1)} %bitcast.102), channel_id=1, source_target_pairs={{448,0},{0,64},{64,128},{128,192},{192,256},{256,320},{320,384},{3... | collective-permute-start | bytes 688136 | tf_op jit(solution)/shard_map/ppermute | solution.py:14
  5.0 13.8 %collective-permute-start.1 = (bf16[32,3584]{1,0:T(8,128)(2,1)}, bf16[32,3584]{1,0:T(8,128)(2,1)S(1)}, u32[]{:S(2)}, u32[]{:S(2)}) collective-permute-start(bf16[32,3584]{1,0:T(8,128)(2,1)} %bitcast.103), channel_id=1, source_target_pairs={{64,0},{128,64},{192,128},{256,192},{320,256},{384,320},{448,384},... | collective-permute-start | bytes 688136 | tf_op jit(solution)/shard_map/ppermute | solution.py:14
  10.2 9.8 %collective-permute-start.2 = (bf16[48,2048]{1,0:T(8,128)(2,1)}, bf16[48,2048]{1,0:T(8,128)(2,1)S(1)}, u32[]{:S(2)}, u32[]{:S(2)}) collective-permute-start(bf16[48,2048]{1,0:T(8,128)(2,1)} %bitcast.104), channel_id=1, source_target_pairs={{0,0},{1,4},{2,2},{3,6},{4,1},{5,3},{6,5},{7,7},{8,8},{9,12},{10,1... | collective-permute-start | bytes 589832 | tf_op jit(solution)/shard_map/ppermute | solution.py:107
  13.9 0.7 copy-start.4
  18.8 1.3 copy-start.6
  20.0 1.7 copy-start.9
  21.7 63.1 %all-to-all-start = ((bf16[64,2,6,448]{3,1,2,0:T(2,128)(2,1)}), bf16[64,2,6,448]{3,1,2,0:T(2,128)(2,1)S(1)}, u32[]{:S(2)}, u32[]{:S(2)}) async-start(bf16[64,2,6,448]{3,1,2,0:T(2,128)(2,1)} %copy.47), calls=%async_computation | async-start | bytes 1572864 | tf_op jit(solution)/shard_map/all_to_all | solution.py:126
  90.6 1.2 copy-start.2
  93.7 6.8 %collective-permute-start.3 = (f32[192,3072]{1,0:T(8,128)}, f32[192,3072]{1,0:T(8,128)}, u32[]{:S(2)}, u32[]{:S(2)}) collective-permute-start(f32[192,3072]{1,0:T(8,128)} %pad_maximum_fusion), channel_id=1, source_target_pairs={{0,1},{1,0},{2,3},{3,2},{4,5},{5,4},{6,7},{7,6},{8,9},{9,8},{10,11... | collective-permute-start | bytes 7077896 | tf_op jit(solution)/shard_map/ppermute | solution.py:142
  102.4 1.4 copy-start.1
  103.8 12.0 %collective-permute-start.4 = (s16[96,3200]{1,0:T(8,128)(2,1)S(1)}, s16[96,3200]{1,0:T(8,128)(2,1)S(1)}, u32[]{:S(2)}, u32[]{:S(2)}) collective-permute-start(s16[96,3200]{1,0:T(8,128)(2,1)S(1)} %pad_add_fusion), channel_id=1, source_target_pairs={{0,2},{1,5},{2,0},{3,7},{4,6},{5,1},{6,4},{7,3},{8,10},{9,13},{10,... | collective-permute-start | bytes 1843208 | tf_op jit(solution)/shard_map/ppermute | solution.py:150
  115.8 0.8 copy-start.8
  118.6 10.2 %copy-start.10 = (bf16[48,2048]{1,0:T(8,128)(2,1)S(1)}, bf16[48,2048]{1,0:T(8,128)(2,1)}, u32[]{:S(2)}) copy-start(bf16[48,2048]{1,0:T(8,128)(2,1)} %copy-done.9) | copy-start | bytes 589828
  119.6 8.9 %collective-permute-start.5 = (s16[48,3200]{1,0:T(8,128)(2,1)}, s16[48,3200]{1,0:T(8,128)(2,1)S(1)}, u32[]{:S(2)}, u32[]{:S(2)}) collective-permute-start(s16[48,3200]{1,0:T(8,128)(2,1)} %pad_add_fusion.1), channel_id=1, source_target_pairs={{0,4},{1,3},{2,6},{3,1},{4,0},{5,7},{6,2},{7,5},{8,12},{9,11},{10,... | collective-permute-start | bytes 921608 | tf_op jit(solution)/shard_map/ppermute | solution.py:150
  129.0 24.2 %copy-start.3 = (bf16[1,1,1024,448]{2,3,1,0:T(8,128)(2,1)S(1)}, bf16[1,1,1024,448]{2,3,1,0:T(8,128)(2,1)}, u32[]{:S(2)}) copy-start(bf16[1,1,1024,448]{2,3,1,0:T(8,128)(2,1)} %param.16) | copy-start | bytes 2752516
  129.0 8.7 %collective-permute-start.6 = (bf16[48,3072]{1,0:T(8,128)(2,1)S(1)}, bf16[48,3072]{1,0:T(8,128)(2,1)S(1)}, u32[]{:S(2)}, u32[]{:S(2)}) collective-permute-start(bf16[48,3072]{1,0:T(8,128)(2,1)S(1)} %pad_maximum_fusion.3), channel_id=1, source_target_pairs={{0,4},{1,3},{2,6},{3,1},{4,0},{5,7},{6,2},{7,5},{8,12},{9,11},{10,... | collective-permute-start | bytes 884744 | tf_op jit(solution)/shard_map/ppermute | solution.py:168
  137.8 11.8 %collective-permute-start.7 = (bf16[96,3072]{1,0:T(8,128)(2,1)S(1)}, bf16[96,3072]{1,0:T(8,128)(2,1)S(1)}, u32[]{:S(2)}, u32[]{:S(2)}) collective-permute-start(bf16[96,3072]{1,0:T(8,128)(2,1)S(1)} %pad_maximum_fusion.2), channel_id=1, source_target_pairs={{0,2},{1,5},{2,0},{3,7},{4,6},{5,1},{6,4},{7,3},{8,10},{9,13},{10,... | collective-permute-start | bytes 1769480 | tf_op jit(solution)/shard_map/ppermute | solution.py:168
  150.7 5.8 %collective-permute-start.8 = (bf16[192,3072]{1,0:T(8,128)(2,1)}, bf16[192,3072]{1,0:T(8,128)(2,1)}, u32[]{:S(2)}, u32[]{:S(2)}) collective-permute-start(bf16[192,3072]{1,0:T(8,128)(2,1)} %pad_maximum_fusion.1), channel_id=1, source_target_pairs={{0,1},{1,0},{2,3},{3,2},{4,5},{5,4},{6,7},{7,6},{8,9},{9,8},{10,11... | collective-permute-start | bytes 3538952 | tf_op jit(solution)/shard_map/ppermute | solution.py:181
  161.3 6.3 %copy-start.11 = (f32[1,32,1]{1,2,0:T(1,128)S(1)}, f32[1,32,1]{1,2,0:T(1,128)}, u32[]{:S(2)}) copy-start(f32[1,32,1]{1,2,0:T(1,128)} %param.14) | copy-start | bytes 388
  161.3 6.3 %copy-start.12 = (f32[1,32,1]{1,2,0:T(1,128)S(1)}, f32[1,32,1]{1,2,0:T(1,128)}, u32[]{:S(2)}) copy-start(f32[1,32,1]{1,2,0:T(1,128)} %param.11) | copy-start | bytes 388
  163.0 49.6 %all-to-all-start.1 = ((bf16[64,2,6,448]{3,1,2,0:T(2,128)(2,1)}), bf16[64,2,6,448]{3,1,2,0:T(2,128)(2,1)S(1)}, u32[]{:S(2)}, u32[]{:S(2)}) async-start(bf16[64,2,6,448]{3,1,2,0:T(2,128)(2,1)} %fusion.32), calls=%async_computation.1 | async-start | bytes 1572864 | tf_op jit(solution)/shard_map/all_to_all | solution.py:201
  213.6 2.0 copy-start.5
  213.6 2.0 copy-start.7

commit v9 on v8

--- a/solution.py
+++ b/solution.py
@@ -66,16 +66,20 @@
 
 
 def encode_rows(values, lanes):
-    largest = jnp.maximum(jnp.max(jnp.abs(values), axis=1, keepdims=True), 1e-30)
+    rows, width = values.shape
+    groups = values.reshape(rows, width // lanes, lanes)
+    largest = jnp.maximum(jnp.max(jnp.abs(groups), axis=2, keepdims=True), 1e-30)
     exponent = jnp.floor(jnp.log2(largest)) - 13.0
-    coded = jnp.round(values * jnp.exp2(-exponent)).astype(jnp.int16)
-    tail = jnp.broadcast_to(exponent.astype(jnp.int16), (values.shape[0], lanes))
+    coded = jnp.round(groups * jnp.exp2(-exponent)).astype(jnp.int16).reshape(rows, width)
+    tail = jnp.pad(exponent[:, :, 0].astype(jnp.int16), ((0, 0), (0, lanes - width // lanes)))
     return jnp.concatenate([coded, tail], axis=1)
 
 
-def decode_rows(coded, width):
-    exponent = coded[:, width : width + 1].astype(jnp.float32)
-    return coded[:, :width].astype(jnp.float32) * jnp.exp2(exponent)
+def decode_rows(coded, width, lanes):
+    rows = coded.shape[0]
+    exponent = coded[:, width : width + width // lanes].astype(jnp.float32)
+    groups = coded[:, :width].astype(jnp.float32).reshape(rows, width // lanes, lanes)
+    return (groups * jnp.exp2(exponent)[:, :, None]).reshape(rows, width)
 
 
 def body(
@@ -150,7 +154,7 @@
         received = lax.ppermute(
             encode_rows(send_part, 128), "expert", stage_route(devices, group_size, stage)
         )
-        current = kept + decode_rows(received, width)
+        current = kept + decode_rows(received, width, 128)
 
     pre_share = current[:, : 2 * hidden_units]
     hidden_grad = current[:, 2 * hidden_units :]

time: 219 us -> 225 us (1.027)
  other arithmetic: 12.5 us -> 15.3 us
  local copies, waits for them, and re-layouts: 16.3 us -> 18.7 us
where the time goes in v9:
time: 225 us; the launch traced here: 224 us
  waiting for transfers between devices  131 us (58%)
  starting transfers between devices  47 us (21%)
  local copies, waits for them, and re-layouts  18.7 us (8%)
  other arithmetic  15.3 us (7%)
  matrix products  10.9 us (5%)
    all_to_all x1, waiting for transfers between devices, body(): lax.all_to_all(result, 'expert', split_axis=0, concat_axis=0, tiled=True)  44.9 us
    all_to_all x1, waiting for transfers between devices, body(): lax.all_to_all(sent, 'expert', split_axis=0, concat_axis=0, tiled=True)  44.8 us
    all_to_all x1, starting transfers between devices, body(): lax.all_to_all(sent, 'expert', split_axis=0, concat_axis=0, tiled=True)  18.2 us
    ppermute x2, waiting for transfers between devices, body(): lax.ppermute(encode_rows(send_part, 128), 'expert', stage_route(devices,...  16.4 us
    ppermute x2, waiting for transfers between devices, body(): lax.ppermute(current, 'expert', stage_route(devices, group_size, stage))  16 us
    ppermute x2, starting transfers between devices, shifted(): return lax.ppermute(block, axis, route)  9.59 us
    ppermute x2, waiting for transfers between devices, shifted(): return lax.ppermute(block, axis, route)  4.93 us
    all_to_all x1, starting transfers between devices, body(): lax.all_to_all(result, 'expert', split_axis=0, concat_axis=0, tiled=True)  4.61 us
  transfers between devices with their start and end apart: 11, of which 9 were waited for; matrix products, arithmetic and copies ran while one was open for 3% of the time, Pallas kernels for 0%

profile of v9, /device:TPU:8, one launch (start us, length us, event | category | flops | bytes accessed | tf_op | source)
XLA Modules:
  0.0 224.1 jit_solution(14206781365870972917)
XLA Ops:
  0.6 4.3 %collective-permute-start = (bf16[32,3584]{1,0:T(8,128)(2,1)}, bf16[32,3584]{1,0:T(8,128)(2,1)S(1)}, u32[]{:S(2)}, u32[]{:S(2)}) collective-permute-start(bf16[32,3584]{1,0:T(8,128)(2,1)} %bitcast.138), channel_id=1, source_target_pairs={{448,0},{0,64},{64,128},{128,192},{192,256},{256,320},{320,384},{3... | collective-permute-start | bytes 688136 | tf_op jit(solution)/shard_map/ppermute | solution.py:14
  5.0 5.3 %collective-permute-start.1 = (bf16[32,3584]{1,0:T(8,128)(2,1)}, bf16[32,3584]{1,0:T(8,128)(2,1)S(1)}, u32[]{:S(2)}, u32[]{:S(2)}) collective-permute-start(bf16[32,3584]{1,0:T(8,128)(2,1)} %bitcast.139), channel_id=1, source_target_pairs={{64,0},{128,64},{192,128},{256,192},{320,256},{384,320},{448,384},... | collective-permute-start | bytes 688136 | tf_op jit(solution)/shard_map/ppermute | solution.py:14
  10.2 1.6 collective-permute-start.2
  11.8 0.7 pad_add_fusion.2
  12.5 0.2 convert_reduce_fusion
  12.7 1.2 collective-permute-done
  13.9 0.7 copy-done.5
  14.6 0.3 stack.97
  15.0 3.7 %collective-permute-done.1 = bf16[32,3584]{1,0:T(8,128)(2,1)S(1)} collective-permute-done((bf16[32,3584]{1,0:T(8,128)(2,1)}, bf16[32,3584]{1,0:T(8,128)(2,1)S(1)}, u32[]{:S(2)}, u32[]{:S(2)}) %collective-permute-start.1) | collective-permute-done | bytes 229408 | tf_op jit(solution)/shard_map/ppermute | solution.py:14
  18.8 0.3 stack.98
  19.2 0.4 fusion.8
  19.6 0.4 copy.112
  20.1 1.7 copy.80
  21.8 18.2 %all-to-all-start = ((bf16[64,2,6,448]{3,1,2,0:T(2,128)(2,1)}), bf16[64,2,6,448]{3,1,2,0:T(2,128)(2,1)S(1)}, u32[]{:S(2)}, u32[]{:S(2)}) async-start(bf16[64,2,6,448]{3,1,2,0:T(2,128)(2,1)} %copy.80), calls=%async_computation | async-start | bytes 1572864 | tf_op jit(solution)/shard_map/all_to_all | solution.py:130
  40.0 44.8 %all-to-all-done = bf16[64,2,6,448]{3,1,2,0:T(2,128)(2,1)S(1)} async-done(((bf16[64,2,6,448]{3,1,2,0:T(2,128)(2,1)}), bf16[64,2,6,448]{3,1,2,0:T(2,128)(2,1)S(1)}, u32[]{:S(2)}, u32[]{:S(2)}) %all-to-all-start) | async-done | bytes 688160 | tf_op jit(solution)/shard_map/all_to_all | solution.py:130
  84.9 4.2 %slice_reduce_fusion.1 = (bf16[64,6,448]{2,1,0:T(8,128)(2,1)}, bf16[64,6,448]{2,1,0:T(8,128)(2,1)S(1)}) fusion(bf16[64,2,6,448]{3,1,2,0:T(2,128)(2,1)S(1)} %all-to-all-done), kind=kLoop, calls=%fused_computation.40 | loop fusion | bytes 1376256 | tf_op jit(solution)/shard_map/slice | solution.py:131
  89.0 2.0 reshape_squeeze.6
  91.1 0.2 reshape_squeeze.7
  91.3 1.6 fusion.4
  92.9 0.4 fusion.28
  93.3 1.6 pad_maximum_fusion
  94.9 2.0 collective-permute-start.3
  97.0 0.4 fusion.30
  97.3 0.6 fusion.6
  97.9 3.9 %collective-permute-done.3 = f32[192,3072]{1,0:T(8,128)} collective-permute-done((f32[192,3072]{1,0:T(8,128)}, f32[192,3072]{1,0:T(8,128)}, u32[]{:S(2)}, u32[]{:S(2)}) %collective-permute-start.3) | collective-permute-done | bytes 2359328 | tf_op jit(solution)/shard_map/ppermute | solution.py:146
  101.8 1.9 maximum_add_fusion
  103.8 0.2 copy.99
  104.1 1.1 copy-done.1
  105.1 0.4 reduce_max.18
  105.7 0.4 mul.152
  106.1 1.6 fusion.11
  107.9 2.6 %collective-permute-start.4 = (s16[96,3200]{1,0:T(8,128)(2,1)S(1)}, s16[96,3200]{1,0:T(8,128)(2,1)S(1)}, u32[]{:S(2)}, u32[]{:S(2)}) collective-permute-start(s16[96,3200]{1,0:T(8,128)(2,1)S(1)} %pad_add_fusion), channel_id=1, source_target_pairs={{0,2},{1,5},{2,0},{3,7},{4,6},{5,1},{6,4},{7,3},{8,10},{9,13},{10,... | collective-permute-start | bytes 1843208 | tf_op jit(solution)/shard_map/ppermute | solution.py:154
  110.5 9.4 %collective-permute-done.4 = s16[96,3200]{1,0:T(8,128)(2,1)S(1)} collective-permute-done((s16[96,3200]{1,0:T(8,128)(2,1)S(1)}, s16[96,3200]{1,0:T(8,128)(2,1)S(1)}, u32[]{:S(2)}, u32[]{:S(2)}) %collective-permute-start.4) | collective-permute-done | bytes 614432 | tf_op jit(solution)/shard_map/ppermute | solution.py:154
  120.1 0.4 mul.155
  120.5 0.3 copy-done.9
  120.7 1.8 fusion.9
  122.6 0.9 copy.102
  123.5 1.3 reduce_max.19
  124.8 0.2 mul.160
  125.0 0.2 fusion.38
  125.2 0.7 pad_add_fusion.1
  126.0 1.9 collective-permute-start.5
  127.9 7.0 %collective-permute-done.5 = s16[48,3200]{1,0:T(8,128)(2,1)S(1)} collective-permute-done((s16[48,3200]{1,0:T(8,128)(2,1)}, s16[48,3200]{1,0:T(8,128)(2,1)S(1)}, u32[]{:S(2)}, u32[]{:S(2)}) %collective-permute-start.5) | collective-permute-done | bytes 307232 | tf_op jit(solution)/shard_map/ppermute | solution.py:154
  134.9 0.2 mul.163
  135.5 2.1 collective-permute-start.6
  137.6 6.7 %collective-permute-done.6 = bf16[48,3072]{1,0:T(8,128)(2,1)S(1)} collective-permute-done((bf16[48,3072]{1,0:T(8,128)(2,1)S(1)}, bf16[48,3072]{1,0:T(8,128)(2,1)S(1)}, u32[]{:S(2)}, u32[]{:S(2)}) %collective-permute-start.6) | collective-permute-done | bytes 294944 | tf_op jit(solution)/shard_map/ppermute | solution.py:172
  144.3 2.4 %collective-permute-start.7 = (bf16[96,3072]{1,0:T(8,128)(2,1)S(1)}, bf16[96,3072]{1,0:T(8,128)(2,1)S(1)}, u32[]{:S(2)}, u32[]{:S(2)}) collective-permute-start(bf16[96,3072]{1,0:T(8,128)(2,1)S(1)} %pad_maximum_fusion.2), channel_id=1, source_target_pairs={{0,2},{1,5},{2,0},{3,7},{4,6},{5,1},{6,4},{7,3},{8,10},{9,13},{10,... | collective-permute-start | bytes 1769480 | tf_op jit(solution)/shard_map/ppermute | solution.py:172
  146.8 9.3 %collective-permute-done.7 = bf16[96,3072]{1,0:T(8,128)(2,1)S(1)} collective-permute-done((bf16[96,3072]{1,0:T(8,128)(2,1)S(1)}, bf16[96,3072]{1,0:T(8,128)(2,1)S(1)}, u32[]{:S(2)}, u32[]{:S(2)}) %collective-permute-start.7) | collective-permute-done | bytes 589856 | tf_op jit(solution)/shard_map/ppermute | solution.py:172
  156.1 1.1 pad_maximum_fusion.1
  157.2 1.9 collective-permute-start.8
  159.6 1.4 fusion.24
  161.1 1.8 fusion.21
  162.9 1.8 fusion.18
  164.7 1.4 fusion.25
  166.2 0.6 gather_fusion
  166.9 0.8 copy.86
  167.7 1.7 fusion.35
  169.4 4.6 %all-to-all-start.1 = ((bf16[64,2,6,448]{3,1,2,0:T(2,128)(2,1)}), bf16[64,2,6,448]{3,1,2,0:T(2,128)(2,1)S(1)}, u32[]{:S(2)}, u32[]{:S(2)}) async-start(bf16[64,2,6,448]{3,1,2,0:T(2,128)(2,1)} %fusion.35), calls=%async_computation.1 | async-start | bytes 1572864 | tf_op jit(solution)/shard_map/all_to_all | solution.py:205
  174.0 44.9 %all-to-all-done.1 = bf16[64,2,6,448]{3,1,2,0:T(2,128)(2,1)S(1)} async-done(((bf16[64,2,6,448]{3,1,2,0:T(2,128)(2,1)}), bf16[64,2,6,448]{3,1,2,0:T(2,128)(2,1)S(1)}, u32[]{:S(2)}, u32[]{:S(2)}) %all-to-all-start.1) | async-done | bytes 688160 | tf_op jit(solution)/shard_map/all_to_all | solution.py:205
  219.0 1.1 convolution_bitcast_fusion
  220.0 0.6 copy.89
  220.6 1.3 reshape.475
  222.0 1.4 add_convert_fusion
  223.3 0.8 fusion.72
  (58 shorter events, 1.9 us)
Async XLA Ops:
  0.6 90.7 %copy-start = (bf16[1,1,448,2048]{3,2,1,0:T(8,128)(2,1)S(1)}, bf16[1,1,448,2048]{3,2,1,0:T(8,128)(2,1)}, u32[]{:S(2)}) copy-start(bf16[1,1,448,2048]{3,2,1,0:T(8,128)(2,1)} %param.15) | copy-start | bytes 5505028
  0.6 13.3 %collective-permute-start = (bf16[32,3584]{1,0:T(8,128)(2,1)}, bf16[32,3584]{1,0:T(8,128)(2,1)S(1)}, u32[]{:S(2)}, u32[]{:S(2)}) collective-permute-start(bf16[32,3584]{1,0:T(8,128)(2,1)} %bitcast.138), channel_id=1, source_target_pairs={{448,0},{0,64},{64,128},{128,192},{192,256},{256,320},{320,384},{3... | collective-permute-start | bytes 688136 | tf_op jit(solution)/shard_map/ppermute | solution.py:14
  5.0 13.8 %collective-permute-start.1 = (bf16[32,3584]{1,0:T(8,128)(2,1)}, bf16[32,3584]{1,0:T(8,128)(2,1)S(1)}, u32[]{:S(2)}, u32[]{:S(2)}) collective-permute-start(bf16[32,3584]{1,0:T(8,128)(2,1)} %bitcast.139), channel_id=1, source_target_pairs={{64,0},{128,64},{192,128},{256,192},{320,256},{384,320},{448,384},... | collective-permute-start | bytes 688136 | tf_op jit(solution)/shard_map/ppermute | solution.py:14
  10.2 9.8 %collective-permute-start.2 = (bf16[48,2048]{1,0:T(8,128)(2,1)}, bf16[48,2048]{1,0:T(8,128)(2,1)S(1)}, u32[]{:S(2)}, u32[]{:S(2)}) collective-permute-start(bf16[48,2048]{1,0:T(8,128)(2,1)} %bitcast.140), channel_id=1, source_target_pairs={{0,0},{1,4},{2,2},{3,6},{4,1},{5,3},{6,5},{7,7},{8,8},{9,12},{10,1... | collective-permute-start | bytes 589832 | tf_op jit(solution)/shard_map/ppermute | solution.py:111
  13.9 0.7 copy-start.5
  18.8 1.3 copy-start.7
  20.0 1.7 copy-start.10
  21.8 63.1 %all-to-all-start = ((bf16[64,2,6,448]{3,1,2,0:T(2,128)(2,1)}), bf16[64,2,6,448]{3,1,2,0:T(2,128)(2,1)S(1)}, u32[]{:S(2)}, u32[]{:S(2)}) async-start(bf16[64,2,6,448]{3,1,2,0:T(2,128)(2,1)} %copy.80), calls=%async_computation | async-start | bytes 1572864 | tf_op jit(solution)/shard_map/all_to_all | solution.py:130
  91.3 1.6 copy-start.2
  94.9 2.4 %copy-start.4 = (bf16[384,448]{1,0:T(8,128)(2,1)S(1)}, bf16[384,448]{1,0:T(8,128)(2,1)}, u32[]{:S(2)}) copy-start(bf16[384,448]{1,0:T(8,128)(2,1)} %reshape_squeeze.6) | copy-start | bytes 1032196
  94.9 6.9 %collective-permute-start.3 = (f32[192,3072]{1,0:T(8,128)}, f32[192,3072]{1,0:T(8,128)}, u32[]{:S(2)}, u32[]{:S(2)}) collective-permute-start(f32[192,3072]{1,0:T(8,128)} %pad_maximum_fusion), channel_id=1, source_target_pairs={{0,1},{1,0},{2,3},{3,2},{4,5},{5,4},{6,7},{7,6},{8,9},{9,8},{10,11... | collective-permute-start | bytes 7077896 | tf_op jit(solution)/shard_map/ppermute | solution.py:146
  103.7 1.4 copy-start.1
  107.9 12.0 %collective-permute-start.4 = (s16[96,3200]{1,0:T(8,128)(2,1)S(1)}, s16[96,3200]{1,0:T(8,128)(2,1)S(1)}, u32[]{:S(2)}, u32[]{:S(2)}) collective-permute-start(s16[96,3200]{1,0:T(8,128)(2,1)S(1)} %pad_add_fusion), channel_id=1, source_target_pairs={{0,2},{1,5},{2,0},{3,7},{4,6},{5,1},{6,4},{7,3},{8,10},{9,13},{10,... | collective-permute-start | bytes 1843208 | tf_op jit(solution)/shard_map/ppermute | solution.py:154
  119.9 0.8 copy-start.9
  125.2 10.1 %copy-start.11 = (bf16[48,2048]{1,0:T(8,128)(2,1)S(1)}, bf16[48,2048]{1,0:T(8,128)(2,1)}, u32[]{:S(2)}) copy-start(bf16[48,2048]{1,0:T(8,128)(2,1)} %copy-done.10) | copy-start | bytes 589828
  126.0 8.9 %collective-permute-start.5 = (s16[48,3200]{1,0:T(8,128)(2,1)}, s16[48,3200]{1,0:T(8,128)(2,1)S(1)}, u32[]{:S(2)}, u32[]{:S(2)}) collective-permute-start(s16[48,3200]{1,0:T(8,128)(2,1)} %pad_add_fusion.1), channel_id=1, source_target_pairs={{0,4},{1,3},{2,6},{3,1},{4,0},{5,7},{6,2},{7,5},{8,12},{9,11},{10,... | collective-permute-start | bytes 921608 | tf_op jit(solution)/shard_map/ppermute | solution.py:154
  135.5 24.1 %copy-start.3 = (bf16[1,1,1024,448]{2,3,1,0:T(8,128)(2,1)S(1)}, bf16[1,1,1024,448]{2,3,1,0:T(8,128)(2,1)}, u32[]{:S(2)}) copy-start(bf16[1,1,1024,448]{2,3,1,0:T(8,128)(2,1)} %param.16) | copy-start | bytes 2752516
  135.5 8.7 %collective-permute-start.6 = (bf16[48,3072]{1,0:T(8,128)(2,1)S(1)}, bf16[48,3072]{1,0:T(8,128)(2,1)S(1)}, u32[]{:S(2)}, u32[]{:S(2)}) collective-permute-start(bf16[48,3072]{1,0:T(8,128)(2,1)S(1)} %pad_maximum_fusion.3), channel_id=1, source_target_pairs={{0,4},{1,3},{2,6},{3,1},{4,0},{5,7},{6,2},{7,5},{8,12},{9,11},{10,... | collective-permute-start | bytes 884744 | tf_op jit(solution)/shard_map/ppermute | solution.py:172
  144.3 11.8 %collective-permute-start.7 = (bf16[96,3072]{1,0:T(8,128)(2,1)S(1)}, bf16[96,3072]{1,0:T(8,128)(2,1)S(1)}, u32[]{:S(2)}, u32[]{:S(2)}) collective-permute-start(bf16[96,3072]{1,0:T(8,128)(2,1)S(1)} %pad_maximum_fusion.2), channel_id=1, source_target_pairs={{0,2},{1,5},{2,0},{3,7},{4,6},{5,1},{6,4},{7,3},{8,10},{9,13},{10,... | collective-permute-start | bytes 1769480 | tf_op jit(solution)/shard_map/ppermute | solution.py:172
  157.2 5.6 %collective-permute-start.8 = (bf16[192,3072]{1,0:T(8,128)(2,1)}, bf16[192,3072]{1,0:T(8,128)(2,1)}, u32[]{:S(2)}, u32[]{:S(2)}) collective-permute-start(bf16[192,3072]{1,0:T(8,128)(2,1)} %pad_maximum_fusion.1), channel_id=1, source_target_pairs={{0,1},{1,0},{2,3},{3,2},{4,5},{5,4},{6,7},{7,6},{8,9},{9,8},{10,11... | collective-permute-start | bytes 3538952 | tf_op jit(solution)/shard_map/ppermute | solution.py:185
  167.7 6.3 %copy-start.12 = (f32[1,32,1]{1,2,0:T(1,128)S(1)}, f32[1,32,1]{1,2,0:T(1,128)}, u32[]{:S(2)}) copy-start(f32[1,32,1]{1,2,0:T(1,128)} %param.14) | copy-start | bytes 388
  167.7 6.3 %copy-start.13 = (f32[1,32,1]{1,2,0:T(1,128)S(1)}, f32[1,32,1]{1,2,0:T(1,128)}, u32[]{:S(2)}) copy-start(f32[1,32,1]{1,2,0:T(1,128)} %param.11) | copy-start | bytes 388
  169.4 49.6 %all-to-all-start.1 = ((bf16[64,2,6,448]{3,1,2,0:T(2,128)(2,1)}), bf16[64,2,6,448]{3,1,2,0:T(2,128)(2,1)S(1)}, u32[]{:S(2)}, u32[]{:S(2)}) async-start(bf16[64,2,6,448]{3,1,2,0:T(2,128)(2,1)} %fusion.35), calls=%async_computation.1 | async-start | bytes 1572864 | tf_op jit(solution)/shard_map/all_to_all | solution.py:205
  220.0 2.0 copy-start.6
  220.0 2.0 copy-start.8

commit v10 on v8

--- a/solution.py
+++ b/solution.py
@@ -63,19 +63,6 @@
     else:
         bit = jnp.where(core == 0, 2, 1)
     return (member >> bit & 1).astype(jnp.int32)
-
-
-def encode_rows(values, lanes):
-    largest = jnp.maximum(jnp.max(jnp.abs(values), axis=1, keepdims=True), 1e-30)
-    exponent = jnp.floor(jnp.log2(largest)) - 13.0
-    coded = jnp.round(values * jnp.exp2(-exponent)).astype(jnp.int16)
-    tail = jnp.broadcast_to(exponent.astype(jnp.int16), (values.shape[0], lanes))
-    return jnp.concatenate([coded, tail], axis=1)
-
-
-def decode_rows(coded, width):
-    exponent = coded[:, width : width + 1].astype(jnp.float32)
-    return coded[:, :width].astype(jnp.float32) * jnp.exp2(exponent)
 
 
 def body(
@@ -146,11 +133,8 @@
         bit = own_stage_bit(index, group_size, stage)
         kept = lax.dynamic_slice_in_dim(current, bit * half, half, axis=0)
         send_part = lax.dynamic_slice_in_dim(current, (1 - bit) * half, half, axis=0)
-        width = send_part.shape[1]
-        received = lax.ppermute(
-            encode_rows(send_part, 128), "expert", stage_route(devices, group_size, stage)
-        )
-        current = kept + decode_rows(received, width)
+        received = lax.ppermute(send_part, "expert", stage_route(devices, group_size, stage))
+        current = kept + received
 
     pre_share = current[:, : 2 * hidden_units]
     hidden_grad = current[:, 2 * hidden_units :]

time: 219 us -> 228 us (1.041)
  waiting for transfers between devices: 131 us -> 140 us
    ppermute x2, waiting for transfers between devices: 16.6 us -> 25.9 us  [body(): lax.ppermute(send_part, 'expert', stage_route(devices, group_size, stage))]
where the time goes in v10:
time: 228 us; the launch traced here: 227 us
  waiting for transfers between devices  140 us (61%)
  starting transfers between devices  46.9 us (21%)
  local copies, waits for them, and re-layouts  16.8 us (7%)
  other arithmetic  11.8 us (5%)
  matrix products  9.84 us (4%)
    all_to_all x1, waiting for transfers between devices, body(): lax.all_to_all(result, 'expert', split_axis=0, concat_axis=0, tiled=True)  44.9 us
    all_to_all x1, waiting for transfers between devices, body(): lax.all_to_all(sent, 'expert', split_axis=0, concat_axis=0, tiled=True)  44.8 us
    ppermute x2, waiting for transfers between devices, body(): lax.ppermute(send_part, 'expert', stage_route(devices, group_size, stage))  25.9 us
    all_to_all x1, starting transfers between devices, body(): lax.all_to_all(sent, 'expert', split_axis=0, concat_axis=0, tiled=True)  18.2 us
    ppermute x2, waiting for transfers between devices, body(): lax.ppermute(current, 'expert', stage_route(devices, group_size, stage))  16 us
    ppermute x2, starting transfers between devices, shifted(): return lax.ppermute(block, axis, route)  9.59 us
    ppermute x2, waiting for transfers between devices, shifted(): return lax.ppermute(block, axis, route)  4.93 us
    all_to_all x1, starting transfers between devices, body(): lax.all_to_all(result, 'expert', split_axis=0, concat_axis=0, tiled=True)  4.61 us
  transfers between devices with their start and end apart: 11, of which 9 were waited for; matrix products, arithmetic and copies ran while one was open for 3% of the time, Pallas kernels for 0%

profile of v10, /device:TPU:8, one launch (start us, length us, event | category | flops | bytes accessed | tf_op | source)
XLA Modules:
  0.0 227.0 jit_solution(9277171360207076803)
XLA Ops:
  0.6 4.3 %collective-permute-start = (bf16[32,3584]{1,0:T(8,128)(2,1)}, bf16[32,3584]{1,0:T(8,128)(2,1)S(1)}, u32[]{:S(2)}, u32[]{:S(2)}) collective-permute-start(bf16[32,3584]{1,0:T(8,128)(2,1)} %bitcast.102), channel_id=1, source_target_pairs={{448,0},{0,64},{64,128},{128,192},{192,256},{256,320},{320,384},{3... | collective-permute-start | bytes 688136 | tf_op jit(solution)/shard_map/ppermute | solution.py:14
  5.0 5.3 %collective-permute-start.1 = (bf16[32,3584]{1,0:T(8,128)(2,1)}, bf16[32,3584]{1,0:T(8,128)(2,1)S(1)}, u32[]{:S(2)}, u32[]{:S(2)}) collective-permute-start(bf16[32,3584]{1,0:T(8,128)(2,1)} %bitcast.103), channel_id=1, source_target_pairs={{64,0},{128,64},{192,128},{256,192},{320,256},{384,320},{448,384},... | collective-permute-start | bytes 688136 | tf_op jit(solution)/shard_map/ppermute | solution.py:14
  10.2 1.6 collective-permute-start.2
  11.8 0.7 pad_add_fusion
  12.5 0.2 convert_reduce_fusion
  12.7 1.2 collective-permute-done
  13.9 0.7 copy-done.4
  14.6 0.3 stack.97
  14.9 0.1 copy.44
  15.0 3.7 %collective-permute-done.1 = bf16[32,3584]{1,0:T(8,128)(2,1)S(1)} collective-permute-done((bf16[32,3584]{1,0:T(8,128)(2,1)}, bf16[32,3584]{1,0:T(8,128)(2,1)S(1)}, u32[]{:S(2)}, u32[]{:S(2)}) %collective-permute-start.1) | collective-permute-done | bytes 229408 | tf_op jit(solution)/shard_map/ppermute | solution.py:14
  18.8 0.3 stack.98
  19.1 0.1 copy.45
  19.2 0.4 fusion.8
  19.6 0.4 copy.62
  20.1 1.7 copy.47
  21.8 18.2 %all-to-all-start = ((bf16[64,2,6,448]{3,1,2,0:T(2,128)(2,1)}), bf16[64,2,6,448]{3,1,2,0:T(2,128)(2,1)S(1)}, u32[]{:S(2)}, u32[]{:S(2)}) async-start(bf16[64,2,6,448]{3,1,2,0:T(2,128)(2,1)} %copy.47), calls=%async_computation | async-start | bytes 1572864 | tf_op jit(solution)/shard_map/all_to_all | solution.py:113
  40.0 44.8 %all-to-all-done = bf16[64,2,6,448]{3,1,2,0:T(2,128)(2,1)S(1)} async-done(((bf16[64,2,6,448]{3,1,2,0:T(2,128)(2,1)}), bf16[64,2,6,448]{3,1,2,0:T(2,128)(2,1)S(1)}, u32[]{:S(2)}, u32[]{:S(2)}) %all-to-all-start) | async-done | bytes 688160 | tf_op jit(solution)/shard_map/all_to_all | solution.py:113
  84.8 4.2 %slice_reduce_fusion.1 = (bf16[64,6,448]{2,1,0:T(8,128)(2,1)}, bf16[64,6,448]{2,1,0:T(8,128)(2,1)S(1)}) fusion(bf16[64,2,6,448]{3,1,2,0:T(2,128)(2,1)S(1)} %all-to-all-done), kind=kLoop, calls=%fused_computation.35 | loop fusion | bytes 1376256 | tf_op jit(solution)/shard_map/slice | solution.py:114
  89.0 1.3 reshape_squeeze.6
  90.3 0.2 reshape_squeeze.7
  90.6 0.6 fusion.4
  91.2 0.6 copy-done.2
  91.8 0.4 fusion.25
  92.1 1.6 pad_maximum_fusion
  93.7 1.9 collective-permute-start.3
  95.6 0.4 fusion.27
  96.0 0.6 fusion.6
  96.6 3.9 %collective-permute-done.3 = f32[192,3072]{1,0:T(8,128)} collective-permute-done((f32[192,3072]{1,0:T(8,128)}, f32[192,3072]{1,0:T(8,128)}, u32[]{:S(2)}, u32[]{:S(2)}) %collective-permute-start.3) | collective-permute-done | bytes 2359328 | tf_op jit(solution)/shard_map/ppermute | solution.py:129
  100.5 1.9 maximum_add_fusion
  102.4 1.4 copy-done.1
  103.8 0.1 constant_dynamic-slice_fusion.1
  103.9 2.4 %collective-permute-start.4 = (f32[96,3072]{1,0:T(8,128)S(1)}, f32[96,3072]{1,0:T(8,128)}, u32[]{:S(2)}, u32[]{:S(2)}) collective-permute-start(f32[96,3072]{1,0:T(8,128)S(1)} %constant_dynamic-slice_fusion.1), channel_id=1, source_target_pairs={{0,2},{1,5},{2,0},{3,7},{4,6},{5,1},{6,4},{7,3},{8,10},{9,13},{10,... | collective-permute-start | bytes 3538952 | tf_op jit(solution)/shard_map/ppermute | solution.py:136
  106.4 15.7 %collective-permute-done.4 = f32[96,3072]{1,0:T(8,128)} collective-permute-done((f32[96,3072]{1,0:T(8,128)S(1)}, f32[96,3072]{1,0:T(8,128)}, u32[]{:S(2)}, u32[]{:S(2)}) %collective-permute-start.4) | collective-permute-done | bytes 1179680 | tf_op jit(solution)/shard_map/ppermute | solution.py:136
  122.1 1.7 dynamic-slice_add_fusion
  123.9 0.9 constant_dynamic-slice_fusion
  124.7 1.9 collective-permute-start.5
  126.7 10.2 %collective-permute-done.5 = f32[48,3072]{1,0:T(8,128)} collective-permute-done((f32[48,3072]{1,0:T(8,128)}, f32[48,3072]{1,0:T(8,128)}, u32[]{:S(2)}, u32[]{:S(2)}) %collective-permute-start.5) | collective-permute-done | bytes 589856 | tf_op jit(solution)/shard_map/ppermute | solution.py:136
  136.8 1.1 dynamic-slice_add_fusion.1
  138.0 0.2 fusion.42
  138.2 2.1 collective-permute-start.6
  140.2 6.7 %collective-permute-done.6 = bf16[48,3072]{1,0:T(8,128)(2,1)S(1)} collective-permute-done((bf16[48,3072]{1,0:T(8,128)(2,1)S(1)}, bf16[48,3072]{1,0:T(8,128)(2,1)S(1)}, u32[]{:S(2)}, u32[]{:S(2)}) %collective-permute-start.6) | collective-permute-done | bytes 294944 | tf_op jit(solution)/shard_map/ppermute | solution.py:152
  147.0 2.4 %collective-permute-start.7 = (bf16[96,3072]{1,0:T(8,128)(2,1)S(1)}, bf16[96,3072]{1,0:T(8,128)(2,1)S(1)}, u32[]{:S(2)}, u32[]{:S(2)}) collective-permute-start(bf16[96,3072]{1,0:T(8,128)(2,1)S(1)} %pad_maximum_fusion.2), channel_id=1, source_target_pairs={{0,2},{1,5},{2,0},{3,7},{4,6},{5,1},{6,4},{7,3},{8,10},{9,13},{10,... | collective-permute-start | bytes 1769480 | tf_op jit(solution)/shard_map/ppermute | solution.py:152
  149.4 9.3 %collective-permute-done.7 = bf16[96,3072]{1,0:T(8,128)(2,1)S(1)} collective-permute-done((bf16[96,3072]{1,0:T(8,128)(2,1)S(1)}, bf16[96,3072]{1,0:T(8,128)(2,1)S(1)}, u32[]{:S(2)}, u32[]{:S(2)}) %collective-permute-start.7) | collective-permute-done | bytes 589856 | tf_op jit(solution)/shard_map/ppermute | solution.py:152
  158.7 1.1 pad_maximum_fusion.1
  159.9 2.1 collective-permute-start.8
  162.0 0.1 stack.96
  162.1 0.1 broadcast_in_dim.19
  162.2 0.1 broadcast_in_dim.20
  162.3 0.1 stack.115
  162.4 1.4 fusion.21
  163.9 1.8 fusion.18
  165.7 1.8 fusion.15
  167.5 1.4 fusion.22
  169.0 0.1 maximum_maximum_fusion
  169.1 0.6 gather_fusion
  169.7 0.8 copy.48
  170.5 1.7 fusion.32
  172.2 4.6 %all-to-all-start.1 = ((bf16[64,2,6,448]{3,1,2,0:T(2,128)(2,1)}), bf16[64,2,6,448]{3,1,2,0:T(2,128)(2,1)S(1)}, u32[]{:S(2)}, u32[]{:S(2)}) async-start(bf16[64,2,6,448]{3,1,2,0:T(2,128)(2,1)} %fusion.32), calls=%async_computation.1 | async-start | bytes 1572864 | tf_op jit(solution)/shard_map/all_to_all | solution.py:185
  176.9 44.9 %all-to-all-done.1 = bf16[64,2,6,448]{3,1,2,0:T(2,128)(2,1)S(1)} async-done(((bf16[64,2,6,448]{3,1,2,0:T(2,128)(2,1)}), bf16[64,2,6,448]{3,1,2,0:T(2,128)(2,1)S(1)}, u32[]{:S(2)}, u32[]{:S(2)}) %all-to-all-start.1) | async-done | bytes 688160 | tf_op jit(solution)/shard_map/all_to_all | solution.py:185
  221.8 1.1 convolution_bitcast_fusion
  222.8 0.6 copy.51
  223.5 1.3 reshape.421
  224.8 1.4 add_convert_fusion
  226.2 0.8 fusion.64
  (32 shorter events, 0.2 us)
Async XLA Ops:
  0.6 89.9 %copy-start = (bf16[1,1,448,2048]{3,2,1,0:T(8,128)(2,1)S(1)}, bf16[1,1,448,2048]{3,2,1,0:T(8,128)(2,1)}, u32[]{:S(2)}) copy-start(bf16[1,1,448,2048]{3,2,1,0:T(8,128)(2,1)} %param.15) | copy-start | bytes 5505028
  0.6 13.3 %collective-permute-start = (bf16[32,3584]{1,0:T(8,128)(2,1)}, bf16[32,3584]{1,0:T(8,128)(2,1)S(1)}, u32[]{:S(2)}, u32[]{:S(2)}) collective-permute-start(bf16[32,3584]{1,0:T(8,128)(2,1)} %bitcast.102), channel_id=1, source_target_pairs={{448,0},{0,64},{64,128},{128,192},{192,256},{256,320},{320,384},{3... | collective-permute-start | bytes 688136 | tf_op jit(solution)/shard_map/ppermute | solution.py:14
  5.0 13.8 %collective-permute-start.1 = (bf16[32,3584]{1,0:T(8,128)(2,1)}, bf16[32,3584]{1,0:T(8,128)(2,1)S(1)}, u32[]{:S(2)}, u32[]{:S(2)}) collective-permute-start(bf16[32,3584]{1,0:T(8,128)(2,1)} %bitcast.103), channel_id=1, source_target_pairs={{64,0},{128,64},{192,128},{256,192},{320,256},{384,320},{448,384},... | collective-permute-start | bytes 688136 | tf_op jit(solution)/shard_map/ppermute | solution.py:14
  10.2 9.8 %collective-permute-start.2 = (bf16[48,2048]{1,0:T(8,128)(2,1)}, bf16[48,2048]{1,0:T(8,128)(2,1)S(1)}, u32[]{:S(2)}, u32[]{:S(2)}) collective-permute-start(bf16[48,2048]{1,0:T(8,128)(2,1)} %bitcast.104), channel_id=1, source_target_pairs={{0,0},{1,4},{2,2},{3,6},{4,1},{5,3},{6,5},{7,7},{8,8},{9,12},{10,1... | collective-permute-start | bytes 589832 | tf_op jit(solution)/shard_map/ppermute | solution.py:94
  13.9 0.7 copy-start.4
  18.8 1.3 copy-start.6
  20.0 1.7 copy-start.8
  21.8 63.1 %all-to-all-start = ((bf16[64,2,6,448]{3,1,2,0:T(2,128)(2,1)}), bf16[64,2,6,448]{3,1,2,0:T(2,128)(2,1)S(1)}, u32[]{:S(2)}, u32[]{:S(2)}) async-start(bf16[64,2,6,448]{3,1,2,0:T(2,128)(2,1)} %copy.47), calls=%async_computation | async-start | bytes 1572864 | tf_op jit(solution)/shard_map/all_to_all | solution.py:113
  90.6 1.2 copy-start.2
  93.7 6.8 %collective-permute-start.3 = (f32[192,3072]{1,0:T(8,128)}, f32[192,3072]{1,0:T(8,128)}, u32[]{:S(2)}, u32[]{:S(2)}) collective-permute-start(f32[192,3072]{1,0:T(8,128)} %pad_maximum_fusion), channel_id=1, source_target_pairs={{0,1},{1,0},{2,3},{3,2},{4,5},{5,4},{6,7},{7,6},{8,9},{9,8},{10,11... | collective-permute-start | bytes 7077896 | tf_op jit(solution)/shard_map/ppermute | solution.py:129
  102.4 1.4 copy-start.1
  103.9 18.2 %collective-permute-start.4 = (f32[96,3072]{1,0:T(8,128)S(1)}, f32[96,3072]{1,0:T(8,128)}, u32[]{:S(2)}, u32[]{:S(2)}) collective-permute-start(f32[96,3072]{1,0:T(8,128)S(1)} %constant_dynamic-slice_fusion.1), channel_id=1, source_target_pairs={{0,2},{1,5},{2,0},{3,7},{4,6},{5,1},{6,4},{7,3},{8,10},{9,13},{10,... | collective-permute-start | bytes 3538952 | tf_op jit(solution)/shard_map/ppermute | solution.py:136
  123.9 14.1 %copy-start.9 = (bf16[48,2048]{1,0:T(8,128)(2,1)S(1)}, bf16[48,2048]{1,0:T(8,128)(2,1)}, u32[]{:S(2)}) copy-start(bf16[48,2048]{1,0:T(8,128)(2,1)} %copy-done.8) | copy-start | bytes 589828
  124.7 12.1 %collective-permute-start.5 = (f32[48,3072]{1,0:T(8,128)}, f32[48,3072]{1,0:T(8,128)}, u32[]{:S(2)}, u32[]{:S(2)}) collective-permute-start(f32[48,3072]{1,0:T(8,128)} %constant_dynamic-slice_fusion), channel_id=1, source_target_pairs={{0,4},{1,3},{2,6},{3,1},{4,0},{5,7},{6,2},{7,5},{8,12},{9,11},{10,... | collective-permute-start | bytes 1769480 | tf_op jit(solution)/shard_map/ppermute | solution.py:136
  138.2 24.3 %copy-start.3 = (bf16[1,1,1024,448]{2,3,1,0:T(8,128)(2,1)S(1)}, bf16[1,1,1024,448]{2,3,1,0:T(8,128)(2,1)}, u32[]{:S(2)}) copy-start(bf16[1,1,1024,448]{2,3,1,0:T(8,128)(2,1)} %param.16) | copy-start | bytes 2752516
  138.2 8.7 %collective-permute-start.6 = (bf16[48,3072]{1,0:T(8,128)(2,1)S(1)}, bf16[48,3072]{1,0:T(8,128)(2,1)S(1)}, u32[]{:S(2)}, u32[]{:S(2)}) collective-permute-start(bf16[48,3072]{1,0:T(8,128)(2,1)S(1)} %pad_maximum_fusion.3), channel_id=1, source_target_pairs={{0,4},{1,3},{2,6},{3,1},{4,0},{5,7},{6,2},{7,5},{8,12},{9,11},{10,... | collective-permute-start | bytes 884744 | tf_op jit(solution)/shard_map/ppermute | solution.py:152
  147.0 11.8 %collective-permute-start.7 = (bf16[96,3072]{1,0:T(8,128)(2,1)S(1)}, bf16[96,3072]{1,0:T(8,128)(2,1)S(1)}, u32[]{:S(2)}, u32[]{:S(2)}) collective-permute-start(bf16[96,3072]{1,0:T(8,128)(2,1)S(1)} %pad_maximum_fusion.2), channel_id=1, source_target_pairs={{0,2},{1,5},{2,0},{3,7},{4,6},{5,1},{6,4},{7,3},{8,10},{9,13},{10,... | collective-permute-start | bytes 1769480 | tf_op jit(solution)/shard_map/ppermute | solution.py:152
  159.9 5.8 %collective-permute-start.8 = (bf16[192,3072]{1,0:T(8,128)(2,1)}, bf16[192,3072]{1,0:T(8,128)(2,1)}, u32[]{:S(2)}, u32[]{:S(2)}) collective-permute-start(bf16[192,3072]{1,0:T(8,128)(2,1)} %pad_maximum_fusion.1), channel_id=1, source_target_pairs={{0,1},{1,0},{2,3},{3,2},{4,5},{5,4},{6,7},{7,6},{8,9},{9,8},{10,11... | collective-permute-start | bytes 3538952 | tf_op jit(solution)/shard_map/ppermute | solution.py:165
  170.5 6.3 %copy-start.10 = (f32[1,32,1]{1,2,0:T(1,128)S(1)}, f32[1,32,1]{1,2,0:T(1,128)}, u32[]{:S(2)}) copy-start(f32[1,32,1]{1,2,0:T(1,128)} %param.14) | copy-start | bytes 388
  170.5 6.3 %copy-start.11 = (f32[1,32,1]{1,2,0:T(1,128)S(1)}, f32[1,32,1]{1,2,0:T(1,128)}, u32[]{:S(2)}) copy-start(f32[1,32,1]{1,2,0:T(1,128)} %param.11) | copy-start | bytes 388
  172.2 49.6 %all-to-all-start.1 = ((bf16[64,2,6,448]{3,1,2,0:T(2,128)(2,1)}), bf16[64,2,6,448]{3,1,2,0:T(2,128)(2,1)S(1)}, u32[]{:S(2)}, u32[]{:S(2)}) async-start(bf16[64,2,6,448]{3,1,2,0:T(2,128)(2,1)} %fusion.32), calls=%async_computation.1 | async-start | bytes 1572864 | tf_op jit(solution)/shard_map/all_to_all | solution.py:185
  222.8 2.0 copy-start.5
  222.8 2.0 copy-start.7

commit v11 on v10

--- a/solution.py
+++ b/solution.py
@@ -114,14 +114,18 @@
     rows_down = got[:, 0].reshape(-1, share_width)
     rows_up = got[:, 1].reshape(-1, share_width)
 
+    both_proj = jnp.concatenate(
+        [
+            jnp.concatenate([proj_in, jnp.zeros((share_width, hidden_units), proj_in.dtype)], axis=1),
+            jnp.concatenate([jnp.zeros((share_width, 2 * hidden_units), proj_out.dtype), proj_out.T], axis=1),
+        ],
+        axis=0,
+    )
+    both_rows = jnp.concatenate([rows_down, rows_up], axis=1)
+
     def first_partial(start, count):
-        part_down = lax.dynamic_slice_in_dim(rows_down, start, count, axis=0)
-        part_up = lax.dynamic_slice_in_dim(rows_up, start, count, axis=0)
-        pre = jnp.dot(part_down, proj_in, preferred_element_type=jnp.float32)
-        grad = lax.dot_general(
-            part_up, proj_out, (((1,), (1,)), ((), ())), preferred_element_type=jnp.float32
-        )
-        return jnp.concatenate([pre, grad], axis=1)
+        part = lax.dynamic_slice_in_dim(both_rows, start, count, axis=0)
+        return jnp.dot(part, both_proj, preferred_element_type=jnp.float32)
 
     half = rows_down.shape[0] // 2
     bit = own_stage_bit(index, group_size, 0)

time: 228 us -> 220 us (0.965)
  other arithmetic: 11.8 us -> 4.64 us
  local copies, waits for them, and re-layouts: 16.8 us -> 11.7 us
  matrix products: 9.84 us -> 14 us
    dot_general x4 -> x2, matrix products: 1.89 us -> 6.94 us  [first_partial(): return jnp.dot(part, both_proj, preferred_element_type=jnp.float32)]
  transfers between devices with their start and end apart: 11 -> 11, of which waited for: 9 -> 9; matrix products, arithmetic and copies ran while one was open for 3% -> 2% of each run, Pallas kernels for 0% -> 0%
where the time goes in v11:
time: 220 us; the launch traced here: 219 us
  waiting for transfers between devices  141 us (64%)
  starting transfers between devices  46.9 us (21%)
  matrix products  14 us (6%)
  local copies, waits for them, and re-layouts  11.7 us (5%)
  other arithmetic  4.64 us (2%)
    all_to_all x1, waiting for transfers between devices, body(): lax.all_to_all(result, 'expert', split_axis=0, concat_axis=0, tiled=True)  44.9 us
    all_to_all x1, waiting for transfers between devices, body(): lax.all_to_all(sent, 'expert', split_axis=0, concat_axis=0, tiled=True)  44.8 us
    ppermute x2, waiting for transfers between devices, body(): lax.ppermute(send_part, 'expert', stage_route(devices, group_size, stage))  25.6 us
    all_to_all x1, starting transfers between devices, body(): lax.all_to_all(sent, 'expert', split_axis=0, concat_axis=0, tiled=True)  18.2 us
    ppermute x2, waiting for transfers between devices, body(): lax.ppermute(current, 'expert', stage_route(devices, group_size, stage))  16 us
    ppermute x2, starting transfers between devices, shifted(): return lax.ppermute(block, axis, route)  9.46 us
    dot_general x2, matrix products, first_partial(): return jnp.dot(part, both_proj, preferred_element_type=jnp.float32)  6.94 us
    ppermute x2, waiting for transfers between devices, shifted(): return lax.ppermute(block, axis, route)  4.93 us
  transfers between devices with their start and end apart: 11, of which 9 were waited for; matrix products, arithmetic and copies ran while one was open for 2% of the time, Pallas kernels for 0%

profile of v11, /device:TPU:8, one launch (start us, length us, event | category | flops | bytes accessed | tf_op | source)
XLA Modules:
  0.0 219.2 jit_solution(12265590646751222959)
XLA Ops:
  0.6 4.2 %collective-permute-start = (bf16[32,3584]{1,0:T(8,128)(2,1)}, bf16[32,3584]{1,0:T(8,128)(2,1)S(1)}, u32[]{:S(2)}, u32[]{:S(2)}) collective-permute-start(bf16[32,3584]{1,0:T(8,128)(2,1)} %bitcast.92), channel_id=1, source_target_pairs={{448,0},{0,64},{64,128},{128,192},{192,256},{256,320},{320,384},{3... | collective-permute-start | bytes 688136 | tf_op jit(solution)/shard_map/ppermute | solution.py:14
  4.8 5.3 %collective-permute-start.1 = (bf16[32,3584]{1,0:T(8,128)(2,1)}, bf16[32,3584]{1,0:T(8,128)(2,1)S(1)}, u32[]{:S(2)}, u32[]{:S(2)}) collective-permute-start(bf16[32,3584]{1,0:T(8,128)(2,1)} %bitcast.93), channel_id=1, source_target_pairs={{64,0},{128,64},{192,128},{256,192},{320,256},{384,320},{448,384},... | collective-permute-start | bytes 688136 | tf_op jit(solution)/shard_map/ppermute | solution.py:14
  10.1 1.6 collective-permute-start.2
  11.7 0.7 pad_add_fusion
  12.4 0.2 convert_reduce_fusion
  12.6 1.2 collective-permute-done
  13.8 0.7 copy-done
  14.5 0.3 stack.97
  14.8 0.1 copy.44
  14.9 3.7 %collective-permute-done.1 = bf16[32,3584]{1,0:T(8,128)(2,1)S(1)} collective-permute-done((bf16[32,3584]{1,0:T(8,128)(2,1)}, bf16[32,3584]{1,0:T(8,128)(2,1)S(1)}, u32[]{:S(2)}, u32[]{:S(2)}) %collective-permute-start.1) | collective-permute-done | bytes 229408 | tf_op jit(solution)/shard_map/ppermute | solution.py:14
  18.6 0.3 stack.98
  18.9 0.1 copy.45
  19.0 0.4 fusion.6
  19.4 0.4 copy.62
  19.9 0.0 collective-permute-done.2
  19.9 1.7 copy.47
  21.6 18.2 %all-to-all-start = ((bf16[64,2,6,448]{3,1,2,0:T(2,128)(2,1)}), bf16[64,2,6,448]{3,1,2,0:T(2,128)(2,1)S(1)}, u32[]{:S(2)}, u32[]{:S(2)}) async-start(bf16[64,2,6,448]{3,1,2,0:T(2,128)(2,1)} %copy.47), calls=%async_computation | async-start | bytes 1572864 | tf_op jit(solution)/shard_map/all_to_all | solution.py:113
  39.9 44.8 %all-to-all-done = bf16[64,2,6,448]{3,1,2,0:T(2,128)(2,1)S(1)} async-done(((bf16[64,2,6,448]{3,1,2,0:T(2,128)(2,1)}), bf16[64,2,6,448]{3,1,2,0:T(2,128)(2,1)S(1)}, u32[]{:S(2)}, u32[]{:S(2)}) %all-to-all-start) | async-done | bytes 688160 | tf_op jit(solution)/shard_map/all_to_all | solution.py:113
  84.7 3.3 %slice_reduce_fusion = (bf16[64,6,448]{2,1,0:T(8,128)(2,1)S(1)}, bf16[64,6,448]{2,1,0:T(8,128)(2,1)S(1)}) fusion(bf16[64,2,6,448]{3,1,2,0:T(2,128)(2,1)S(1)} %all-to-all-done), kind=kLoop, calls=%fused_computation.27 | loop fusion | bytes 1376256 | tf_op jit(solution)/shard_map/slice | solution.py:115
  88.0 0.2 reshape_squeeze.6
  88.3 0.2 reshape_squeeze.7
  88.5 3.1 %fusion.3 = f32[192,3072]{1,0:T(8,128)S(1)} fusion(bf16[448,1024]{1,0:T(8,128)(2,1)} %bitcast.90, bf16[448,2048]{1,0:T(8,128)(2,1)} %bitcast.88, s32[]{:T(128)S(6)} %select_n.113, bf16[384,448]{1,0:T(8,128)(2,1)S(1)} %reshape_squeeze.6, bf16[384,448]{1,0:T(8,128)(2,1)S(1)} %reshape_squeeze.7), kind=kOutput, calls=%fused_computation.7 | convolution fusion | flops 1079672832 | bytes 5799940 | tf_op jit(solution)/shard_map/dot_general | solution.py:128
  91.6 1.9 collective-permute-start.3
  93.5 4.6 %collective-permute-done.3 = f32[192,3072]{1,0:T(8,128)} collective-permute-done((f32[192,3072]{1,0:T(8,128)S(1)}, f32[192,3072]{1,0:T(8,128)}, u32[]{:S(2)}, u32[]{:S(2)}) %collective-permute-start.3) | collective-permute-done | bytes 2359328 | tf_op jit(solution)/shard_map/ppermute | solution.py:133
  98.1 3.9 %convolution_add_fusion = f32[192,3072]{1,0:T(8,128)S(1)} fusion(f32[192,3072]{1,0:T(8,128)} %collective-permute-done.3, bf16[448,1024]{1,0:T(8,128)(2,1)} %bitcast.91, bf16[448,2048]{1,0:T(8,128)(2,1)} %bitcast.89, s32[]{:T(128)S(6)} %select_n.112, bf16[384,448]{1,0:T(8,128)(2,1)S(1)} %reshape_squeeze.6, bf16[384,448]{1,0:T(8,128)(2,1)S(1)} %reshape_squeeze.7), kind=kOutput, calls=%fused_computation.6 | convolution fusion | flops 1080262656 | bytes 8159236 | tf_op jit(solution)/shard_map/dot_general | solution.py:128
  102.0 0.1 constant_dynamic-slice_fusion.1
  102.1 2.4 %collective-permute-start.4 = (f32[96,3072]{1,0:T(8,128)S(1)}, f32[96,3072]{1,0:T(8,128)}, u32[]{:S(2)}, u32[]{:S(2)}) collective-permute-start(f32[96,3072]{1,0:T(8,128)S(1)} %constant_dynamic-slice_fusion.1), channel_id=1, source_target_pairs={{0,2},{1,5},{2,0},{3,7},{4,6},{5,1},{6,4},{7,3},{8,10},{9,13},{10,... | collective-permute-start | bytes 3538952 | tf_op jit(solution)/shard_map/ppermute | solution.py:140
  104.6 15.7 %collective-permute-done.4 = f32[96,3072]{1,0:T(8,128)} collective-permute-done((f32[96,3072]{1,0:T(8,128)S(1)}, f32[96,3072]{1,0:T(8,128)}, u32[]{:S(2)}, u32[]{:S(2)}) %collective-permute-start.4) | collective-permute-done | bytes 1179680 | tf_op jit(solution)/shard_map/ppermute | solution.py:140
  120.3 1.4 dynamic-slice_add_fusion
  121.8 2.1 collective-permute-start.5
  123.9 9.8 %collective-permute-done.5 = f32[48,3072]{1,0:T(8,128)S(1)} collective-permute-done((f32[48,3072]{1,0:T(8,128)S(1)}, f32[48,3072]{1,0:T(8,128)S(1)}, u32[]{:S(2)}, u32[]{:S(2)}) %collective-permute-start.5) | collective-permute-done | bytes 589856 | tf_op jit(solution)/shard_map/ppermute | solution.py:140
  133.7 0.1 dynamic-slice_add_fusion.1
  133.8 0.2 fusion.30
  134.0 1.9 collective-permute-start.6
  135.9 6.7 %collective-permute-done.6 = bf16[48,3072]{1,0:T(8,128)(2,1)S(1)} collective-permute-done((bf16[48,3072]{1,0:T(8,128)(2,1)S(1)}, bf16[48,3072]{1,0:T(8,128)(2,1)S(1)}, u32[]{:S(2)}, u32[]{:S(2)}) %collective-permute-start.6) | collective-permute-done | bytes 294944 | tf_op jit(solution)/shard_map/ppermute | solution.py:156
  142.6 0.0 copy-start.8
  142.7 2.6 %collective-permute-start.7 = (bf16[96,3072]{1,0:T(8,128)(2,1)S(1)}, bf16[96,3072]{1,0:T(8,128)(2,1)S(1)}, u32[]{:S(2)}, u32[]{:S(2)}) collective-permute-start(bf16[96,3072]{1,0:T(8,128)(2,1)S(1)} %pad_maximum_fusion.1), channel_id=1, source_target_pairs={{0,2},{1,5},{2,0},{3,7},{4,6},{5,1},{6,4},{7,3},{8,10},{9,13},{10,... | collective-permute-start | bytes 1769480 | tf_op jit(solution)/shard_map/ppermute | solution.py:156
  145.2 9.3 %collective-permute-done.7 = bf16[96,3072]{1,0:T(8,128)(2,1)S(1)} collective-permute-done((bf16[96,3072]{1,0:T(8,128)(2,1)S(1)}, bf16[96,3072]{1,0:T(8,128)(2,1)S(1)}, u32[]{:S(2)}, u32[]{:S(2)}) %collective-permute-start.7) | collective-permute-done | bytes 589856 | tf_op jit(solution)/shard_map/ppermute | solution.py:156
  154.6 0.1 pad_maximum_fusion
  154.6 2.1 collective-permute-start.8
  156.8 0.1 stack.96
  156.9 0.1 broadcast_in_dim.21
  157.0 0.1 broadcast_in_dim.22
  157.1 0.1 stack.115
  157.2 1.6 fusion.9
  158.8 0.0 copy-start.9
  158.9 0.7 fusion.7
  159.5 0.5 copy-done.9
  160.0 1.5 fusion.10
  161.5 1.8 fusion.8
  163.3 0.1 maximum_maximum_fusion
  163.4 0.6 gather_fusion
  164.0 0.8 copy.48
  164.8 0.0 copy-start.6
  164.8 0.0 copy-start.7
  164.9 1.7 fusion.16
  166.6 4.6 %all-to-all-start.1 = ((bf16[64,2,6,448]{3,1,2,0:T(2,128)(2,1)}), bf16[64,2,6,448]{3,1,2,0:T(2,128)(2,1)S(1)}, u32[]{:S(2)}, u32[]{:S(2)}) async-start(bf16[64,2,6,448]{3,1,2,0:T(2,128)(2,1)} %fusion.16), calls=%async_computation.1 | async-start | bytes 1572864 | tf_op jit(solution)/shard_map/all_to_all | solution.py:189
  171.2 44.9 %all-to-all-done.1 = bf16[64,2,6,448]{3,1,2,0:T(2,128)(2,1)S(1)} async-done(((bf16[64,2,6,448]{3,1,2,0:T(2,128)(2,1)}), bf16[64,2,6,448]{3,1,2,0:T(2,128)(2,1)S(1)}, u32[]{:S(2)}, u32[]{:S(2)}) %all-to-all-start.1) | async-done | bytes 688160 | tf_op jit(solution)/shard_map/all_to_all | solution.py:189
  216.1 1.1 convolution_bitcast_fusion
  217.2 0.0 copy-start.3
  217.2 0.6 copy.51
  217.8 0.4 reshape.421
  218.2 0.2 add_convert_fusion
  218.4 0.8 fusion.54
  (24 shorter events, 0.2 us)
Async XLA Ops:
  0.6 13.2 %collective-permute-start = (bf16[32,3584]{1,0:T(8,128)(2,1)}, bf16[32,3584]{1,0:T(8,128)(2,1)S(1)}, u32[]{:S(2)}, u32[]{:S(2)}) collective-permute-start(bf16[32,3584]{1,0:T(8,128)(2,1)} %bitcast.92), channel_id=1, source_target_pairs={{448,0},{0,64},{64,128},{128,192},{192,256},{256,320},{320,384},{3... | collective-permute-start | bytes 688136 | tf_op jit(solution)/shard_map/ppermute | solution.py:14
  4.8 13.8 %collective-permute-start.1 = (bf16[32,3584]{1,0:T(8,128)(2,1)}, bf16[32,3584]{1,0:T(8,128)(2,1)S(1)}, u32[]{:S(2)}, u32[]{:S(2)}) collective-permute-start(bf16[32,3584]{1,0:T(8,128)(2,1)} %bitcast.93), channel_id=1, source_target_pairs={{64,0},{128,64},{192,128},{256,192},{320,256},{384,320},{448,384},... | collective-permute-start | bytes 688136 | tf_op jit(solution)/shard_map/ppermute | solution.py:14
  10.1 9.8 %collective-permute-start.2 = (bf16[48,2048]{1,0:T(8,128)(2,1)}, bf16[48,2048]{1,0:T(8,128)(2,1)S(1)}, u32[]{:S(2)}, u32[]{:S(2)}) collective-permute-start(bf16[48,2048]{1,0:T(8,128)(2,1)} %bitcast.94), channel_id=1, source_target_pairs={{0,0},{1,4},{2,2},{3,6},{4,1},{5,3},{6,5},{7,7},{8,8},{9,12},{10,1... | collective-permute-start | bytes 589832 | tf_op jit(solution)/shard_map/ppermute | solution.py:94
  13.8 0.7 copy-start
  18.6 1.3 copy-start.2
  19.9 1.7 copy-start.4
  21.6 63.1 %all-to-all-start = ((bf16[64,2,6,448]{3,1,2,0:T(2,128)(2,1)}), bf16[64,2,6,448]{3,1,2,0:T(2,128)(2,1)S(1)}, u32[]{:S(2)}, u32[]{:S(2)}) async-start(bf16[64,2,6,448]{3,1,2,0:T(2,128)(2,1)} %copy.47), calls=%async_computation | async-start | bytes 1572864 | tf_op jit(solution)/shard_map/all_to_all | solution.py:113
  91.6 6.6 %collective-permute-start.3 = (f32[192,3072]{1,0:T(8,128)S(1)}, f32[192,3072]{1,0:T(8,128)}, u32[]{:S(2)}, u32[]{:S(2)}) collective-permute-start(f32[192,3072]{1,0:T(8,128)S(1)} %fusion.3), channel_id=1, source_target_pairs={{0,1},{1,0},{2,3},{3,2},{4,5},{5,4},{6,7},{7,6},{8,9},{9,8},{10,11... | collective-permute-start | bytes 7077896 | tf_op jit(solution)/shard_map/ppermute | solution.py:133
  102.1 18.2 %collective-permute-start.4 = (f32[96,3072]{1,0:T(8,128)S(1)}, f32[96,3072]{1,0:T(8,128)}, u32[]{:S(2)}, u32[]{:S(2)}) collective-permute-start(f32[96,3072]{1,0:T(8,128)S(1)} %constant_dynamic-slice_fusion.1), channel_id=1, source_target_pairs={{0,2},{1,5},{2,0},{3,7},{4,6},{5,1},{6,4},{7,3},{8,10},{9,13},{10,... | collective-permute-start | bytes 3538952 | tf_op jit(solution)/shard_map/ppermute | solution.py:140
  121.7 12.0 %copy-start.5 = (bf16[48,2048]{1,0:T(8,128)(2,1)S(1)}, bf16[48,2048]{1,0:T(8,128)(2,1)}, u32[]{:S(2)}) copy-start(bf16[48,2048]{1,0:T(8,128)(2,1)} %copy-done.4) | copy-start | bytes 589828
  121.8 11.9 %collective-permute-start.5 = (f32[48,3072]{1,0:T(8,128)S(1)}, f32[48,3072]{1,0:T(8,128)S(1)}, u32[]{:S(2)}, u32[]{:S(2)}) collective-permute-start(f32[48,3072]{1,0:T(8,128)S(1)} %constant_dynamic-slice_fusion), channel_id=1, source_target_pairs={{0,4},{1,3},{2,6},{3,1},{4,0},{5,7},{6,2},{7,5},{8,12},{9,11},{10,... | collective-permute-start | bytes 1769480 | tf_op jit(solution)/shard_map/ppermute | solution.py:140
  134.0 8.6 %collective-permute-start.6 = (bf16[48,3072]{1,0:T(8,128)(2,1)S(1)}, bf16[48,3072]{1,0:T(8,128)(2,1)S(1)}, u32[]{:S(2)}, u32[]{:S(2)}) collective-permute-start(bf16[48,3072]{1,0:T(8,128)(2,1)S(1)} %pad_maximum_fusion.2), channel_id=1, source_target_pairs={{0,4},{1,3},{2,6},{3,1},{4,0},{5,7},{6,2},{7,5},{8,12},{9,11},{10,... | collective-permute-start | bytes 884744 | tf_op jit(solution)/shard_map/ppermute | solution.py:156
  142.6 16.2 %copy-start.8 = (bf16[1,1,448,2048]{3,2,1,0:T(8,128)(2,1)S(1)}, bf16[1,1,448,2048]{3,2,1,0:T(8,128)(2,1)}, u32[]{:S(2)}) copy-start(bf16[1,1,448,2048]{3,2,1,0:T(8,128)(2,1)} %param.15) | copy-start | bytes 5505028
  142.7 11.9 %collective-permute-start.7 = (bf16[96,3072]{1,0:T(8,128)(2,1)S(1)}, bf16[96,3072]{1,0:T(8,128)(2,1)S(1)}, u32[]{:S(2)}, u32[]{:S(2)}) collective-permute-start(bf16[96,3072]{1,0:T(8,128)(2,1)S(1)} %pad_maximum_fusion.1), channel_id=1, source_target_pairs={{0,2},{1,5},{2,0},{3,7},{4,6},{5,1},{6,4},{7,3},{8,10},{9,13},{10,... | collective-permute-start | bytes 1769480 | tf_op jit(solution)/shard_map/ppermute | solution.py:156
  154.6 4.9 %collective-permute-start.8 = (bf16[192,3072]{1,0:T(8,128)(2,1)S(1)}, bf16[192,3072]{1,0:T(8,128)(2,1)}, u32[]{:S(2)}, u32[]{:S(2)}) collective-permute-start(bf16[192,3072]{1,0:T(8,128)(2,1)S(1)} %pad_maximum_fusion), channel_id=1, source_target_pairs={{0,1},{1,0},{2,3},{3,2},{4,5},{5,4},{6,7},{7,6},{8,9},{9,8},{10,11... | collective-permute-start | bytes 3538952 | tf_op jit(solution)/shard_map/ppermute | solution.py:169
  158.8 1.2 copy-start.9
  164.8 6.4 %copy-start.6 = (f32[1,32,1]{1,2,0:T(1,128)S(1)}, f32[1,32,1]{1,2,0:T(1,128)}, u32[]{:S(2)}) copy-start(f32[1,32,1]{1,2,0:T(1,128)} %param.14) | copy-start | bytes 388
  164.8 6.3 %copy-start.7 = (f32[1,32,1]{1,2,0:T(1,128)S(1)}, f32[1,32,1]{1,2,0:T(1,128)}, u32[]{:S(2)}) copy-start(f32[1,32,1]{1,2,0:T(1,128)} %param.11) | copy-start | bytes 388
  166.6 49.6 %all-to-all-start.1 = ((bf16[64,2,6,448]{3,1,2,0:T(2,128)(2,1)}), bf16[64,2,6,448]{3,1,2,0:T(2,128)(2,1)S(1)}, u32[]{:S(2)}, u32[]{:S(2)}) async-start(bf16[64,2,6,448]{3,1,2,0:T(2,128)(2,1)} %fusion.16), calls=%async_computation.1 | async-start | bytes 1572864 | tf_op jit(solution)/shard_map/all_to_all | solution.py:189
  217.2 1.1 copy-start.1
  217.2 1.1 copy-start.3

commit v12 on v11

--- a/solution.py
+++ b/solution.py
@@ -156,15 +156,17 @@
         partner = lax.ppermute(current, "expert", stage_route(devices, group_size, stage))
         current = jnp.concatenate([current, partner], axis=0)
 
+    last_proj = jnp.concatenate(
+        [
+            jnp.concatenate([proj_out, jnp.zeros((hidden_units, share_width), proj_out.dtype)], axis=1),
+            jnp.concatenate([jnp.zeros((2 * hidden_units, share_width), proj_in.dtype), proj_in.T], axis=1),
+        ],
+        axis=0,
+    )
+
     def last_matmul(block):
-        out_down = jnp.dot(
-            block[:, :hidden_units], proj_out, preferred_element_type=jnp.float32
-        ).astype(jnp.bfloat16)
-        out_up = lax.dot_general(
-            block[:, hidden_units:], proj_in, (((1,), (1,)), ((), ())),
-            preferred_element_type=jnp.float32,
-        ).astype(jnp.bfloat16)
-        return jnp.stack([out_down, out_up])
+        both = jnp.dot(block, last_proj, preferred_element_type=jnp.float32).astype(jnp.bfloat16)
+        return jnp.stack([both[:, :share_width], both[:, share_width:]])
 
     partner = lax.ppermute(current, "expert", stage_route(devices, group_size, 0))
     own_out = last_matmul(current)

time: 220 us -> 220 us (level)
    dot_general x4 -> x2, matrix products: 5.56 us -> 6.15 us  [last_matmul(): jnp.dot(block, last_proj, preferred_element_type=jnp.float32)]
  transfers between devices with their start and end apart: 11 -> 11, of which waited for: 9 -> 9; matrix products, arithmetic and copies ran while one was open for 2% -> 3% of each run, Pallas kernels for 0% -> 0%
where the time goes in v12:
time: 220 us; the launch traced here: 219 us
  waiting for transfers between devices  141 us (64%)
  starting transfers between devices  46.9 us (21%)
  matrix products  14.6 us (7%)
  local copies, waits for them, and re-layouts  11.4 us (5%)
  other arithmetic  4.62 us (2%)
    all_to_all x1, waiting for transfers between devices, body(): lax.all_to_all(result, 'expert', split_axis=0, concat_axis=0, tiled=True)  44.9 us
    all_to_all x1, waiting for transfers between devices, body(): lax.all_to_all(sent, 'expert', split_axis=0, concat_axis=0, tiled=True)  44.8 us
    ppermute x2, waiting for transfers between devices, body(): lax.ppermute(send_part, 'expert', stage_route(devices, group_size, stage))  25.6 us
    all_to_all x1, starting transfers between devices, body(): lax.all_to_all(sent, 'expert', split_axis=0, concat_axis=0, tiled=True)  18.2 us
    ppermute x2, waiting for transfers between devices, body(): lax.ppermute(current, 'expert', stage_route(devices, group_size, stage))  15.8 us
    ppermute x2, starting transfers between devices, shifted(): return lax.ppermute(block, axis, route)  9.46 us
    dot_general x2, matrix products, first_partial(): return jnp.dot(part, both_proj, preferred_element_type=jnp.float32)  6.94 us
    dot_general x2, matrix products, last_matmul(): jnp.dot(block, last_proj, preferred_element_type=jnp.float32)  6.15 us
  transfers between devices with their start and end apart: 11, of which 9 were waited for; matrix products, arithmetic and copies ran while one was open for 3% of the time, Pallas kernels for 0%

profile of v12, /device:TPU:8, one launch (start us, length us, event | category | flops | bytes accessed | tf_op | source)
XLA Modules:
  0.0 219.3 jit_solution(7233780786838895602)
XLA Ops:
  0.6 4.2 %collective-permute-start = (bf16[32,3584]{1,0:T(8,128)(2,1)}, bf16[32,3584]{1,0:T(8,128)(2,1)S(1)}, u32[]{:S(2)}, u32[]{:S(2)}) collective-permute-start(bf16[32,3584]{1,0:T(8,128)(2,1)} %bitcast.91), channel_id=1, source_target_pairs={{448,0},{0,64},{64,128},{128,192},{192,256},{256,320},{320,384},{3... | collective-permute-start | bytes 688136 | tf_op jit(solution)/shard_map/ppermute | solution.py:14
  4.8 5.3 %collective-permute-start.1 = (bf16[32,3584]{1,0:T(8,128)(2,1)}, bf16[32,3584]{1,0:T(8,128)(2,1)S(1)}, u32[]{:S(2)}, u32[]{:S(2)}) collective-permute-start(bf16[32,3584]{1,0:T(8,128)(2,1)} %bitcast.92), channel_id=1, source_target_pairs={{64,0},{128,64},{192,128},{256,192},{320,256},{384,320},{448,384},... | collective-permute-start | bytes 688136 | tf_op jit(solution)/shard_map/ppermute | solution.py:14
  10.1 1.6 collective-permute-start.2
  11.7 0.7 pad_add_fusion
  12.4 0.2 convert_reduce_fusion
  12.6 1.2 collective-permute-done
  13.8 0.7 copy-done
  14.5 0.3 stack.97
  14.8 0.1 copy.44
  14.9 3.7 %collective-permute-done.1 = bf16[32,3584]{1,0:T(8,128)(2,1)S(1)} collective-permute-done((bf16[32,3584]{1,0:T(8,128)(2,1)}, bf16[32,3584]{1,0:T(8,128)(2,1)S(1)}, u32[]{:S(2)}, u32[]{:S(2)}) %collective-permute-start.1) | collective-permute-done | bytes 229408 | tf_op jit(solution)/shard_map/ppermute | solution.py:14
  18.6 0.3 stack.98
  18.9 0.1 copy.45
  19.0 0.4 fusion.13
  19.4 0.4 copy.62
  19.9 0.0 collective-permute-done.2
  19.9 1.7 copy.47
  21.6 18.2 %all-to-all-start = ((bf16[64,2,6,448]{3,1,2,0:T(2,128)(2,1)}), bf16[64,2,6,448]{3,1,2,0:T(2,128)(2,1)S(1)}, u32[]{:S(2)}, u32[]{:S(2)}) async-start(bf16[64,2,6,448]{3,1,2,0:T(2,128)(2,1)} %copy.47), calls=%async_computation | async-start | bytes 1572864 | tf_op jit(solution)/shard_map/all_to_all | solution.py:113
  39.9 44.8 %all-to-all-done = bf16[64,2,6,448]{3,1,2,0:T(2,128)(2,1)S(1)} async-done(((bf16[64,2,6,448]{3,1,2,0:T(2,128)(2,1)}), bf16[64,2,6,448]{3,1,2,0:T(2,128)(2,1)S(1)}, u32[]{:S(2)}, u32[]{:S(2)}) %all-to-all-start) | async-done | bytes 688160 | tf_op jit(solution)/shard_map/all_to_all | solution.py:113
  84.7 3.3 %slice_reduce_fusion = (bf16[64,6,448]{2,1,0:T(8,128)(2,1)S(1)}, bf16[64,6,448]{2,1,0:T(8,128)(2,1)S(1)}) fusion(bf16[64,2,6,448]{3,1,2,0:T(2,128)(2,1)S(1)} %all-to-all-done), kind=kLoop, calls=%fused_computation.24 | loop fusion | bytes 1376256 | tf_op jit(solution)/shard_map/slice | solution.py:115
  88.0 0.2 reshape_squeeze.6
  88.3 0.2 reshape_squeeze.7
  88.5 3.1 %fusion.6 = f32[192,3072]{1,0:T(8,128)S(1)} fusion(bf16[448,1024]{1,0:T(8,128)(2,1)} %bitcast.87, bf16[448,2048]{1,0:T(8,128)(2,1)} %bitcast.83, s32[]{:T(128)S(6)} %select_n.113, bf16[384,448]{1,0:T(8,128)(2,1)S(1)} %reshape_squeeze.6, bf16[384,448]{1,0:T(8,128)(2,1)S(1)} %reshape_squeeze.7), kind=kOutput, calls=%fused_computation.12 | convolution fusion | flops 1079672832 | bytes 5799940 | tf_op jit(solution)/shard_map/dot_general | solution.py:128
  91.6 1.9 collective-permute-start.3
  93.5 4.6 %collective-permute-done.3 = f32[192,3072]{1,0:T(8,128)} collective-permute-done((f32[192,3072]{1,0:T(8,128)S(1)}, f32[192,3072]{1,0:T(8,128)}, u32[]{:S(2)}, u32[]{:S(2)}) %collective-permute-start.3) | collective-permute-done | bytes 2359328 | tf_op jit(solution)/shard_map/ppermute | solution.py:133
  98.1 3.9 %convolution_add_fusion = f32[192,3072]{1,0:T(8,128)S(1)} fusion(f32[192,3072]{1,0:T(8,128)} %collective-permute-done.3, bf16[448,1024]{1,0:T(8,128)(2,1)} %bitcast.88, bf16[448,2048]{1,0:T(8,128)(2,1)} %bitcast.84, s32[]{:T(128)S(6)} %select_n.112, bf16[384,448]{1,0:T(8,128)(2,1)S(1)} %reshape_squeeze.6, bf16[384,448]{1,0:T(8,128)(2,1)S(1)} %reshape_squeeze.7), kind=kOutput, calls=%fused_computation.11 | convolution fusion | flops 1080262656 | bytes 8159236 | tf_op jit(solution)/shard_map/dot_general | solution.py:128
  102.0 0.1 constant_dynamic-slice_fusion.1
  102.1 2.4 %collective-permute-start.4 = (f32[96,3072]{1,0:T(8,128)S(1)}, f32[96,3072]{1,0:T(8,128)}, u32[]{:S(2)}, u32[]{:S(2)}) collective-permute-start(f32[96,3072]{1,0:T(8,128)S(1)} %constant_dynamic-slice_fusion.1), channel_id=1, source_target_pairs={{0,2},{1,5},{2,0},{3,7},{4,6},{5,1},{6,4},{7,3},{8,10},{9,13},{10,... | collective-permute-start | bytes 3538952 | tf_op jit(solution)/shard_map/ppermute | solution.py:140
  104.6 15.7 %collective-permute-done.4 = f32[96,3072]{1,0:T(8,128)} collective-permute-done((f32[96,3072]{1,0:T(8,128)S(1)}, f32[96,3072]{1,0:T(8,128)}, u32[]{:S(2)}, u32[]{:S(2)}) %collective-permute-start.4) | collective-permute-done | bytes 1179680 | tf_op jit(solution)/shard_map/ppermute | solution.py:140
  120.3 1.4 dynamic-slice_add_fusion
  121.8 2.1 collective-permute-start.5
  123.8 9.8 %collective-permute-done.5 = f32[48,3072]{1,0:T(8,128)S(1)} collective-permute-done((f32[48,3072]{1,0:T(8,128)S(1)}, f32[48,3072]{1,0:T(8,128)S(1)}, u32[]{:S(2)}, u32[]{:S(2)}) %collective-permute-start.5) | collective-permute-done | bytes 589856 | tf_op jit(solution)/shard_map/ppermute | solution.py:140
  133.7 0.1 dynamic-slice_add_fusion.1
  133.8 0.2 fusion.33
  133.9 0.0 copy-start.9
  134.0 2.1 collective-permute-start.6
  136.0 6.7 %collective-permute-done.6 = bf16[48,3072]{1,0:T(8,128)(2,1)S(1)} collective-permute-done((bf16[48,3072]{1,0:T(8,128)(2,1)S(1)}, bf16[48,3072]{1,0:T(8,128)(2,1)S(1)}, u32[]{:S(2)}, u32[]{:S(2)}) %collective-permute-start.6) | collective-permute-done | bytes 294944 | tf_op jit(solution)/shard_map/ppermute | solution.py:156
  142.8 2.4 %collective-permute-start.7 = (bf16[96,3072]{1,0:T(8,128)(2,1)S(1)}, bf16[96,3072]{1,0:T(8,128)(2,1)S(1)}, u32[]{:S(2)}, u32[]{:S(2)}) collective-permute-start(bf16[96,3072]{1,0:T(8,128)(2,1)S(1)} %pad_maximum_fusion.1), channel_id=1, source_target_pairs={{0,2},{1,5},{2,0},{3,7},{4,6},{5,1},{6,4},{7,3},{8,10},{9,13},{10,... | collective-permute-start | bytes 1769480 | tf_op jit(solution)/shard_map/ppermute | solution.py:156
  145.3 0.1 stack.115
  145.4 0.1 stack.96
  145.5 9.1 %collective-permute-done.7 = bf16[96,3072]{1,0:T(8,128)(2,1)S(1)} collective-permute-done((bf16[96,3072]{1,0:T(8,128)(2,1)S(1)}, bf16[96,3072]{1,0:T(8,128)(2,1)S(1)}, u32[]{:S(2)}, u32[]{:S(2)}) %collective-permute-start.7) | collective-permute-done | bytes 589856 | tf_op jit(solution)/shard_map/ppermute | solution.py:156
  154.5 0.1 pad_maximum_fusion
  154.6 2.1 collective-permute-start.8
  156.8 0.1 broadcast_in_dim.14
  156.8 0.1 broadcast_in_dim.24
  156.9 0.0 copy-start.8
  156.9 3.3 %fusion.14 = bf16[192,896]{1,0:T(8,128)(2,1)S(1)} fusion(bf16[2048,448]{0,1:T(8,128)(2,1)} %bitcast.85, bf16[1024,448]{0,1:T(8,128)(2,1)S(1)} %bitcast.89, bf16[96,3072]{1,0:T(8,128)(2,1)S(1)} %collective-permute-done.7, bf16[48,3072]{1,0:T(8,128)(2,1)S(1)} %collective-permute-done.6, bf16[48,1024]{1,0:T(8,128)(2,1)S(1)} %get-tuple-element.9, ...), kind=kOutput, calls=%fused_computation.19 | convolution fusion | flops 1085054976 | bytes 4276224 | tf_op jit(solution)/shard_map/dot_general | solution.py:168
  160.2 0.1 slice_bitcast_fusion.3
  160.3 0.0 collective-permute-done.8
  160.4 2.9 %fusion.17 = bf16[192,896]{1,0:T(8,128)(2,1)S(1)} fusion(bf16[192,3072]{1,0:T(8,128)(2,1)} %collective-permute-done.8, bf16[2048,448]{0,1:T(8,128)(2,1)S(1)} %bitcast.86, bf16[1024,448]{0,1:T(8,128)(2,1)S(1)} %bitcast.90), kind=kOutput, calls=%fused_computation.20 | convolution fusion | flops 1079156736 | bytes 4276224 | tf_op jit(solution)/shard_map/dot_general | solution.py:168
  163.3 0.1 slice_bitcast_fusion.1
  163.4 0.1 maximum_maximum_fusion
  163.5 0.6 gather_fusion
  164.1 0.0 copy-start.6
  164.1 0.0 copy-start.7
  164.1 0.8 copy.48
  164.9 1.7 fusion.21
  166.6 4.6 %all-to-all-start.1 = ((bf16[64,2,6,448]{3,1,2,0:T(2,128)(2,1)}), bf16[64,2,6,448]{3,1,2,0:T(2,128)(2,1)S(1)}, u32[]{:S(2)}, u32[]{:S(2)}) async-start(bf16[64,2,6,448]{3,1,2,0:T(2,128)(2,1)} %fusion.21), calls=%async_computation.1 | async-start | bytes 1572864 | tf_op jit(solution)/shard_map/all_to_all | solution.py:191
  171.3 44.9 %all-to-all-done.1 = bf16[64,2,6,448]{3,1,2,0:T(2,128)(2,1)S(1)} async-done(((bf16[64,2,6,448]{3,1,2,0:T(2,128)(2,1)}), bf16[64,2,6,448]{3,1,2,0:T(2,128)(2,1)S(1)}, u32[]{:S(2)}, u32[]{:S(2)}) %all-to-all-start.1) | async-done | bytes 688160 | tf_op jit(solution)/shard_map/all_to_all | solution.py:191
  216.2 1.1 convolution_bitcast_fusion
  217.3 0.0 copy-start.3
  217.3 0.6 copy.51
  217.9 0.4 reshape.421
  218.3 0.2 add_convert_fusion
  218.5 0.8 fusion.61
  (24 shorter events, 0.2 us)
Async XLA Ops:
  0.6 13.2 %collective-permute-start = (bf16[32,3584]{1,0:T(8,128)(2,1)}, bf16[32,3584]{1,0:T(8,128)(2,1)S(1)}, u32[]{:S(2)}, u32[]{:S(2)}) collective-permute-start(bf16[32,3584]{1,0:T(8,128)(2,1)} %bitcast.91), channel_id=1, source_target_pairs={{448,0},{0,64},{64,128},{128,192},{192,256},{256,320},{320,384},{3... | collective-permute-start | bytes 688136 | tf_op jit(solution)/shard_map/ppermute | solution.py:14
  4.8 13.8 %collective-permute-start.1 = (bf16[32,3584]{1,0:T(8,128)(2,1)}, bf16[32,3584]{1,0:T(8,128)(2,1)S(1)}, u32[]{:S(2)}, u32[]{:S(2)}) collective-permute-start(bf16[32,3584]{1,0:T(8,128)(2,1)} %bitcast.92), channel_id=1, source_target_pairs={{64,0},{128,64},{192,128},{256,192},{320,256},{384,320},{448,384},... | collective-permute-start | bytes 688136 | tf_op jit(solution)/shard_map/ppermute | solution.py:14
  10.1 9.8 %collective-permute-start.2 = (bf16[48,2048]{1,0:T(8,128)(2,1)}, bf16[48,2048]{1,0:T(8,128)(2,1)S(1)}, u32[]{:S(2)}, u32[]{:S(2)}) collective-permute-start(bf16[48,2048]{1,0:T(8,128)(2,1)} %bitcast.93), channel_id=1, source_target_pairs={{0,0},{1,4},{2,2},{3,6},{4,1},{5,3},{6,5},{7,7},{8,8},{9,12},{10,1... | collective-permute-start | bytes 589832 | tf_op jit(solution)/shard_map/ppermute | solution.py:94
  13.8 0.7 copy-start
  18.6 3.0 %copy-start.2 = (bf16[32,3584]{1,0:T(8,128)(2,1)}, bf16[32,3584]{1,0:T(8,128)(2,1)S(1)}, u32[]{:S(2)}) copy-start(bf16[32,3584]{1,0:T(8,128)(2,1)S(1)} %collective-permute-done.1) | copy-start | bytes 688132
  19.9 1.7 copy-start.4
  21.6 63.1 %all-to-all-start = ((bf16[64,2,6,448]{3,1,2,0:T(2,128)(2,1)}), bf16[64,2,6,448]{3,1,2,0:T(2,128)(2,1)S(1)}, u32[]{:S(2)}, u32[]{:S(2)}) async-start(bf16[64,2,6,448]{3,1,2,0:T(2,128)(2,1)} %copy.47), calls=%async_computation | async-start | bytes 1572864 | tf_op jit(solution)/shard_map/all_to_all | solution.py:113
  91.6 6.6 %collective-permute-start.3 = (f32[192,3072]{1,0:T(8,128)S(1)}, f32[192,3072]{1,0:T(8,128)}, u32[]{:S(2)}, u32[]{:S(2)}) collective-permute-start(f32[192,3072]{1,0:T(8,128)S(1)} %fusion.6), channel_id=1, source_target_pairs={{0,1},{1,0},{2,3},{3,2},{4,5},{5,4},{6,7},{7,6},{8,9},{9,8},{10,11... | collective-permute-start | bytes 7077896 | tf_op jit(solution)/shard_map/ppermute | solution.py:133
  102.1 18.2 %collective-permute-start.4 = (f32[96,3072]{1,0:T(8,128)S(1)}, f32[96,3072]{1,0:T(8,128)}, u32[]{:S(2)}, u32[]{:S(2)}) collective-permute-start(f32[96,3072]{1,0:T(8,128)S(1)} %constant_dynamic-slice_fusion.1), channel_id=1, source_target_pairs={{0,2},{1,5},{2,0},{3,7},{4,6},{5,1},{6,4},{7,3},{8,10},{9,13},{10,... | collective-permute-start | bytes 3538952 | tf_op jit(solution)/shard_map/ppermute | solution.py:140
  121.7 12.0 %copy-start.5 = (bf16[48,2048]{1,0:T(8,128)(2,1)S(1)}, bf16[48,2048]{1,0:T(8,128)(2,1)}, u32[]{:S(2)}) copy-start(bf16[48,2048]{1,0:T(8,128)(2,1)} %copy-done.4) | copy-start | bytes 589828
  121.8 11.9 %collective-permute-start.5 = (f32[48,3072]{1,0:T(8,128)S(1)}, f32[48,3072]{1,0:T(8,128)S(1)}, u32[]{:S(2)}, u32[]{:S(2)}) collective-permute-start(f32[48,3072]{1,0:T(8,128)S(1)} %constant_dynamic-slice_fusion), channel_id=1, source_target_pairs={{0,4},{1,3},{2,6},{3,1},{4,0},{5,7},{6,2},{7,5},{8,12},{9,11},{10,... | collective-permute-start | bytes 1769480 | tf_op jit(solution)/shard_map/ppermute | solution.py:140
  133.9 23.0 %copy-start.9 = (bf16[1,1,1024,448]{2,3,1,0:T(8,128)(2,1)S(1)}, bf16[1,1,1024,448]{2,3,1,0:T(8,128)(2,1)}, u32[]{:S(2)}) copy-start(bf16[1,1,1024,448]{2,3,1,0:T(8,128)(2,1)} %param.16) | copy-start | bytes 2752516
  134.0 8.7 %collective-permute-start.6 = (bf16[48,3072]{1,0:T(8,128)(2,1)S(1)}, bf16[48,3072]{1,0:T(8,128)(2,1)S(1)}, u32[]{:S(2)}, u32[]{:S(2)}) collective-permute-start(bf16[48,3072]{1,0:T(8,128)(2,1)S(1)} %pad_maximum_fusion.2), channel_id=1, source_target_pairs={{0,4},{1,3},{2,6},{3,1},{4,0},{5,7},{6,2},{7,5},{8,12},{9,11},{10,... | collective-permute-start | bytes 884744 | tf_op jit(solution)/shard_map/ppermute | solution.py:156
  142.8 11.8 %collective-permute-start.7 = (bf16[96,3072]{1,0:T(8,128)(2,1)S(1)}, bf16[96,3072]{1,0:T(8,128)(2,1)S(1)}, u32[]{:S(2)}, u32[]{:S(2)}) collective-permute-start(bf16[96,3072]{1,0:T(8,128)(2,1)S(1)} %pad_maximum_fusion.1), channel_id=1, source_target_pairs={{0,2},{1,5},{2,0},{3,7},{4,6},{5,1},{6,4},{7,3},{8,10},{9,13},{10,... | collective-permute-start | bytes 1769480 | tf_op jit(solution)/shard_map/ppermute | solution.py:156
  154.6 5.7 %collective-permute-start.8 = (bf16[192,3072]{1,0:T(8,128)(2,1)S(1)}, bf16[192,3072]{1,0:T(8,128)(2,1)}, u32[]{:S(2)}, u32[]{:S(2)}) collective-permute-start(bf16[192,3072]{1,0:T(8,128)(2,1)S(1)} %pad_maximum_fusion), channel_id=1, source_target_pairs={{0,1},{1,0},{2,3},{3,2},{4,5},{5,4},{6,7},{7,6},{8,9},{9,8},{10,11... | collective-permute-start | bytes 3538952 | tf_op jit(solution)/shard_map/ppermute | solution.py:171
  156.9 3.4 %copy-start.8 = (bf16[1,1,448,2048]{3,2,1,0:T(8,128)(2,1)S(1)}, bf16[1,1,448,2048]{3,2,1,0:T(8,128)(2,1)}, u32[]{:S(2)}) copy-start(bf16[1,1,448,2048]{3,2,1,0:T(8,128)(2,1)} %param.15) | copy-start | bytes 5505028
  164.1 7.2 %copy-start.6 = (f32[1,32,1]{1,2,0:T(1,128)S(1)}, f32[1,32,1]{1,2,0:T(1,128)}, u32[]{:S(2)}) copy-start(f32[1,32,1]{1,2,0:T(1,128)} %param.14) | copy-start | bytes 388
  164.1 7.2 %copy-start.7 = (f32[1,32,1]{1,2,0:T(1,128)S(1)}, f32[1,32,1]{1,2,0:T(1,128)}, u32[]{:S(2)}) copy-start(f32[1,32,1]{1,2,0:T(1,128)} %param.11) | copy-start | bytes 388
  166.6 49.6 %all-to-all-start.1 = ((bf16[64,2,6,448]{3,1,2,0:T(2,128)(2,1)}), bf16[64,2,6,448]{3,1,2,0:T(2,128)(2,1)S(1)}, u32[]{:S(2)}, u32[]{:S(2)}) async-start(bf16[64,2,6,448]{3,1,2,0:T(2,128)(2,1)} %fusion.21), calls=%async_computation.1 | async-start | bytes 1572864 | tf_op jit(solution)/shard_map/all_to_all | solution.py:191
  217.3 1.1 copy-start.1
  217.3 1.1 copy-start.3

commit v13 on v11

--- a/solution.py
+++ b/solution.py
@@ -131,7 +131,7 @@
     bit = own_stage_bit(index, group_size, 0)
     send_part = first_partial((1 - bit) * half, half)
     received = lax.ppermute(send_part, "expert", stage_route(devices, group_size, 0))
-    current = first_partial(bit * half, half) + received
+    current = lax.optimization_barrier(first_partial(bit * half, half)) + received
     for stage in range(1, levels):
         half = current.shape[0] // 2
         bit = own_stage_bit(index, group_size, stage)

time: 220 us -> 218 us (level)
  waiting for transfers between devices: 141 us -> 138 us
  other arithmetic: 4.64 us -> 6.88 us
    ppermute x1, waiting for transfers between devices: 4.62 us -> 1.54 us  [body(): lax.ppermute(send_part, 'expert', stage_route(devices, group_size, 0))]
  transfers between devices with their start and end apart: 11 -> 11, of which waited for: 9 -> 9; matrix products, arithmetic and copies ran while one was open for 2% -> 4% of each run, Pallas kernels for 0% -> 0%
where the time goes in v13:
time: 218 us
  waiting for transfers between devices  138 us (63%)
  starting transfers between devices  46.9 us (22%)
  matrix products  13.2 us (6%)
  local copies, waits for them, and re-layouts  11.7 us (5%)
  other arithmetic  6.88 us (3%)
    all_to_all x1, waiting for transfers between devices, body(): lax.all_to_all(result, 'expert', split_axis=0, concat_axis=0, tiled=True)  44.9 us
    all_to_all x1, waiting for transfers between devices, body(): lax.all_to_all(sent, 'expert', split_axis=0, concat_axis=0, tiled=True)  44.8 us
    ppermute x2, waiting for transfers between devices, body(): lax.ppermute(send_part, 'expert', stage_route(devices, group_size, stage))  25.6 us
    all_to_all x1, starting transfers between devices, body(): lax.all_to_all(sent, 'expert', split_axis=0, concat_axis=0, tiled=True)  18.2 us
    ppermute x2, waiting for transfers between devices, body(): lax.ppermute(current, 'expert', stage_route(devices, group_size, stage))  16 us
    ppermute x2, starting transfers between devices, shifted(): return lax.ppermute(block, axis, route)  9.46 us
    dot_general x2, matrix products, first_partial(): return jnp.dot(part, both_proj, preferred_element_type=jnp.float32)  6.13 us
    ppermute x2, waiting for transfers between devices, shifted(): return lax.ppermute(block, axis, route)  4.93 us
  transfers between devices with their start and end apart: 11, of which 9 were waited for; matrix products, arithmetic and copies ran while one was open for 4% of the time, Pallas kernels for 0%

profile of v13, /device:TPU:8, one launch (start us, length us, event | category | flops | bytes accessed | tf_op | source)
XLA Modules:
  0.0 217.6 jit_solution(7754634964985099580)
XLA Ops:
  0.6 4.2 %collective-permute-start = (bf16[32,3584]{1,0:T(8,128)(2,1)}, bf16[32,3584]{1,0:T(8,128)(2,1)S(1)}, u32[]{:S(2)}, u32[]{:S(2)}) collective-permute-start(bf16[32,3584]{1,0:T(8,128)(2,1)} %bitcast.92), channel_id=1, source_target_pairs={{448,0},{0,64},{64,128},{128,192},{192,256},{256,320},{320,384},{3... | collective-permute-start | bytes 688136 | tf_op jit(solution)/shard_map/ppermute | solution.py:14
  4.8 5.3 %collective-permute-start.1 = (bf16[32,3584]{1,0:T(8,128)(2,1)}, bf16[32,3584]{1,0:T(8,128)(2,1)S(1)}, u32[]{:S(2)}, u32[]{:S(2)}) collective-permute-start(bf16[32,3584]{1,0:T(8,128)(2,1)} %bitcast.93), channel_id=1, source_target_pairs={{64,0},{128,64},{192,128},{256,192},{320,256},{384,320},{448,384},... | collective-permute-start | bytes 688136 | tf_op jit(solution)/shard_map/ppermute | solution.py:14
  10.1 1.6 collective-permute-start.2
  11.7 0.7 pad_add_fusion
  12.4 0.2 convert_reduce_fusion
  12.6 1.2 collective-permute-done
  13.8 0.7 copy-done
  14.5 0.3 stack.97
  14.8 0.1 copy.44
  14.9 3.7 %collective-permute-done.1 = bf16[32,3584]{1,0:T(8,128)(2,1)S(1)} collective-permute-done((bf16[32,3584]{1,0:T(8,128)(2,1)}, bf16[32,3584]{1,0:T(8,128)(2,1)S(1)}, u32[]{:S(2)}, u32[]{:S(2)}) %collective-permute-start.1) | collective-permute-done | bytes 229408 | tf_op jit(solution)/shard_map/ppermute | solution.py:14
  18.6 0.3 stack.98
  18.9 0.1 copy.45
  19.0 0.4 fusion.7
  19.4 0.4 copy.62
  19.9 1.7 copy.47
  21.6 18.2 %all-to-all-start = ((bf16[64,2,6,448]{3,1,2,0:T(2,128)(2,1)}), bf16[64,2,6,448]{3,1,2,0:T(2,128)(2,1)S(1)}, u32[]{:S(2)}, u32[]{:S(2)}) async-start(bf16[64,2,6,448]{3,1,2,0:T(2,128)(2,1)} %copy.47), calls=%async_computation | async-start | bytes 1572864 | tf_op jit(solution)/shard_map/all_to_all | solution.py:113
  39.9 44.8 %all-to-all-done = bf16[64,2,6,448]{3,1,2,0:T(2,128)(2,1)S(1)} async-done(((bf16[64,2,6,448]{3,1,2,0:T(2,128)(2,1)}), bf16[64,2,6,448]{3,1,2,0:T(2,128)(2,1)S(1)}, u32[]{:S(2)}, u32[]{:S(2)}) %all-to-all-start) | async-done | bytes 688160 | tf_op jit(solution)/shard_map/all_to_all | solution.py:113
  84.7 3.3 %slice_reduce_fusion = (bf16[64,6,448]{2,1,0:T(8,128)(2,1)S(1)}, bf16[64,6,448]{2,1,0:T(8,128)(2,1)S(1)}) fusion(bf16[64,2,6,448]{3,1,2,0:T(2,128)(2,1)S(1)} %all-to-all-done), kind=kLoop, calls=%fused_computation.27 | loop fusion | bytes 1376256 | tf_op jit(solution)/shard_map/slice | solution.py:115
  88.0 0.2 reshape_squeeze.6
  88.3 0.2 reshape_squeeze.7
  88.5 3.1 %fusion.3 = f32[192,3072]{1,0:T(8,128)S(1)} fusion(bf16[448,1024]{1,0:T(8,128)(2,1)} %bitcast.90, bf16[448,2048]{1,0:T(8,128)(2,1)} %bitcast.88, s32[]{:T(128)S(6)} %select_n.113, bf16[384,448]{1,0:T(8,128)(2,1)S(1)} %reshape_squeeze.6, bf16[384,448]{1,0:T(8,128)(2,1)S(1)} %reshape_squeeze.7), kind=kOutput, calls=%fused_computation.6 | convolution fusion | flops 1079672832 | bytes 5799940 | tf_op jit(solution)/shard_map/dot_general | solution.py:128
  91.6 1.9 collective-permute-start.3
  93.5 3.1 %fusion.5 = f32[192,3072]{1,0:T(8,128)S(1)} fusion(bf16[448,1024]{1,0:T(8,128)(2,1)} %bitcast.91, bf16[448,2048]{1,0:T(8,128)(2,1)} %bitcast.89, s32[]{:T(128)S(6)} %select_n.112, bf16[384,448]{1,0:T(8,128)(2,1)S(1)} %reshape_squeeze.6, bf16[384,448]{1,0:T(8,128)(2,1)S(1)} %reshape_squeeze.7), kind=kOutput, calls=%fused_computation.7 | convolution fusion | flops 1079672832 | bytes 5799940 | tf_op jit(solution)/shard_map/dot_general | solution.py:128
  96.6 1.5 collective-permute-done.3
  98.2 2.1 add.139
  100.3 0.1 constant_dynamic-slice_fusion.1
  100.4 2.4 %collective-permute-start.4 = (f32[96,3072]{1,0:T(8,128)S(1)}, f32[96,3072]{1,0:T(8,128)}, u32[]{:S(2)}, u32[]{:S(2)}) collective-permute-start(f32[96,3072]{1,0:T(8,128)S(1)} %constant_dynamic-slice_fusion.1), channel_id=1, source_target_pairs={{0,2},{1,5},{2,0},{3,7},{4,6},{5,1},{6,4},{7,3},{8,10},{9,13},{10,... | collective-permute-start | bytes 3538952 | tf_op jit(solution)/shard_map/ppermute | solution.py:140
  102.8 15.7 %collective-permute-done.4 = f32[96,3072]{1,0:T(8,128)} collective-permute-done((f32[96,3072]{1,0:T(8,128)S(1)}, f32[96,3072]{1,0:T(8,128)}, u32[]{:S(2)}, u32[]{:S(2)}) %collective-permute-start.4) | collective-permute-done | bytes 1179680 | tf_op jit(solution)/shard_map/ppermute | solution.py:140
  118.6 1.5 dynamic-slice_add_fusion
  120.1 2.1 collective-permute-start.5
  122.2 9.8 %collective-permute-done.5 = f32[48,3072]{1,0:T(8,128)S(1)} collective-permute-done((f32[48,3072]{1,0:T(8,128)S(1)}, f32[48,3072]{1,0:T(8,128)S(1)}, u32[]{:S(2)}, u32[]{:S(2)}) %collective-permute-start.5) | collective-permute-done | bytes 589856 | tf_op jit(solution)/shard_map/ppermute | solution.py:140
  132.0 0.1 dynamic-slice_add_fusion.1
  132.1 0.2 fusion.31
  132.3 1.9 collective-permute-start.6
  134.2 6.7 %collective-permute-done.6 = bf16[48,3072]{1,0:T(8,128)(2,1)S(1)} collective-permute-done((bf16[48,3072]{1,0:T(8,128)(2,1)S(1)}, bf16[48,3072]{1,0:T(8,128)(2,1)S(1)}, u32[]{:S(2)}, u32[]{:S(2)}) %collective-permute-start.6) | collective-permute-done | bytes 294944 | tf_op jit(solution)/shard_map/ppermute | solution.py:156
  141.0 0.0 copy-start.8
  141.0 2.6 %collective-permute-start.7 = (bf16[96,3072]{1,0:T(8,128)(2,1)S(1)}, bf16[96,3072]{1,0:T(8,128)(2,1)S(1)}, u32[]{:S(2)}, u32[]{:S(2)}) collective-permute-start(bf16[96,3072]{1,0:T(8,128)(2,1)S(1)} %pad_maximum_fusion.1), channel_id=1, source_target_pairs={{0,2},{1,5},{2,0},{3,7},{4,6},{5,1},{6,4},{7,3},{8,10},{9,13},{10,... | collective-permute-start | bytes 1769480 | tf_op jit(solution)/shard_map/ppermute | solution.py:156
  143.6 9.3 %collective-permute-done.7 = bf16[96,3072]{1,0:T(8,128)(2,1)S(1)} collective-permute-done((bf16[96,3072]{1,0:T(8,128)(2,1)S(1)}, bf16[96,3072]{1,0:T(8,128)(2,1)S(1)}, u32[]{:S(2)}, u32[]{:S(2)}) %collective-permute-start.7) | collective-permute-done | bytes 589856 | tf_op jit(solution)/shard_map/ppermute | solution.py:156
  152.9 0.1 pad_maximum_fusion
  153.0 2.1 collective-permute-start.8
  155.1 0.1 stack.96
  155.2 0.1 broadcast_in_dim.21
  155.3 0.1 broadcast_in_dim.22
  155.4 0.1 stack.115
  155.5 1.6 fusion.10
  157.2 0.0 copy-start.9
  157.2 0.7 fusion.8
  157.9 0.5 copy-done.9
  158.4 1.5 fusion.11
  159.8 1.8 fusion.9
  161.6 0.1 maximum_maximum_fusion
  161.8 0.6 gather_fusion
  162.4 0.8 copy.48
  163.2 0.0 copy-start.6
  163.2 0.0 copy-start.7
  163.2 1.7 fusion.17
  164.9 4.6 %all-to-all-start.1 = ((bf16[64,2,6,448]{3,1,2,0:T(2,128)(2,1)}), bf16[64,2,6,448]{3,1,2,0:T(2,128)(2,1)S(1)}, u32[]{:S(2)}, u32[]{:S(2)}) async-start(bf16[64,2,6,448]{3,1,2,0:T(2,128)(2,1)} %fusion.17), calls=%async_computation.1 | async-start | bytes 1572864 | tf_op jit(solution)/shard_map/all_to_all | solution.py:189
  169.6 44.9 %all-to-all-done.1 = bf16[64,2,6,448]{3,1,2,0:T(2,128)(2,1)S(1)} async-done(((bf16[64,2,6,448]{3,1,2,0:T(2,128)(2,1)}), bf16[64,2,6,448]{3,1,2,0:T(2,128)(2,1)S(1)}, u32[]{:S(2)}, u32[]{:S(2)}) %all-to-all-start.1) | async-done | bytes 688160 | tf_op jit(solution)/shard_map/all_to_all | solution.py:189
  214.5 1.1 convolution_bitcast_fusion
  215.5 0.0 copy-start.3
  215.5 0.6 copy.51
  216.2 0.4 reshape.421
  216.6 0.2 add_convert_fusion
  216.8 0.8 fusion.55
  (25 shorter events, 0.2 us)
Async XLA Ops:
  0.6 13.2 %collective-permute-start = (bf16[32,3584]{1,0:T(8,128)(2,1)}, bf16[32,3584]{1,0:T(8,128)(2,1)S(1)}, u32[]{:S(2)}, u32[]{:S(2)}) collective-permute-start(bf16[32,3584]{1,0:T(8,128)(2,1)} %bitcast.92), channel_id=1, source_target_pairs={{448,0},{0,64},{64,128},{128,192},{192,256},{256,320},{320,384},{3... | collective-permute-start | bytes 688136 | tf_op jit(solution)/shard_map/ppermute | solution.py:14
  4.8 13.8 %collective-permute-start.1 = (bf16[32,3584]{1,0:T(8,128)(2,1)}, bf16[32,3584]{1,0:T(8,128)(2,1)S(1)}, u32[]{:S(2)}, u32[]{:S(2)}) collective-permute-start(bf16[32,3584]{1,0:T(8,128)(2,1)} %bitcast.93), channel_id=1, source_target_pairs={{64,0},{128,64},{192,128},{256,192},{320,256},{384,320},{448,384},... | collective-permute-start | bytes 688136 | tf_op jit(solution)/shard_map/ppermute | solution.py:14
  10.1 9.8 %collective-permute-start.2 = (bf16[48,2048]{1,0:T(8,128)(2,1)}, bf16[48,2048]{1,0:T(8,128)(2,1)S(1)}, u32[]{:S(2)}, u32[]{:S(2)}) collective-permute-start(bf16[48,2048]{1,0:T(8,128)(2,1)} %bitcast.94), channel_id=1, source_target_pairs={{0,0},{1,4},{2,2},{3,6},{4,1},{5,3},{6,5},{7,7},{8,8},{9,12},{10,1... | collective-permute-start | bytes 589832 | tf_op jit(solution)/shard_map/ppermute | solution.py:94
  13.8 0.7 copy-start
  18.6 1.3 copy-start.2
  19.9 1.7 copy-start.4
  21.6 63.1 %all-to-all-start = ((bf16[64,2,6,448]{3,1,2,0:T(2,128)(2,1)}), bf16[64,2,6,448]{3,1,2,0:T(2,128)(2,1)S(1)}, u32[]{:S(2)}, u32[]{:S(2)}) async-start(bf16[64,2,6,448]{3,1,2,0:T(2,128)(2,1)} %copy.47), calls=%async_computation | async-start | bytes 1572864 | tf_op jit(solution)/shard_map/all_to_all | solution.py:113
  91.6 6.6 %collective-permute-start.3 = (f32[192,3072]{1,0:T(8,128)S(1)}, f32[192,3072]{1,0:T(8,128)}, u32[]{:S(2)}, u32[]{:S(2)}) collective-permute-start(f32[192,3072]{1,0:T(8,128)S(1)} %fusion.3), channel_id=1, source_target_pairs={{0,1},{1,0},{2,3},{3,2},{4,5},{5,4},{6,7},{7,6},{8,9},{9,8},{10,11... | collective-permute-start | bytes 7077896 | tf_op jit(solution)/shard_map/ppermute | solution.py:133
  100.4 18.2 %collective-permute-start.4 = (f32[96,3072]{1,0:T(8,128)S(1)}, f32[96,3072]{1,0:T(8,128)}, u32[]{:S(2)}, u32[]{:S(2)}) collective-permute-start(f32[96,3072]{1,0:T(8,128)S(1)} %constant_dynamic-slice_fusion.1), channel_id=1, source_target_pairs={{0,2},{1,5},{2,0},{3,7},{4,6},{5,1},{6,4},{7,3},{8,10},{9,13},{10,... | collective-permute-start | bytes 3538952 | tf_op jit(solution)/shard_map/ppermute | solution.py:140
  120.1 12.0 %copy-start.5 = (bf16[48,2048]{1,0:T(8,128)(2,1)S(1)}, bf16[48,2048]{1,0:T(8,128)(2,1)}, u32[]{:S(2)}) copy-start(bf16[48,2048]{1,0:T(8,128)(2,1)} %copy-done.4) | copy-start | bytes 589828
  120.1 11.9 %collective-permute-start.5 = (f32[48,3072]{1,0:T(8,128)S(1)}, f32[48,3072]{1,0:T(8,128)S(1)}, u32[]{:S(2)}, u32[]{:S(2)}) collective-permute-start(f32[48,3072]{1,0:T(8,128)S(1)} %constant_dynamic-slice_fusion), channel_id=1, source_target_pairs={{0,4},{1,3},{2,6},{3,1},{4,0},{5,7},{6,2},{7,5},{8,12},{9,11},{10,... | collective-permute-start | bytes 1769480 | tf_op jit(solution)/shard_map/ppermute | solution.py:140
  132.3 8.6 %collective-permute-start.6 = (bf16[48,3072]{1,0:T(8,128)(2,1)S(1)}, bf16[48,3072]{1,0:T(8,128)(2,1)S(1)}, u32[]{:S(2)}, u32[]{:S(2)}) collective-permute-start(bf16[48,3072]{1,0:T(8,128)(2,1)S(1)} %pad_maximum_fusion.2), channel_id=1, source_target_pairs={{0,4},{1,3},{2,6},{3,1},{4,0},{5,7},{6,2},{7,5},{8,12},{9,11},{10,... | collective-permute-start | bytes 884744 | tf_op jit(solution)/shard_map/ppermute | solution.py:156
  141.0 16.2 %copy-start.8 = (bf16[1,1,448,2048]{3,2,1,0:T(8,128)(2,1)S(1)}, bf16[1,1,448,2048]{3,2,1,0:T(8,128)(2,1)}, u32[]{:S(2)}) copy-start(bf16[1,1,448,2048]{3,2,1,0:T(8,128)(2,1)} %param.15) | copy-start | bytes 5505028
  141.0 11.9 %collective-permute-start.7 = (bf16[96,3072]{1,0:T(8,128)(2,1)S(1)}, bf16[96,3072]{1,0:T(8,128)(2,1)S(1)}, u32[]{:S(2)}, u32[]{:S(2)}) collective-permute-start(bf16[96,3072]{1,0:T(8,128)(2,1)S(1)} %pad_maximum_fusion.1), channel_id=1, source_target_pairs={{0,2},{1,5},{2,0},{3,7},{4,6},{5,1},{6,4},{7,3},{8,10},{9,13},{10,... | collective-permute-start | bytes 1769480 | tf_op jit(solution)/shard_map/ppermute | solution.py:156
  153.0 4.9 %collective-permute-start.8 = (bf16[192,3072]{1,0:T(8,128)(2,1)S(1)}, bf16[192,3072]{1,0:T(8,128)(2,1)}, u32[]{:S(2)}, u32[]{:S(2)}) collective-permute-start(bf16[192,3072]{1,0:T(8,128)(2,1)S(1)} %pad_maximum_fusion), channel_id=1, source_target_pairs={{0,1},{1,0},{2,3},{3,2},{4,5},{5,4},{6,7},{7,6},{8,9},{9,8},{10,11... | collective-permute-start | bytes 3538952 | tf_op jit(solution)/shard_map/ppermute | solution.py:169
  157.2 1.2 copy-start.9
  163.2 6.3 %copy-start.6 = (f32[1,32,1]{1,2,0:T(1,128)S(1)}, f32[1,32,1]{1,2,0:T(1,128)}, u32[]{:S(2)}) copy-start(f32[1,32,1]{1,2,0:T(1,128)} %param.14) | copy-start | bytes 388
  163.2 6.3 %copy-start.7 = (f32[1,32,1]{1,2,0:T(1,128)S(1)}, f32[1,32,1]{1,2,0:T(1,128)}, u32[]{:S(2)}) copy-start(f32[1,32,1]{1,2,0:T(1,128)} %param.11) | copy-start | bytes 388
  164.9 49.6 %all-to-all-start.1 = ((bf16[64,2,6,448]{3,1,2,0:T(2,128)(2,1)}), bf16[64,2,6,448]{3,1,2,0:T(2,128)(2,1)S(1)}, u32[]{:S(2)}, u32[]{:S(2)}) async-start(bf16[64,2,6,448]{3,1,2,0:T(2,128)(2,1)} %fusion.17), calls=%async_computation.1 | async-start | bytes 1572864 | tf_op jit(solution)/shard_map/all_to_all | solution.py:189
  215.5 1.1 copy-start.1
  215.5 1.1 copy-start.3

commit v14 on v13

--- a/solution.py
+++ b/solution.py
@@ -129,7 +129,17 @@
 
     half = rows_down.shape[0] // 2
     bit = own_stage_bit(index, group_size, 0)
-    send_part = first_partial((1 - bit) * half, half)
+    sent_down = lax.dynamic_slice_in_dim(rows_down, (1 - bit) * half, half, axis=0)
+    sent_up = lax.dynamic_slice_in_dim(rows_up, (1 - bit) * half, half, axis=0)
+    send_part = jnp.concatenate(
+        [
+            jnp.dot(sent_down, proj_in, preferred_element_type=jnp.float32),
+            lax.dot_general(
+                sent_up, proj_out, (((1,), (1,)), ((), ())), preferred_element_type=jnp.float32
+            ),
+        ],
+        axis=1,
+    )
     received = lax.ppermute(send_part, "expert", stage_route(devices, group_size, 0))
     current = lax.optimization_barrier(first_partial(bit * half, half)) + received
     for stage in range(1, levels):

time: 218 us -> 217 us (level)
    dot_general x2 -> x1, matrix products: 6.13 us -> 3.09 us  [first_partial(): return jnp.dot(part, both_proj, preferred_element_type=jnp.float32)]
    dot_general x0 -> x2, matrix products: none -> 2.6 us  [the longest x1 2.23 us: body(): jnp.dot(sent_down, proj_in, preferred_element_type=jnp.float32)]
where the time goes in v14:
time: 217 us
  waiting for transfers between devices  138 us (64%)
  starting transfers between devices  46.9 us (22%)
  matrix products  12.8 us (6%)
  local copies, waits for them, and re-layouts  11.2 us (5%)
  other arithmetic  6.71 us (3%)
    all_to_all x1, waiting for transfers between devices, body(): lax.all_to_all(result, 'expert', split_axis=0, concat_axis=0, tiled=True)  44.9 us
    all_to_all x1, waiting for transfers between devices, body(): lax.all_to_all(sent, 'expert', split_axis=0, concat_axis=0, tiled=True)  44.8 us
    ppermute x2, waiting for transfers between devices, body(): lax.ppermute(send_part, 'expert', stage_route(devices, group_size, stage))  25.6 us
    all_to_all x1, starting transfers between devices, body(): lax.all_to_all(sent, 'expert', split_axis=0, concat_axis=0, tiled=True)  18.2 us
    ppermute x2, waiting for transfers between devices, body(): lax.ppermute(current, 'expert', stage_route(devices, group_size, stage))  16 us
    ppermute x2, starting transfers between devices, shifted(): return lax.ppermute(block, axis, route)  9.46 us
    ppermute x2, waiting for transfers between devices, shifted(): return lax.ppermute(block, axis, route)  4.93 us
    all_to_all x1, starting transfers between devices, body(): lax.all_to_all(result, 'expert', split_axis=0, concat_axis=0, tiled=True)  4.62 us
  transfers between devices with their start and end apart: 11, of which 9 were waited for; matrix products, arithmetic and copies ran while one was open for 4% of the time, Pallas kernels for 0%

profile of v14, /device:TPU:8, one launch (start us, length us, event | category | flops | bytes accessed | tf_op | source)
XLA Modules:
  0.0 216.6 jit_solution(17508030234187640629)
XLA Ops:
  0.6 4.2 %collective-permute-start = (bf16[32,3584]{1,0:T(8,128)(2,1)}, bf16[32,3584]{1,0:T(8,128)(2,1)S(1)}, u32[]{:S(2)}, u32[]{:S(2)}) collective-permute-start(bf16[32,3584]{1,0:T(8,128)(2,1)} %bitcast.94), channel_id=1, source_target_pairs={{448,0},{0,64},{64,128},{128,192},{192,256},{256,320},{320,384},{3... | collective-permute-start | bytes 688136 | tf_op jit(solution)/shard_map/ppermute | solution.py:14
  4.8 5.3 %collective-permute-start.1 = (bf16[32,3584]{1,0:T(8,128)(2,1)}, bf16[32,3584]{1,0:T(8,128)(2,1)S(1)}, u32[]{:S(2)}, u32[]{:S(2)}) collective-permute-start(bf16[32,3584]{1,0:T(8,128)(2,1)} %bitcast.95), channel_id=1, source_target_pairs={{64,0},{128,64},{192,128},{256,192},{320,256},{384,320},{448,384},... | collective-permute-start | bytes 688136 | tf_op jit(solution)/shard_map/ppermute | solution.py:14
  10.1 1.6 collective-permute-start.2
  11.7 0.7 pad_add_fusion
  12.4 0.2 convert_reduce_fusion
  12.6 1.2 collective-permute-done
  13.8 0.7 copy-done.1
  14.5 0.3 stack.97
  14.8 0.1 copy.44
  14.9 3.7 %collective-permute-done.1 = bf16[32,3584]{1,0:T(8,128)(2,1)S(1)} collective-permute-done((bf16[32,3584]{1,0:T(8,128)(2,1)}, bf16[32,3584]{1,0:T(8,128)(2,1)S(1)}, u32[]{:S(2)}, u32[]{:S(2)}) %collective-permute-start.1) | collective-permute-done | bytes 229408 | tf_op jit(solution)/shard_map/ppermute | solution.py:14
  18.6 0.3 stack.98
  18.9 0.1 copy.45
  19.0 0.4 fusion.10
  19.4 0.4 copy.62
  19.9 1.7 copy.47
  21.6 18.2 %all-to-all-start = ((bf16[64,2,6,448]{3,1,2,0:T(2,128)(2,1)}), bf16[64,2,6,448]{3,1,2,0:T(2,128)(2,1)S(1)}, u32[]{:S(2)}, u32[]{:S(2)}) async-start(bf16[64,2,6,448]{3,1,2,0:T(2,128)(2,1)} %copy.47), calls=%async_computation | async-start | bytes 1572864 | tf_op jit(solution)/shard_map/all_to_all | solution.py:113
  39.9 44.8 %all-to-all-done = bf16[64,2,6,448]{3,1,2,0:T(2,128)(2,1)S(1)} async-done(((bf16[64,2,6,448]{3,1,2,0:T(2,128)(2,1)}), bf16[64,2,6,448]{3,1,2,0:T(2,128)(2,1)S(1)}, u32[]{:S(2)}, u32[]{:S(2)}) %all-to-all-start) | async-done | bytes 688160 | tf_op jit(solution)/shard_map/all_to_all | solution.py:113
  84.7 3.3 %slice_reduce_fusion = (bf16[64,6,448]{2,1,0:T(8,128)(2,1)S(1)}, bf16[64,6,448]{2,1,0:T(8,128)(2,1)S(1)}) fusion(bf16[64,2,6,448]{3,1,2,0:T(2,128)(2,1)S(1)} %all-to-all-done), kind=kLoop, calls=%fused_computation.33 | loop fusion | bytes 1376256 | tf_op jit(solution)/shard_map/slice | solution.py:115
  88.0 0.2 reshape_squeeze.6
  88.3 0.2 reshape_squeeze.7
  88.5 0.0 copy-start.5
  88.5 2.2 %fusion.39 = f32[192,2048]{1,0:T(8,128)S(1)} fusion(bf16[384,448]{1,0:T(8,128)(2,1)S(1)} %reshape_squeeze.6, s32[]{:T(128)S(6)} %select_n.114, bf16[1,1,448,2048]{3,2,1,0:T(8,128)(2,1)} %param.15), kind=kOutput, calls=%fused_computation.64 | convolution fusion | flops 352321536 | bytes 3604484 | tf_op jit(solution)/shard_map/dot_general | solution.py:136
  90.8 0.4 fusion.16
  91.2 0.2 pad_maximum_fusion
  91.3 1.9 collective-permute-start.3
  93.3 3.1 %fusion.3 = f32[192,3072]{1,0:T(8,128)S(1)} fusion(bf16[448,1024]{1,0:T(8,128)(2,1)S(1)} %bitcast.90, bf16[448,2048]{1,0:T(8,128)(2,1)} %bitcast.87, s32[]{:T(128)S(6)} %select_n.113, bf16[384,448]{1,0:T(8,128)(2,1)} %copy-done.8, bf16[384,448]{1,0:T(8,128)(2,1)} %copy-done.7), kind=kOutput, calls=%fused_computation.6 | convolution fusion | flops 1079672832 | bytes 5799940 | tf_op jit(solution)/shard_map/dot_general | solution.py:128
  96.4 1.5 collective-permute-done.3
  97.9 1.9 add.140
  99.8 0.1 constant_dynamic-slice_fusion.1
  99.9 2.4 %collective-permute-start.4 = (f32[96,3072]{1,0:T(8,128)S(1)}, f32[96,3072]{1,0:T(8,128)}, u32[]{:S(2)}, u32[]{:S(2)}) collective-permute-start(f32[96,3072]{1,0:T(8,128)S(1)} %constant_dynamic-slice_fusion.1), channel_id=1, source_target_pairs={{0,2},{1,5},{2,0},{3,7},{4,6},{5,1},{6,4},{7,3},{8,10},{9,13},{10,... | collective-permute-start | bytes 3538952 | tf_op jit(solution)/shard_map/ppermute | solution.py:150
  102.4 15.7 %collective-permute-done.4 = f32[96,3072]{1,0:T(8,128)} collective-permute-done((f32[96,3072]{1,0:T(8,128)S(1)}, f32[96,3072]{1,0:T(8,128)}, u32[]{:S(2)}, u32[]{:S(2)}) %collective-permute-start.4) | collective-permute-done | bytes 1179680 | tf_op jit(solution)/shard_map/ppermute | solution.py:150
  118.1 1.4 dynamic-slice_add_fusion
  119.6 2.1 collective-permute-start.5
  121.6 9.8 %collective-permute-done.5 = f32[48,3072]{1,0:T(8,128)S(1)} collective-permute-done((f32[48,3072]{1,0:T(8,128)S(1)}, f32[48,3072]{1,0:T(8,128)S(1)}, u32[]{:S(2)}, u32[]{:S(2)}) %collective-permute-start.5) | collective-permute-done | bytes 589856 | tf_op jit(solution)/shard_map/ppermute | solution.py:150
  131.5 0.1 dynamic-slice_add_fusion.1
  131.6 0.2 fusion.34
  131.8 1.9 collective-permute-start.6
  133.7 6.7 %collective-permute-done.6 = bf16[48,3072]{1,0:T(8,128)(2,1)S(1)} collective-permute-done((bf16[48,3072]{1,0:T(8,128)(2,1)S(1)}, bf16[48,3072]{1,0:T(8,128)(2,1)S(1)}, u32[]{:S(2)}, u32[]{:S(2)}) %collective-permute-start.6) | collective-permute-done | bytes 294944 | tf_op jit(solution)/shard_map/ppermute | solution.py:166
  140.4 0.0 copy-start
  140.4 2.6 %collective-permute-start.7 = (bf16[96,3072]{1,0:T(8,128)(2,1)S(1)}, bf16[96,3072]{1,0:T(8,128)(2,1)S(1)}, u32[]{:S(2)}, u32[]{:S(2)}) collective-permute-start(bf16[96,3072]{1,0:T(8,128)(2,1)S(1)} %pad_maximum_fusion.2), channel_id=1, source_target_pairs={{0,2},{1,5},{2,0},{3,7},{4,6},{5,1},{6,4},{7,3},{8,10},{9,13},{10,... | collective-permute-start | bytes 1769480 | tf_op jit(solution)/shard_map/ppermute | solution.py:166
  143.0 9.3 %collective-permute-done.7 = bf16[96,3072]{1,0:T(8,128)(2,1)S(1)} collective-permute-done((bf16[96,3072]{1,0:T(8,128)(2,1)S(1)}, bf16[96,3072]{1,0:T(8,128)(2,1)S(1)}, u32[]{:S(2)}, u32[]{:S(2)}) %collective-permute-start.7) | collective-permute-done | bytes 589856 | tf_op jit(solution)/shard_map/ppermute | solution.py:166
  152.3 0.1 pad_maximum_fusion.1
  152.4 2.1 collective-permute-start.8
  154.6 0.1 stack.96
  154.7 0.1 broadcast_in_dim.21
  154.8 0.1 broadcast_in_dim.22
  154.9 0.1 stack.115
  155.0 1.6 fusion.13
  156.6 0.7 fusion.11
  157.3 0.0 copy-start.6
  157.3 1.9 fusion.12
  159.2 1.5 fusion.14
  160.7 0.1 maximum_maximum_fusion
  160.8 0.6 gather_fusion
  161.4 0.8 copy.48
  162.2 0.0 copy-start.11
  162.2 1.7 fusion.22
  163.9 4.6 %all-to-all-start.1 = ((bf16[64,2,6,448]{3,1,2,0:T(2,128)(2,1)}), bf16[64,2,6,448]{3,1,2,0:T(2,128)(2,1)S(1)}, u32[]{:S(2)}, u32[]{:S(2)}) async-start(bf16[64,2,6,448]{3,1,2,0:T(2,128)(2,1)} %fusion.22), calls=%async_computation.1 | async-start | bytes 1572864 | tf_op jit(solution)/shard_map/all_to_all | solution.py:199
  168.6 44.9 %all-to-all-done.1 = bf16[64,2,6,448]{3,1,2,0:T(2,128)(2,1)S(1)} async-done(((bf16[64,2,6,448]{3,1,2,0:T(2,128)(2,1)}), bf16[64,2,6,448]{3,1,2,0:T(2,128)(2,1)S(1)}, u32[]{:S(2)}, u32[]{:S(2)}) %all-to-all-start.1) | async-done | bytes 688160 | tf_op jit(solution)/shard_map/all_to_all | solution.py:199
  213.5 1.1 convolution_bitcast_fusion
  214.6 0.6 copy.51
  215.2 0.4 reshape.421
  215.6 0.2 add_convert_fusion
  215.8 0.8 fusion.60
  (33 shorter events, 0.2 us)
Async XLA Ops:
  0.6 13.2 %collective-permute-start = (bf16[32,3584]{1,0:T(8,128)(2,1)}, bf16[32,3584]{1,0:T(8,128)(2,1)S(1)}, u32[]{:S(2)}, u32[]{:S(2)}) collective-permute-start(bf16[32,3584]{1,0:T(8,128)(2,1)} %bitcast.94), channel_id=1, source_target_pairs={{448,0},{0,64},{64,128},{128,192},{192,256},{256,320},{320,384},{3... | collective-permute-start | bytes 688136 | tf_op jit(solution)/shard_map/ppermute | solution.py:14
  4.8 13.8 %collective-permute-start.1 = (bf16[32,3584]{1,0:T(8,128)(2,1)}, bf16[32,3584]{1,0:T(8,128)(2,1)S(1)}, u32[]{:S(2)}, u32[]{:S(2)}) collective-permute-start(bf16[32,3584]{1,0:T(8,128)(2,1)} %bitcast.95), channel_id=1, source_target_pairs={{64,0},{128,64},{192,128},{256,192},{320,256},{384,320},{448,384},... | collective-permute-start | bytes 688136 | tf_op jit(solution)/shard_map/ppermute | solution.py:14
  10.1 9.8 %collective-permute-start.2 = (bf16[48,2048]{1,0:T(8,128)(2,1)}, bf16[48,2048]{1,0:T(8,128)(2,1)S(1)}, u32[]{:S(2)}, u32[]{:S(2)}) collective-permute-start(bf16[48,2048]{1,0:T(8,128)(2,1)} %bitcast.96), channel_id=1, source_target_pairs={{0,0},{1,4},{2,2},{3,6},{4,1},{5,3},{6,5},{7,7},{8,8},{9,12},{10,1... | collective-permute-start | bytes 589832 | tf_op jit(solution)/shard_map/ppermute | solution.py:94
  13.8 0.7 copy-start.1
  18.6 1.3 copy-start.3
  19.9 1.7 copy-start.9
  21.6 63.1 %all-to-all-start = ((bf16[64,2,6,448]{3,1,2,0:T(2,128)(2,1)}), bf16[64,2,6,448]{3,1,2,0:T(2,128)(2,1)S(1)}, u32[]{:S(2)}, u32[]{:S(2)}) async-start(bf16[64,2,6,448]{3,1,2,0:T(2,128)(2,1)} %copy.47), calls=%async_computation | async-start | bytes 1572864 | tf_op jit(solution)/shard_map/all_to_all | solution.py:113
  88.3 2.5 %copy-start.8 = (bf16[384,448]{1,0:T(8,128)(2,1)}, bf16[384,448]{1,0:T(8,128)(2,1)S(1)}, u32[]{:S(2)}) copy-start(bf16[384,448]{1,0:T(8,128)(2,1)S(1)} %reshape_squeeze.6) | copy-start | bytes 1032196
  88.5 2.3 %copy-start.7 = (bf16[384,448]{1,0:T(8,128)(2,1)}, bf16[384,448]{1,0:T(8,128)(2,1)S(1)}, u32[]{:S(2)}) copy-start(bf16[384,448]{1,0:T(8,128)(2,1)S(1)} %reshape_squeeze.7) | copy-start | bytes 1032196
  88.5 2.3 %copy-start.5 = (bf16[1,1,1024,448]{2,3,1,0:T(8,128)(2,1)S(1)}, bf16[1,1,1024,448]{2,3,1,0:T(8,128)(2,1)}, u32[]{:S(2)}) copy-start(bf16[1,1,1024,448]{2,3,1,0:T(8,128)(2,1)} %param.16) | copy-start | bytes 2752516
  91.3 6.6 %collective-permute-start.3 = (f32[192,3072]{1,0:T(8,128)S(1)}, f32[192,3072]{1,0:T(8,128)}, u32[]{:S(2)}, u32[]{:S(2)}) collective-permute-start(f32[192,3072]{1,0:T(8,128)S(1)} %pad_maximum_fusion), channel_id=1, source_target_pairs={{0,1},{1,0},{2,3},{3,2},{4,5},{5,4},{6,7},{7,6},{8,9},{9,8},{10,11... | collective-permute-start | bytes 7077896 | tf_op jit(solution)/shard_map/ppermute | solution.py:143
  99.9 18.2 %collective-permute-start.4 = (f32[96,3072]{1,0:T(8,128)S(1)}, f32[96,3072]{1,0:T(8,128)}, u32[]{:S(2)}, u32[]{:S(2)}) collective-permute-start(f32[96,3072]{1,0:T(8,128)S(1)} %constant_dynamic-slice_fusion.1), channel_id=1, source_target_pairs={{0,2},{1,5},{2,0},{3,7},{4,6},{5,1},{6,4},{7,3},{8,10},{9,13},{10,... | collective-permute-start | bytes 3538952 | tf_op jit(solution)/shard_map/ppermute | solution.py:150
  119.5 12.0 %copy-start.10 = (bf16[48,2048]{1,0:T(8,128)(2,1)S(1)}, bf16[48,2048]{1,0:T(8,128)(2,1)}, u32[]{:S(2)}) copy-start(bf16[48,2048]{1,0:T(8,128)(2,1)} %copy-done.9) | copy-start | bytes 589828
  119.6 11.9 %collective-permute-start.5 = (f32[48,3072]{1,0:T(8,128)S(1)}, f32[48,3072]{1,0:T(8,128)S(1)}, u32[]{:S(2)}, u32[]{:S(2)}) collective-permute-start(f32[48,3072]{1,0:T(8,128)S(1)} %constant_dynamic-slice_fusion), channel_id=1, source_target_pairs={{0,4},{1,3},{2,6},{3,1},{4,0},{5,7},{6,2},{7,5},{8,12},{9,11},{10,... | collective-permute-start | bytes 1769480 | tf_op jit(solution)/shard_map/ppermute | solution.py:150
  131.8 8.6 %collective-permute-start.6 = (bf16[48,3072]{1,0:T(8,128)(2,1)S(1)}, bf16[48,3072]{1,0:T(8,128)(2,1)S(1)}, u32[]{:S(2)}, u32[]{:S(2)}) collective-permute-start(bf16[48,3072]{1,0:T(8,128)(2,1)S(1)} %pad_maximum_fusion.3), channel_id=1, source_target_pairs={{0,4},{1,3},{2,6},{3,1},{4,0},{5,7},{6,2},{7,5},{8,12},{9,11},{10,... | collective-permute-start | bytes 884744 | tf_op jit(solution)/shard_map/ppermute | solution.py:166
  140.4 16.2 %copy-start = (bf16[1,1,448,2048]{3,2,1,0:T(8,128)(2,1)S(1)}, bf16[1,1,448,2048]{3,2,1,0:T(8,128)(2,1)}, u32[]{:S(2)}) copy-start(bf16[1,1,448,2048]{3,2,1,0:T(8,128)(2,1)} %param.15) | copy-start | bytes 5505028
  140.4 11.9 %collective-permute-start.7 = (bf16[96,3072]{1,0:T(8,128)(2,1)S(1)}, bf16[96,3072]{1,0:T(8,128)(2,1)S(1)}, u32[]{:S(2)}, u32[]{:S(2)}) collective-permute-start(bf16[96,3072]{1,0:T(8,128)(2,1)S(1)} %pad_maximum_fusion.2), channel_id=1, source_target_pairs={{0,2},{1,5},{2,0},{3,7},{4,6},{5,1},{6,4},{7,3},{8,10},{9,13},{10,... | collective-permute-start | bytes 1769480 | tf_op jit(solution)/shard_map/ppermute | solution.py:166
  152.4 4.9 %collective-permute-start.8 = (bf16[192,3072]{1,0:T(8,128)(2,1)S(1)}, bf16[192,3072]{1,0:T(8,128)(2,1)}, u32[]{:S(2)}, u32[]{:S(2)}) collective-permute-start(bf16[192,3072]{1,0:T(8,128)(2,1)S(1)} %pad_maximum_fusion.1), channel_id=1, source_target_pairs={{0,1},{1,0},{2,3},{3,2},{4,5},{5,4},{6,7},{7,6},{8,9},{9,8},{10,11... | collective-permute-start | bytes 3538952 | tf_op jit(solution)/shard_map/ppermute | solution.py:179
  157.3 1.9 copy-start.6
  162.2 6.3 %copy-start.11 = (f32[1,32,1]{1,2,0:T(1,128)S(1)}, f32[1,32,1]{1,2,0:T(1,128)}, u32[]{:S(2)}) copy-start(f32[1,32,1]{1,2,0:T(1,128)} %param.14) | copy-start | bytes 388
  162.2 6.3 %copy-start.12 = (f32[1,32,1]{1,2,0:T(1,128)S(1)}, f32[1,32,1]{1,2,0:T(1,128)}, u32[]{:S(2)}) copy-start(f32[1,32,1]{1,2,0:T(1,128)} %param.11) | copy-start | bytes 388
  163.9 49.6 %all-to-all-start.1 = ((bf16[64,2,6,448]{3,1,2,0:T(2,128)(2,1)}), bf16[64,2,6,448]{3,1,2,0:T(2,128)(2,1)S(1)}, u32[]{:S(2)}, u32[]{:S(2)}) async-start(bf16[64,2,6,448]{3,1,2,0:T(2,128)(2,1)} %fusion.22), calls=%async_computation.1 | async-start | bytes 1572864 | tf_op jit(solution)/shard_map/all_to_all | solution.py:199
  214.6 1.1 copy-start.2
  214.6 1.1 copy-start.4
